TPU v7x, 1024 devices: a whole 4x4x32 slice. The times are simulated.
1024 devices in a mesh: ctx: 64 (over z, core), head: 16 (over y, x).
Axes of the slice: x: 4, y: 4, z: 32, core: 2. Of those that a mesh axis runs over, the one named last changes fastest.
Arguments:
- queries: bfloat16 [32768, 8192], P('ctx', 'head'), may hold values from -136 to 136
- keys: bfloat16 [32768, 8192], P('ctx', 'head'), may hold values from -6 to 6
- values: bfloat16 [32768, 8192], P('ctx', 'head'), may hold values from -6 to 6
- segment_ids: int32 [32768], P('ctx'), may hold values from 0 to 3, never falling along the last dimension, each value on 1 to 16384 neighbouring positions
Outputs:
- attended: bfloat16 [32768, 8192], P('ctx', 'head')
Inputs may be any that keep to these rules, and one draw needn't show every extreme that they name: `segment_ids`: document numbers never fall along the tokens; every document of 0 to 3 appears, with 1 to 16384 tokens, one with exactly 16384.
All inputs are finite; a program needn't handle non-finite values.
Results may differ from a plain program's by a relative error of at most 0.0049.
Values may be sent and summed in bfloat16 or wider, within the bound.
No kernel may reach another device: no remote copies, remote signals or barrier semaphores. Data moves between devices by JAX's collectives and lax.ppermute only.
A program may use at most 64 MiB of HBM per device.

v0:
```python
import jax
import jax.numpy as jnp
from jax import lax
from jax.sharding import PartitionSpec as P

HEADS = 64
DH = 128
BLK = 512


def carried_in(value, axis, join, neutral):
    count, mine = (lax.axis_size(axis), lax.axis_index(axis))
    pieces = jax.tree.map(lambda part: lax.all_gather(part, axis), value)
    running = jax.tree.map(
        lambda part, zero: jnp.full_like(part, 0) + jnp.asarray(zero, part.dtype), value, neutral
    )

    def hop(position, running):
        longer = join(running, jax.tree.map(lambda part: part[position], pieces))
        return jax.tree.map(lambda new, old: jnp.where(position < mine, new, old), longer, running)

    return lax.fori_loop(0, count - 1, hop, running)


def combine_states(earlier, later):
    state_e, last_e = earlier
    state_l, last_l = later
    joined = state_l + jnp.where(last_e == last_l, state_e, jnp.zeros_like(state_e))
    state = jnp.where(last_l < 0, state_e, joined)
    last = jnp.where(last_l < 0, last_e, last_l)
    return (state, last)


def on_device(queries, keys, values, segment_ids):
    rows = queries.shape[0]
    heads = queries.shape[1] // DH
    blocks = rows // BLK
    q_all = queries.reshape(blocks, BLK, heads, DH)
    k_all = keys.reshape(blocks, BLK, heads, DH)
    v_all = values.reshape(blocks, BLK, heads, DH)
    s_all = segment_ids.reshape(blocks, BLK)
    positions = jnp.arange(BLK)
    causal = positions[:, None] >= positions[None, :]

    def local_block(item):
        qb, kb, vb, sb = item
        scores = jnp.einsum("thd,shd->hts", qb, kb, preferred_element_type=jnp.float32)
        mask = causal & (sb[:, None] == sb[None, :])
        probs = jnp.where(mask[None], scores, 0.0).astype(jnp.bfloat16)
        intra = jnp.einsum("hts,shd->thd", probs, vb, preferred_element_type=jnp.float32)
        block_last = sb[-1]
        keep = (sb == block_last)[:, None, None]
        kv_sum = jnp.einsum(
            "thd,the->hde",
            jnp.where(keep, kb, jnp.zeros_like(kb)),
            vb,
            preferred_element_type=jnp.float32,
        )
        return (intra, kv_sum, block_last)

    intra_all, kv_all, last_all = lax.map(local_block, (q_all, k_all, v_all, s_all))
    empty_state = (jnp.zeros((heads, DH, DH), jnp.float32), jnp.int32(-1))

    def fold_local(carry, item):
        return (combine_states(carry, item), None)

    own_state, _ = lax.scan(fold_local, empty_state, (kv_all, last_all))
    prefix = carried_in(own_state, "ctx", combine_states, empty_state)

    def inter_block(carry, item):
        qb, sb, kv_sum, block_last = item
        state, last = carry
        inter = jnp.einsum(
            "thd,hde->the", qb, state.astype(jnp.bfloat16), preferred_element_type=jnp.float32
        )
        inter = jnp.where((sb == last)[:, None, None], inter, 0.0)
        return (combine_states(carry, (kv_sum, block_last)), inter)

    _, inter_all = lax.scan(inter_block, prefix, (q_all, s_all, kv_all, last_all))
    outputs = (intra_all + inter_all).reshape(rows, heads * DH)
    squares = jnp.sum(outputs * outputs, axis=1)
    totals = lax.psum(squares, "head")
    scaled = outputs * lax.rsqrt(totals / (HEADS * DH) + 1e-05)[:, None]
    return scaled.astype(jnp.bfloat16)


def solution(mesh):
    in_specs = (P("ctx", "head"), P("ctx", "head"), P("ctx", "head"), P("ctx"))
    out_specs = P("ctx", "head")
    return jax.shard_map(
        on_device, mesh=mesh, in_specs=in_specs, out_specs=out_specs, check_vma=False
    )
```

profile of v0, /device:TPU:32, one launch (start us, length us, event | category | flops | bytes accessed | tf_op | source)
XLA Modules:
  0.0 450.7 jit_solution(4634444713845175749)
XLA Ops:
  6.5 1.3 slice.4
  7.9 1.2 broadcast_compare_fusion.1
  9.7 1.3 copy.18
  10.9 2.0 convolution_select_fusion.1
  13.6 1.3 dynamic-slice.2
  15.6 45.3 %all-reduce = s32[64]{0:T(128)S(1)} all-reduce(s32[64]{0:T(128)S(1)} %dynamic-update-slice), channel_id=1, replica_groups=mesh['ctx'=64,'head'=16] {'ctx'}, use_global_device_ids=true, to_apply=%add | all-reduce | flops 64 | bytes 512
  61.9 2.4 fusion.3
  64.2 108.7 %all-gather.3.cloned.1.call-done = f32[256,128,128]{2,1,0:T(8,128)} async-done(((f32[4,128,128]{2,1,0:T(8,128)}), f32[256,128,128]{2,1,0:T(8,128)}) %all-gather.3.cloned.1.call-update) | async-done | bytes 16777232 | tf_op jit(solution)/shard_map/all_gather | solution.py:13
  172.9 229.3 %while.10 = (s32[]{:T(128)}, f32[4,128,128]{2,1,0:T(8,128)S(1)}, s32[]{:T(128)}, s32[]{:T(128)}, s32[64]{0:T(128)S(1)}, /*index=5*/f32[64,4,128,128]{3,2,1,0:T(8,128)}, s32[]{:T(128)}, s32[]{:T(128)}) while((s32[]{:T(128)}, f32[4,128,128]{2,1,0:T(8,128)S(1)}, s32[]{:T(128)}, s32[]{:T(128)}, s32[64]{0:T(128)S(1)}, ...), condition=%wide.region_1.2_spmd.clone, body=%wide.region_0.1_spmd.clone.sunk | while | flops 327688 | bytes 786599 | solution.py:22
  174.8 1.1 select_select_fusion.2
  178.4 1.1 select_select_fusion.2
  182.1 1.1 select_select_fusion.2
  185.7 1.1 select_select_fusion.2
  189.3 1.1 select_select_fusion.2
  193.0 1.1 select_select_fusion.2
  196.6 1.1 select_select_fusion.2
  200.3 1.1 select_select_fusion.2
  203.9 1.1 select_select_fusion.2
  207.5 1.1 select_select_fusion.2
  214.8 1.1 select_select_fusion.2
  218.5 1.1 select_select_fusion.2
  225.8 1.1 select_select_fusion.2
  229.4 1.1 select_select_fusion.2
  403.0 39.9 %psum.7 = f32[512]{0:T(512)S(1)} all-reduce(f32[512]{0:T(512)S(1)} %get-tuple-element.216), channel_id=1, replica_groups=mesh['ctx'=64,'head'=16] {'head'}, use_global_device_ids=true, to_apply=%region_3.4 | all-reduce | flops 512 | bytes 4096 | tf_op jit(solution)/shard_map/psum | solution.py:82
  (127 shorter events, 93.0 us)
Async XLA Ops:
  6.5 55.3 %copy-start = (bf16[512,512]{1,0:T(8,128)(2,1)S(1)}, bf16[512,512]{1,0:T(8,128)(2,1)}, u32[]{:S(2)}) copy-start(bf16[512,512]{1,0:T(8,128)(2,1)} %param.6) | copy-start | bytes 1572868
  6.5 166.4 %all-gather.3.cloned.1.call-start = ((), (), s32[]{:S(2)}) async-start(), calls=%async_computation | async-start | bytes 17039360 | tf_op jit(solution)/shard_map/all_gather | solution.py:13
  61.9 340.4 %copy-start.1 = (s32[512]{0:T(512)S(1)}, s32[512]{0:T(512)}, u32[]{:S(2)}) copy-start(s32[512]{0:T(512)} %param.9) | copy-start | bytes 6148
Sparse Core Ops, SparseCore 0:
  13.1 159.7 all-gather.2
where the time goes:
time: 455 us; the launch traced here: 451 us
  loops' own time  125 us (27%)
  waiting for transfers between devices  109 us (24%)
  blocking collectives  85.2 us (19%)
  other arithmetic  70.9 us (16%)
  local copies, waits for them, and re-layouts  41.9 us (9%)
  between operations  14.6 us (3%)
  matrix products  4.78 us (1%)
    another operation x1, loops' own time, carried_in(): return lax.fori_loop(0, count - 1, hop, running)  125 us
    all_gather x1, waiting for transfers between devices, carried_in(): pieces = jax.tree.map(lambda part: lax.all_gather(part, axis), value)  109 us
    select_n x63, other arithmetic, hop(): jnp.where(position < mine, new, old)  67.7 us
    unnamed x1, blocking collectives  45.3 us
    psum x1, blocking collectives, on_device(): totals = lax.psum(squares, 'head')  39.9 us
    dynamic_slice x63, local copies, waits for them, and re-layouts, hop(): longer = join(running, jax.tree.map(lambda part: part[position], pieces))  36.9 us
  transfers between devices with their start and end apart: 1, of which 1 were waited for; matrix products, arithmetic and copies ran while one was open for 1% of the time, Pallas kernels for 0%

commit v1 on v0

--- a/solution.py
+++ b/solution.py
@@ -8,20 +8,6 @@
 BLK = 512
 
 
-def carried_in(value, axis, join, neutral):
-    count, mine = (lax.axis_size(axis), lax.axis_index(axis))
-    pieces = jax.tree.map(lambda part: lax.all_gather(part, axis), value)
-    running = jax.tree.map(
-        lambda part, zero: jnp.full_like(part, 0) + jnp.asarray(zero, part.dtype), value, neutral
-    )
-
-    def hop(position, running):
-        longer = join(running, jax.tree.map(lambda part: part[position], pieces))
-        return jax.tree.map(lambda new, old: jnp.where(position < mine, new, old), longer, running)
-
-    return lax.fori_loop(0, count - 1, hop, running)
-
-
 def combine_states(earlier, later):
     state_e, last_e = earlier
     state_l, last_l = later
@@ -29,6 +15,24 @@
     state = jnp.where(last_l < 0, state_e, joined)
     last = jnp.where(last_l < 0, last_e, last_l)
     return (state, last)
+
+
+def carried_in(own, axis):
+    count, mine = (lax.axis_size(axis), lax.axis_index(axis))
+    state, last = own
+    excl = (jnp.zeros_like(state), jnp.full_like(last, -1))
+    incl = (state, last)
+    shift = 1
+    while shift < count:
+        pairs = [(j, j + shift) for j in range(count - shift)]
+        got_state, got_last = lax.ppermute(incl, axis, pairs)
+        got_last = jnp.where(mine >= shift, got_last, -1)
+        got = (got_state, got_last)
+        excl = combine_states(got, excl)
+        if 2 * shift < count:
+            incl = combine_states(got, incl)
+        shift *= 2
+    return excl
 
 
 def on_device(queries, keys, values, segment_ids):
@@ -65,7 +69,7 @@
         return (combine_states(carry, item), None)
 
     own_state, _ = lax.scan(fold_local, empty_state, (kv_all, last_all))
-    prefix = carried_in(own_state, "ctx", combine_states, empty_state)
+    prefix = carried_in(own_state, "ctx")
 
     def inter_block(carry, item):
         qb, sb, kv_sum, block_last = item

time: 455 us -> 284 us (0.62)
  the two profiles are of different devices: /device:TPU:32 before, /device:TPU:64 now
where the time goes in v1:
time: 284 us
  starting transfers between devices  183 us (64%)
  waiting for transfers between devices  45.1 us (16%)
  blocking collectives  40.7 us (14%)
  between operations  5.25 us (2%)
  matrix products  4.15 us (1%)
  local copies, waits for them, and re-layouts  3.61 us (1%)
    ppermute x12, starting transfers between devices, carried_in(): got_state, got_last = lax.ppermute(incl, axis, pairs)  183 us
    ppermute x12, waiting for transfers between devices, carried_in(): got_state, got_last = lax.ppermute(incl, axis, pairs)  45.1 us
    psum x1, blocking collectives, on_device(): totals = lax.psum(squares, 'head')  40.7 us
  transfers between devices with their start and end apart: 12, of which 9 were waited for; matrix products, arithmetic and copies ran while one was open for 1% of the time, Pallas kernels for 0%

profile of v1, /device:TPU:64, one launch (start us, length us, event | category | flops | bytes accessed | tf_op | source)
XLA Modules:
  0.0 283.7 jit_solution(5899174498315401775)
XLA Ops:
  0.0 1.4 slice.4
  2.7 2.7 collective-permute-start
  5.4 1.3 copy.12
  8.2 5.1 %collective-permute-start.1 = (s32[]{:T(128)}, s32[]{:T(128)}, u32[]{:S(2)}, u32[]{:S(2)}) collective-permute-start(s32[]{:T(128)} %select_n.225), channel_id=1, source_target_pairs={{0,32},{16,48},{32,64},{48,80},{64,96},{80,112},{96,128},{112,144}... | collective-permute-start | bytes 20 | tf_op jit(solution)/shard_map/ppermute | solution.py:28
  14.2 10.1 %collective-permute-start.2 = (s32[]{:T(128)}, s32[]{:T(128)}, u32[]{:S(2)}, u32[]{:S(2)}) collective-permute-start(s32[]{:T(128)} %select_n.228), channel_id=1, source_target_pairs={{0,64},{16,80},{32,96},{48,112},{64,128},{80,144},{96,160},{112,17... | collective-permute-start | bytes 20 | tf_op jit(solution)/shard_map/ppermute | solution.py:28
  25.7 9.6 %collective-permute-start.3 = (s32[]{:T(128)}, s32[]{:T(128)}, u32[]{:S(2)}, u32[]{:S(2)}) collective-permute-start(s32[]{:T(128)} %select_n.231), channel_id=1, source_target_pairs={{0,128},{16,144},{32,160},{48,176},{64,192},{80,208},{96,224},{112... | collective-permute-start | bytes 20 | tf_op jit(solution)/shard_map/ppermute | solution.py:28
  35.9 17.0 %collective-permute-start.4 = (s32[]{:T(128)}, s32[]{:T(128)}, u32[]{:S(2)}, u32[]{:S(2)}) collective-permute-start(s32[]{:T(128)} %select_n.234), channel_id=1, source_target_pairs={{0,256},{16,272},{32,288},{48,304},{64,320},{80,336},{96,352},{112... | collective-permute-start | bytes 20 | tf_op jit(solution)/shard_map/ppermute | solution.py:28
  53.5 22.2 %collective-permute-start.5 = (s32[]{:T(128)}, s32[]{:T(128)}, u32[]{:S(2)}, u32[]{:S(2)}) collective-permute-start(s32[]{:T(128)} %select_n.237), channel_id=1, source_target_pairs={{0,512},{16,528},{32,544},{48,560},{64,576},{80,592},{96,608},{112... | collective-permute-start | bytes 20 | tf_op jit(solution)/shard_map/ppermute | solution.py:28
  77.3 1.9 collective-permute-start.6
  79.2 5.8 %collective-permute-done.6 = f32[4,128,128]{2,1,0:T(8,128)S(1)} collective-permute-done((f32[4,128,128]{2,1,0:T(8,128)S(1)}, f32[4,128,128]{2,1,0:T(8,128)S(1)}, u32[]{:S(2)}, u32[]{:S(2)}) %collective-permute-start.6) | collective-permute-done | bytes 262176 | tf_op jit(solution)/shard_map/ppermute | solution.py:28
  85.0 2.0 collective-permute-start.7
  87.0 6.3 %collective-permute-done.7 = f32[4,128,128]{2,1,0:T(8,128)S(1)} collective-permute-done((f32[4,128,128]{2,1,0:T(8,128)S(1)}, f32[4,128,128]{2,1,0:T(8,128)S(1)}, u32[]{:S(2)}, u32[]{:S(2)}) %collective-permute-start.7) | collective-permute-done | bytes 262176 | tf_op jit(solution)/shard_map/ppermute | solution.py:28
  93.3 8.5 %collective-permute-start.8 = (f32[4,128,128]{2,1,0:T(8,128)S(1)}, f32[4,128,128]{2,1,0:T(8,128)S(1)}, u32[]{:S(2)}, u32[]{:S(2)}) collective-permute-start(f32[4,128,128]{2,1,0:T(8,128)S(1)} %add_select_fusion.3), channel_id=1, source_target_pairs={{0,64},{16,80},{32,96},{48,112},{64,128},{80,144},{96,160},{112,17... | collective-permute-start | bytes 786440 | tf_op jit(solution)/shard_map/ppermute | solution.py:28
  101.8 19.6 %collective-permute-done.8 = f32[4,128,128]{2,1,0:T(8,128)S(1)} collective-permute-done((f32[4,128,128]{2,1,0:T(8,128)S(1)}, f32[4,128,128]{2,1,0:T(8,128)S(1)}, u32[]{:S(2)}, u32[]{:S(2)}) %collective-permute-start.8) | collective-permute-done | bytes 262176 | tf_op jit(solution)/shard_map/ppermute | solution.py:28
  121.4 1.3 collective-permute-start.9
  122.8 3.9 %collective-permute-done.9 = f32[4,128,128]{2,1,0:T(8,128)S(1)} collective-permute-done((f32[4,128,128]{2,1,0:T(8,128)S(1)}, f32[4,128,128]{2,1,0:T(8,128)S(1)}, u32[]{:S(2)}, u32[]{:S(2)}) %collective-permute-start.9) | collective-permute-done | bytes 262176 | tf_op jit(solution)/shard_map/ppermute | solution.py:28
  126.7 21.5 %collective-permute-start.10 = (f32[4,128,128]{2,1,0:T(8,128)S(1)}, f32[4,128,128]{2,1,0:T(8,128)S(1)}, u32[]{:S(2)}, u32[]{:S(2)}) collective-permute-start(f32[4,128,128]{2,1,0:T(8,128)S(1)} %add_select_fusion.1), channel_id=1, source_target_pairs={{0,256},{16,272},{32,288},{48,304},{64,320},{80,336},{96,352},{112... | collective-permute-start | bytes 786440 | tf_op jit(solution)/shard_map/ppermute | solution.py:28
  148.4 5.2 %collective-permute-done.10 = f32[4,128,128]{2,1,0:T(8,128)S(1)} collective-permute-done((f32[4,128,128]{2,1,0:T(8,128)S(1)}, f32[4,128,128]{2,1,0:T(8,128)S(1)}, u32[]{:S(2)}, u32[]{:S(2)}) %collective-permute-start.10) | collective-permute-done | bytes 262176 | tf_op jit(solution)/shard_map/ppermute | solution.py:28
  154.3 81.1 %collective-permute-start.11 = (f32[4,128,128]{2,1,0:T(8,128)S(1)}, f32[4,128,128]{2,1,0:T(8,128)}, u32[]{:S(2)}, u32[]{:S(2)}) collective-permute-start(f32[4,128,128]{2,1,0:T(8,128)S(1)} %add_select_fusion), channel_id=1, source_target_pairs={{0,512},{16,528},{32,544},{48,560},{64,576},{80,592},{96,608},{112... | collective-permute-start | bytes 786440 | tf_op jit(solution)/shard_map/ppermute | solution.py:28
  235.5 2.4 fusion.1
  237.9 2.4 collective-permute-done.11
  240.3 1.5 multiply_reduce_fusion
  241.8 40.7 %psum.7 = f32[512]{0:T(512)S(1)} all-reduce(f32[512]{0:T(512)S(1)} %get-tuple-element.50), channel_id=1, replica_groups=mesh['ctx'=64,'head'=16] {'head'}, use_global_device_ids=true, to_apply=%region_1.2 | all-reduce | flops 512 | bytes 4096 | tf_op jit(solution)/shard_map/psum | solution.py:86
  282.8 0.9 multiply_convert_fusion
  (26 shorter events, 4.3 us)
Async XLA Ops:
  0.0 235.5 %copy-start = (bf16[512,512]{1,0:T(8,128)(2,1)S(1)}, bf16[512,512]{1,0:T(8,128)(2,1)}, u32[]{:S(2)}) copy-start(bf16[512,512]{1,0:T(8,128)(2,1)} %param.4) | copy-start | bytes 1572868
  0.0 76.3 %copy-start.3 = (s32[512]{0:T(512)S(1)}, s32[512]{0:T(512)}, u32[]{:S(2)}) copy-start(s32[512]{0:T(512)} %param.7) | copy-start | bytes 6148
  0.0 77.0 %copy-start.4 = (bf16[512,512]{1,0:T(8,128)(2,1)S(1)}, bf16[512,512]{1,0:T(8,128)(2,1)}, u32[]{:S(2)}) copy-start(bf16[512,512]{1,0:T(8,128)(2,1)} %param.6) | copy-start | bytes 1572868
  2.7 4.8 %collective-permute-start = (s32[]{:T(128)}, s32[]{:T(128)}, u32[]{:S(2)}, u32[]{:S(2)}) collective-permute-start(s32[]{:T(128)} %select_n.223), channel_id=1, source_target_pairs={{0,16},{16,32},{32,48},{48,64},{64,80},{80,96},{96,112},{112,128},... | collective-permute-start | bytes 20 | tf_op jit(solution)/shard_map/ppermute | solution.py:28
  8.2 5.4 %collective-permute-start.1 = (s32[]{:T(128)}, s32[]{:T(128)}, u32[]{:S(2)}, u32[]{:S(2)}) collective-permute-start(s32[]{:T(128)} %select_n.225), channel_id=1, source_target_pairs={{0,32},{16,48},{32,64},{48,80},{64,96},{80,112},{96,128},{112,144}... | collective-permute-start | bytes 20 | tf_op jit(solution)/shard_map/ppermute | solution.py:28
  14.2 10.9 %collective-permute-start.2 = (s32[]{:T(128)}, s32[]{:T(128)}, u32[]{:S(2)}, u32[]{:S(2)}) collective-permute-start(s32[]{:T(128)} %select_n.228), channel_id=1, source_target_pairs={{0,64},{16,80},{32,96},{48,112},{64,128},{80,144},{96,160},{112,17... | collective-permute-start | bytes 20 | tf_op jit(solution)/shard_map/ppermute | solution.py:28
  25.7 9.6 %collective-permute-start.3 = (s32[]{:T(128)}, s32[]{:T(128)}, u32[]{:S(2)}, u32[]{:S(2)}) collective-permute-start(s32[]{:T(128)} %select_n.231), channel_id=1, source_target_pairs={{0,128},{16,144},{32,160},{48,176},{64,192},{80,208},{96,224},{112... | collective-permute-start | bytes 20 | tf_op jit(solution)/shard_map/ppermute | solution.py:28
  35.9 17.0 %collective-permute-start.4 = (s32[]{:T(128)}, s32[]{:T(128)}, u32[]{:S(2)}, u32[]{:S(2)}) collective-permute-start(s32[]{:T(128)} %select_n.234), channel_id=1, source_target_pairs={{0,256},{16,272},{32,288},{48,304},{64,320},{80,336},{96,352},{112... | collective-permute-start | bytes 20 | tf_op jit(solution)/shard_map/ppermute | solution.py:28
  53.5 22.2 %collective-permute-start.5 = (s32[]{:T(128)}, s32[]{:T(128)}, u32[]{:S(2)}, u32[]{:S(2)}) collective-permute-start(s32[]{:T(128)} %select_n.237), channel_id=1, source_target_pairs={{0,512},{16,528},{32,544},{48,560},{64,576},{80,592},{96,608},{112... | collective-permute-start | bytes 20 | tf_op jit(solution)/shard_map/ppermute | solution.py:28
  77.3 7.7 %collective-permute-start.6 = (f32[4,128,128]{2,1,0:T(8,128)S(1)}, f32[4,128,128]{2,1,0:T(8,128)S(1)}, u32[]{:S(2)}, u32[]{:S(2)}) collective-permute-start(f32[4,128,128]{2,1,0:T(8,128)S(1)} %convolution_select_fusion), channel_id=1, source_target_pairs={{0,16},{16,32},{32,48},{48,64},{64,80},{80,96},{96,112},{112,128},... | collective-permute-start | bytes 786440 | tf_op jit(solution)/shard_map/ppermute | solution.py:28
  85.0 8.3 %collective-permute-start.7 = (f32[4,128,128]{2,1,0:T(8,128)S(1)}, f32[4,128,128]{2,1,0:T(8,128)S(1)}, u32[]{:S(2)}, u32[]{:S(2)}) collective-permute-start(f32[4,128,128]{2,1,0:T(8,128)S(1)} %add_select_fusion.4), channel_id=1, source_target_pairs={{0,32},{16,48},{32,64},{48,80},{64,96},{80,112},{96,128},{112,144}... | collective-permute-start | bytes 786440 | tf_op jit(solution)/shard_map/ppermute | solution.py:28
  93.3 28.1 %collective-permute-start.8 = (f32[4,128,128]{2,1,0:T(8,128)S(1)}, f32[4,128,128]{2,1,0:T(8,128)S(1)}, u32[]{:S(2)}, u32[]{:S(2)}) collective-permute-start(f32[4,128,128]{2,1,0:T(8,128)S(1)} %add_select_fusion.3), channel_id=1, source_target_pairs={{0,64},{16,80},{32,96},{48,112},{64,128},{80,144},{96,160},{112,17... | collective-permute-start | bytes 786440 | tf_op jit(solution)/shard_map/ppermute | solution.py:28
  121.4 5.2 %collective-permute-start.9 = (f32[4,128,128]{2,1,0:T(8,128)S(1)}, f32[4,128,128]{2,1,0:T(8,128)S(1)}, u32[]{:S(2)}, u32[]{:S(2)}) collective-permute-start(f32[4,128,128]{2,1,0:T(8,128)S(1)} %add_select_fusion.2), channel_id=1, source_target_pairs={{0,128},{16,144},{32,160},{48,176},{64,192},{80,208},{96,224},{112... | collective-permute-start | bytes 786440 | tf_op jit(solution)/shard_map/ppermute | solution.py:28
  126.7 27.0 %copy-start.1 = (f32[4,128,128]{2,1,0:T(8,128)}, f32[4,128,128]{2,1,0:T(8,128)S(1)}, u32[]{:S(2)}) copy-start(f32[4,128,128]{2,1,0:T(8,128)S(1)} %collective-permute-done.9) | copy-start | bytes 786436
  126.7 26.9 %collective-permute-start.10 = (f32[4,128,128]{2,1,0:T(8,128)S(1)}, f32[4,128,128]{2,1,0:T(8,128)S(1)}, u32[]{:S(2)}, u32[]{:S(2)}) collective-permute-start(f32[4,128,128]{2,1,0:T(8,128)S(1)} %add_select_fusion.1), channel_id=1, source_target_pairs={{0,256},{16,272},{32,288},{48,304},{64,320},{80,336},{96,352},{112... | collective-permute-start | bytes 786440 | tf_op jit(solution)/shard_map/ppermute | solution.py:28
  153.6 0.7 copy-start.2
  154.3 86.0 %collective-permute-start.11 = (f32[4,128,128]{2,1,0:T(8,128)S(1)}, f32[4,128,128]{2,1,0:T(8,128)}, u32[]{:S(2)}, u32[]{:S(2)}) collective-permute-start(f32[4,128,128]{2,1,0:T(8,128)S(1)} %add_select_fusion), channel_id=1, source_target_pairs={{0,512},{16,528},{32,544},{48,560},{64,576},{80,592},{96,608},{112... | collective-permute-start | bytes 786440 | tf_op jit(solution)/shard_map/ppermute | solution.py:28

commit v2 on v1

--- a/solution.py
+++ b/solution.py
@@ -1,11 +1,13 @@
 import jax
 import jax.numpy as jnp
 from jax import lax
+from jax.sharding import Mesh
 from jax.sharding import PartitionSpec as P
 
 HEADS = 64
 DH = 128
 BLK = 512
+TAG = 8
 
 
 def combine_states(earlier, later):
@@ -17,7 +19,22 @@
     return (state, last)
 
 
-def carried_in(own, axis):
+def pack(value):
+    state, last = value
+    tag = jnp.full((TAG, DH), last.astype(jnp.float32))
+    return jnp.concatenate([state.reshape(-1, DH), tag], axis=0)
+
+
+def unpack(packed):
+    state = packed[:-TAG].reshape(-1, DH, DH)
+    return (state, packed[-TAG, 0].astype(jnp.int32))
+
+
+def swap_cores(value, core_axis):
+    return unpack(lax.ppermute(pack(value), core_axis, [(0, 1), (1, 0)]))
+
+
+def scan_chips(own, axis):
     count, mine = (lax.axis_size(axis), lax.axis_index(axis))
     state, last = own
     excl = (jnp.zeros_like(state), jnp.full_like(last, -1))
@@ -25,14 +42,39 @@
     shift = 1
     while shift < count:
         pairs = [(j, j + shift) for j in range(count - shift)]
-        got_state, got_last = lax.ppermute(incl, axis, pairs)
-        got_last = jnp.where(mine >= shift, got_last, -1)
-        got = (got_state, got_last)
+        got_state, got_last = unpack(lax.ppermute(pack(incl), axis, pairs))
+        got = (got_state, jnp.where(mine >= shift, got_last, -1))
         excl = combine_states(got, excl)
         if 2 * shift < count:
             incl = combine_states(got, incl)
         shift *= 2
     return excl
+
+
+def carried_in(own, chip_axis, core_axis):
+    core = lax.axis_index(core_axis)
+    other = swap_cores(own, core_axis)
+    first = jax.tree.map(lambda a, b: jnp.where(core == 0, a, b), own, other)
+    second = jax.tree.map(lambda a, b: jnp.where(core == 0, b, a), own, other)
+    chip = combine_states(first, second)
+    empty = (jnp.zeros_like(own[0]), jnp.full_like(own[1], -1))
+    in_chip = jax.tree.map(lambda a, b: jnp.where(core == 0, a, b), empty, first)
+    half = chip[0].shape[0] // 2
+    mine = jnp.where(core == 0, chip[0][:half], chip[0][half:])
+    before = scan_chips((mine, chip[1]), chip_axis)
+    theirs = swap_cores(before, core_axis)
+    whole = jnp.where(
+        core == 0,
+        jnp.concatenate([before[0], theirs[0]], axis=0),
+        jnp.concatenate([theirs[0], before[0]], axis=0),
+    )
+    return combine_states((whole, before[1]), in_chip)
+
+
+def head_sum(x, axis):
+    count = lax.axis_size(axis)
+    spread = jnp.broadcast_to(x[None], (count,) + x.shape)
+    return jnp.sum(lax.all_to_all(spread, axis, 0, 0, tiled=True), axis=0)
 
 
 def on_device(queries, keys, values, segment_ids):
@@ -69,7 +111,7 @@
         return (combine_states(carry, item), None)
 
     own_state, _ = lax.scan(fold_local, empty_state, (kv_all, last_all))
-    prefix = carried_in(own_state, "ctx")
+    prefix = carried_in(own_state, "chip", "core")
 
     def inter_block(carry, item):
         qb, sb, kv_sum, block_last = item
@@ -83,14 +125,14 @@
     _, inter_all = lax.scan(inter_block, prefix, (q_all, s_all, kv_all, last_all))
     outputs = (intra_all + inter_all).reshape(rows, heads * DH)
     squares = jnp.sum(outputs * outputs, axis=1)
-    totals = lax.psum(squares, "head")
+    totals = head_sum(squares, "head")
     scaled = outputs * lax.rsqrt(totals / (HEADS * DH) + 1e-05)[:, None]
     return scaled.astype(jnp.bfloat16)
 
 
 def solution(mesh):
-    in_specs = (P("ctx", "head"), P("ctx", "head"), P("ctx", "head"), P("ctx"))
-    out_specs = P("ctx", "head")
-    return jax.shard_map(
-        on_device, mesh=mesh, in_specs=in_specs, out_specs=out_specs, check_vma=False
-    )
+    ctx, head = (mesh.shape["ctx"], mesh.shape["head"])
+    split = Mesh(mesh.devices.reshape(ctx // 2, 2, head), ("chip", "core", "head"))
+    rows = P(("chip", "core"), "head")
+    in_specs = (rows, rows, rows, P(("chip", "core")))
+    return jax.shard_map(on_device, mesh=split, in_specs=in_specs, out_specs=rows, check_vma=False)

time: 284 us -> 138 us (0.49)
  the two profiles are of different devices: /device:TPU:64 before, /device:TPU:1 now
where the time goes in v2:
time: 138 us; the launch traced here: 137 us
  starting transfers between devices  100 us (72%)
  waiting for transfers between devices  17.4 us (13%)
  local copies, waits for them, and re-layouts  7.06 us (5%)
  between operations  5.69 us (4%)
  matrix products  4.03 us (3%)
  other arithmetic  2.83 us (2%)
    ppermute x5, starting transfers between devices, scan_chips(): got_state, got_last = unpack(lax.ppermute(pack(incl), axis, pairs))  57.6 us
    all_to_all x1, starting transfers between devices, head_sum(): return jnp.sum(lax.all_to_all(spread, axis, 0, 0, tiled=True), axis=0)  23.4 us
    ppermute x2, starting transfers between devices, swap_cores(): return unpack(lax.ppermute(pack(value), core_axis, [(0, 1), (1, 0)]))  19.1 us
    ppermute x5, waiting for transfers between devices, scan_chips(): got_state, got_last = unpack(lax.ppermute(pack(incl), axis, pairs))  9.24 us
    all_to_all x1, waiting for transfers between devices, head_sum(): return jnp.sum(lax.all_to_all(spread, axis, 0, 0, tiled=True), axis=0)  6.11 us
    dot_general x1, matrix products, local_block(): jnp.einsum('hts,shd->thd', probs, vb, preferred_element_type=jnp.float32)  3.35 us
    slice x6, local copies, waits for them, and re-layouts, unpack(): return (state, packed[-TAG, 0].astype(jnp.int32))  3.3 us
  transfers between devices with their start and end apart: 8, of which 7 were waited for; matrix products, arithmetic and copies ran while one was open for 3% of the time, Pallas kernels for 0%

profile of v2, /device:TPU:1, one launch (start us, length us, event | category | flops | bytes accessed | tf_op | source)
XLA Modules:
  0.0 137.1 jit_solution(17516328434698890619)
XLA Ops:
  0.0 1.4 slice.49
  1.4 1.3 broadcast_compare_fusion.1
  3.3 1.3 copy.28
  5.6 16.0 %collective-permute-start = (f32[520,128]{1,0:T(8,128)S(1)}, f32[520,128]{1,0:T(8,128)S(1)}, u32[]{:S(2)}, u32[]{:S(2)}) collective-permute-start(f32[520,128]{1,0:T(8,128)S(1)} %concatenate.27), channel_id=1, source_target_pairs={{0,16},{16,0},{1,17},{17,1},{2,18},{18,2},{3,19},{19,3},{4,20},{20... | collective-permute-start | bytes 798728 | tf_op jit(solution)/shard_map/ppermute | solution.py:34
  21.6 1.1 collective-permute-done
  22.8 0.6 slice.65
  24.1 1.3 collective-permute-start.1
  25.4 2.8 %collective-permute-done.1 = f32[264,128]{1,0:T(8,128)S(1)} collective-permute-done((f32[264,128]{1,0:T(8,128)S(1)}, f32[264,128]{1,0:T(8,128)S(1)}, u32[]{:S(2)}, u32[]{:S(2)}) %collective-permute-start.1) | collective-permute-done | bytes 135200 | tf_op jit(solution)/shard_map/ppermute | solution.py:45
  29.5 1.3 collective-permute-start.2
  30.8 2.2 %collective-permute-done.2 = f32[264,128]{1,0:T(8,128)S(1)} collective-permute-done((f32[264,128]{1,0:T(8,128)S(1)}, f32[264,128]{1,0:T(8,128)S(1)}, u32[]{:S(2)}, u32[]{:S(2)}) %collective-permute-start.2) | collective-permute-done | bytes 135200 | tf_op jit(solution)/shard_map/ppermute | solution.py:45
  33.1 0.5 slice.71
  34.3 4.4 %collective-permute-start.3 = (f32[264,128]{1,0:T(8,128)S(1)}, f32[264,128]{1,0:T(8,128)S(1)}, u32[]{:S(2)}, u32[]{:S(2)}) collective-permute-start(f32[264,128]{1,0:T(8,128)S(1)} %concatenate.30), channel_id=1, source_target_pairs={{0,128},{32,160},{64,192},{96,224},{128,256},{160,288},{192,320},{... | collective-permute-start | bytes 405512 | tf_op jit(solution)/shard_map/ppermute | solution.py:45
  38.7 1.9 %collective-permute-done.3 = f32[264,128]{1,0:T(8,128)S(1)} collective-permute-done((f32[264,128]{1,0:T(8,128)S(1)}, f32[264,128]{1,0:T(8,128)S(1)}, u32[]{:S(2)}, u32[]{:S(2)}) %collective-permute-start.3) | collective-permute-done | bytes 135200 | tf_op jit(solution)/shard_map/ppermute | solution.py:45
  41.9 26.9 %collective-permute-start.4 = (f32[264,128]{1,0:T(8,128)S(1)}, f32[264,128]{1,0:T(8,128)S(1)}, u32[]{:S(2)}, u32[]{:S(2)}) collective-permute-start(f32[264,128]{1,0:T(8,128)S(1)} %concatenate.31), channel_id=1, source_target_pairs={{0,256},{32,288},{64,320},{96,352},{128,384},{160,416},{192,448},{... | collective-permute-start | bytes 405512 | tf_op jit(solution)/shard_map/ppermute | solution.py:45
  69.0 2.2 %collective-permute-done.4 = f32[264,128]{1,0:T(8,128)S(1)} collective-permute-done((f32[264,128]{1,0:T(8,128)S(1)}, f32[264,128]{1,0:T(8,128)S(1)}, u32[]{:S(2)}, u32[]{:S(2)}) %collective-permute-start.4) | collective-permute-done | bytes 135200 | tf_op jit(solution)/shard_map/ppermute | solution.py:45
  72.5 23.8 %collective-permute-start.5 = (f32[264,128]{1,0:T(8,128)S(1)}, f32[264,128]{1,0:T(8,128)S(1)}, u32[]{:S(2)}, u32[]{:S(2)}) collective-permute-start(f32[264,128]{1,0:T(8,128)S(1)} %concatenate.32), channel_id=1, source_target_pairs={{0,512},{32,544},{64,576},{96,608},{128,640},{160,672},{192,704},{... | collective-permute-start | bytes 405512 | tf_op jit(solution)/shard_map/ppermute | solution.py:45
  96.3 3.3 %fusion.3 = f32[512,4,128]{0,2,1:T(8,128)} fusion(bf16[512,4,128]{0,2,1:T(8,128)(2,1)S(1)} %bitcast.74, pred[512,512]{1,0:T(8,128)(4,1)S(1)} %fusion.4, bf16[512,512]{1,0:T(8,128)(2,1)} %param.6, bf16[512,512]{1,0:T(8,128)(2,1)S(1)} %copy-done), kind=kOutput, calls=%fused_computation.5 | convolution fusion | flops 538968064 | bytes 2883584 | tf_op jit(solution)/shard_map/while/body/eval_jaxpr/hts,shd->thd/dot_general | solution.py:96
  99.7 0.6 slice.77
  101.1 3.1 %collective-permute-start.6 = (f32[264,128]{1,0:T(8,128)S(1)}, f32[264,128]{1,0:T(8,128)S(1)}, u32[]{:S(2)}, u32[]{:S(2)}) collective-permute-start(f32[264,128]{1,0:T(8,128)S(1)} %concatenate.33), channel_id=1, source_target_pairs={{0,16},{16,0},{1,17},{17,1},{2,18},{18,2},{3,19},{19,3},{4,20},{20... | collective-permute-start | bytes 405512 | tf_op jit(solution)/shard_map/ppermute | solution.py:34
  104.3 0.9 collective-permute-done.6
  105.6 0.6 broadcast_in_dim.84
  106.2 23.4 %all-to-all-start = ((f32[16,1,512]{2,1,0:T(1,128)}), f32[16,1,512]{2,1,0:T(1,128)S(1)}, u32[]{:S(2)}, u32[]{:S(2)}) async-start(f32[16,1,512]{2,1,0:T(1,128)} %broadcast_in_dim.84), calls=%async_computation | async-start | bytes 65536 | tf_op jit(solution)/shard_map/all_to_all | solution.py:77
  130.0 6.1 %all-to-all-done = f32[16,1,512]{2,1,0:T(1,128)S(1)} async-done(((f32[16,1,512]{2,1,0:T(1,128)}), f32[16,1,512]{2,1,0:T(1,128)S(1)}, u32[]{:S(2)}, u32[]{:S(2)}) %all-to-all-start) | async-done | bytes 32800 | tf_op jit(solution)/shard_map/all_to_all | solution.py:77
  136.1 0.9 multiply_convert_fusion
  (43 shorter events, 3.4 us)
Async XLA Ops:
  0.0 96.3 %copy-start = (bf16[512,512]{1,0:T(8,128)(2,1)S(1)}, bf16[512,512]{1,0:T(8,128)(2,1)}, u32[]{:S(2)}) copy-start(bf16[512,512]{1,0:T(8,128)(2,1)} %param.4) | copy-start | bytes 1572868
  0.0 5.2 %copy-start.4 = (bf16[512,512]{1,0:T(8,128)(2,1)S(1)}, bf16[512,512]{1,0:T(8,128)(2,1)}, u32[]{:S(2)}) copy-start(bf16[512,512]{1,0:T(8,128)(2,1)} %param.6) | copy-start | bytes 1572868
  5.6 17.2 %collective-permute-start = (f32[520,128]{1,0:T(8,128)S(1)}, f32[520,128]{1,0:T(8,128)S(1)}, u32[]{:S(2)}, u32[]{:S(2)}) collective-permute-start(f32[520,128]{1,0:T(8,128)S(1)} %concatenate.27), channel_id=1, source_target_pairs={{0,16},{16,0},{1,17},{17,1},{2,18},{18,2},{3,19},{19,3},{4,20},{20... | collective-permute-start | bytes 798728 | tf_op jit(solution)/shard_map/ppermute | solution.py:34
  22.8 76.9 %copy-start.2 = (f32[520,128]{1,0:T(8,128)}, f32[520,128]{1,0:T(8,128)S(1)}, u32[]{:S(2)}) copy-start(f32[520,128]{1,0:T(8,128)S(1)} %collective-permute-done) | copy-start | bytes 798724
  24.1 4.1 %collective-permute-start.1 = (f32[264,128]{1,0:T(8,128)S(1)}, f32[264,128]{1,0:T(8,128)S(1)}, u32[]{:S(2)}, u32[]{:S(2)}) collective-permute-start(f32[264,128]{1,0:T(8,128)S(1)} %concatenate.28), channel_id=1, source_target_pairs={{0,32},{32,64},{64,96},{96,128},{128,160},{160,192},{192,224},{224... | collective-permute-start | bytes 405512 | tf_op jit(solution)/shard_map/ppermute | solution.py:45
  29.5 39.3 %copy-start.3 = (s32[512]{0:T(512)S(1)}, s32[512]{0:T(512)}, u32[]{:S(2)}) copy-start(s32[512]{0:T(512)} %param.7) | copy-start | bytes 6148
  29.5 3.6 %collective-permute-start.2 = (f32[264,128]{1,0:T(8,128)S(1)}, f32[264,128]{1,0:T(8,128)S(1)}, u32[]{:S(2)}, u32[]{:S(2)}) collective-permute-start(f32[264,128]{1,0:T(8,128)S(1)} %concatenate.29), channel_id=1, source_target_pairs={{0,64},{32,96},{64,128},{96,160},{128,192},{160,224},{192,256},{22... | collective-permute-start | bytes 405512 | tf_op jit(solution)/shard_map/ppermute | solution.py:45
  34.3 6.3 %collective-permute-start.3 = (f32[264,128]{1,0:T(8,128)S(1)}, f32[264,128]{1,0:T(8,128)S(1)}, u32[]{:S(2)}, u32[]{:S(2)}) collective-permute-start(f32[264,128]{1,0:T(8,128)S(1)} %concatenate.30), channel_id=1, source_target_pairs={{0,128},{32,160},{64,192},{96,224},{128,256},{160,288},{192,320},{... | collective-permute-start | bytes 405512 | tf_op jit(solution)/shard_map/ppermute | solution.py:45
  41.9 29.4 %collective-permute-start.4 = (f32[264,128]{1,0:T(8,128)S(1)}, f32[264,128]{1,0:T(8,128)S(1)}, u32[]{:S(2)}, u32[]{:S(2)}) collective-permute-start(f32[264,128]{1,0:T(8,128)S(1)} %concatenate.31), channel_id=1, source_target_pairs={{0,256},{32,288},{64,320},{96,352},{128,384},{160,416},{192,448},{... | collective-permute-start | bytes 405512 | tf_op jit(solution)/shard_map/ppermute | solution.py:45
  72.5 27.1 %collective-permute-start.5 = (f32[264,128]{1,0:T(8,128)S(1)}, f32[264,128]{1,0:T(8,128)S(1)}, u32[]{:S(2)}, u32[]{:S(2)}) collective-permute-start(f32[264,128]{1,0:T(8,128)S(1)} %concatenate.32), channel_id=1, source_target_pairs={{0,512},{32,544},{64,576},{96,608},{128,640},{160,672},{192,704},{... | collective-permute-start | bytes 405512 | tf_op jit(solution)/shard_map/ppermute | solution.py:45
  101.0 4.2 %copy-start.1 = (f32[512,4,128]{0,2,1:T(8,128)S(1)}, f32[512,4,128]{0,2,1:T(8,128)}, u32[]{:S(2)}) copy-start(f32[512,4,128]{0,2,1:T(8,128)} %fusion.3) | copy-start | bytes 3145732
  101.0 4.2 %slice-start = ((f32[520,128]{1,0:T(8,128)}), f32[512,128]{1,0:T(8,128)S(1)}, s32[]{:S(2)}) async-start(f32[520,128]{1,0:T(8,128)} %copy-done.2), calls=%async_computation.1 | async-start | bytes 524288 | tf_op jit(solution)/shard_map/slice | solution.py:29
  101.1 4.1 %collective-permute-start.6 = (f32[264,128]{1,0:T(8,128)S(1)}, f32[264,128]{1,0:T(8,128)S(1)}, u32[]{:S(2)}, u32[]{:S(2)}) collective-permute-start(f32[264,128]{1,0:T(8,128)S(1)} %concatenate.33), channel_id=1, source_target_pairs={{0,16},{16,0},{1,17},{17,1},{2,18},{18,2},{3,19},{19,3},{4,20},{20... | collective-permute-start | bytes 405512 | tf_op jit(solution)/shard_map/ppermute | solution.py:34
  106.2 29.8 %all-to-all-start = ((f32[16,1,512]{2,1,0:T(1,128)}), f32[16,1,512]{2,1,0:T(1,128)S(1)}, u32[]{:S(2)}, u32[]{:S(2)}) async-start(f32[16,1,512]{2,1,0:T(1,128)} %broadcast_in_dim.84), calls=%async_computation | async-start | bytes 65536 | tf_op jit(solution)/shard_map/all_to_all | solution.py:77

commit v3 on v2

--- a/solution.py
+++ b/solution.py
@@ -8,6 +8,7 @@
 DH = 128
 BLK = 512
 TAG = 8
+GROUP = 4
 
 
 def combine_states(earlier, later):
@@ -34,21 +35,52 @@
     return unpack(lax.ppermute(pack(value), core_axis, [(0, 1), (1, 0)]))
 
 
+def received(value, axis, pairs, valid):
+    state, last = unpack(lax.ppermute(pack(value), axis, pairs))
+    return (jnp.where(valid, state, 0.0), jnp.where(valid, last, -1))
+
+
+def select(cond, a, b):
+    return jax.tree.map(lambda x, y: jnp.where(cond, x, y), a, b)
+
+
 def scan_chips(own, axis):
     count, mine = (lax.axis_size(axis), lax.axis_index(axis))
-    state, last = own
-    excl = (jnp.zeros_like(state), jnp.full_like(last, -1))
-    incl = (state, last)
+    group = GROUP if count % GROUP == 0 else 1
+    groups = count // group
+    offset, which = (mine % group, mine // group)
+    empty = (jnp.zeros_like(own[0]), jnp.full_like(own[1], -1))
+    incl, excl = (own, empty)
     shift = 1
-    while shift < count:
-        pairs = [(j, j + shift) for j in range(count - shift)]
-        got_state, got_last = unpack(lax.ppermute(pack(incl), axis, pairs))
-        got = (got_state, jnp.where(mine >= shift, got_last, -1))
+    while shift < group:
+        pairs = [(j, j + shift) for j in range(count - shift) if j % group + shift < group]
+        got = received(incl, axis, pairs, offset >= shift)
         excl = combine_states(got, excl)
-        if 2 * shift < count:
-            incl = combine_states(got, incl)
+        incl = combine_states(got, incl)
         shift *= 2
-    return excl
+    ends = [group * j + group - 1 for j in range(groups)]
+    upto, before = (incl, empty)
+    shift = 1
+    while shift < groups:
+        pairs = [(ends[j], ends[j + shift]) for j in range(groups - shift)]
+        got = received(upto, axis, pairs, which >= shift)
+        before = combine_states(got, before)
+        if 2 * shift < groups:
+            upto = combine_states(got, upto)
+        shift *= 2
+    through = combine_states(before, incl)
+    carried = before
+    for place in range(group - 1):
+        ahead = place + 1
+        behind = group - 1 - place
+        if ahead <= behind:
+            pairs = [(ends[j], ends[j] + ahead) for j in range(groups - 1)]
+            got = received(through, axis, pairs, which >= 1)
+        else:
+            pairs = [(ends[j], ends[j] - behind) for j in range(groups)]
+            got = received(before, axis, pairs, which >= 0)
+        carried = select(offset == place, got, carried)
+    return combine_states(carried, excl)
 
 
 def carried_in(own, chip_axis, core_axis):

time: 138 us -> 137 us (level)
  the two profiles are of different devices: /device:TPU:1 before, /device:TPU:96 now
where the time goes in v3:
time: 137 us; the launch traced here: 136 us
  starting transfers between devices  63.2 us (46%)
  waiting for transfers between devices  45.1 us (33%)
  local copies, waits for them, and re-layouts  10.8 us (8%)
  between operations  7.75 us (6%)
  other arithmetic  5.59 us (4%)
  matrix products  4.02 us (3%)
    ppermute x8, starting transfers between devices, received(): state, last = unpack(lax.ppermute(pack(value), axis, pairs))  52.1 us
    ppermute x8, waiting for transfers between devices, received(): state, last = unpack(lax.ppermute(pack(value), axis, pairs))  35.1 us
    all_to_all x1, waiting for transfers between devices, head_sum(): return jnp.sum(lax.all_to_all(spread, axis, 0, 0, tiled=True), axis=0)  7.26 us
    slice x9, local copies, waits for them, and re-layouts, unpack(): return (state, packed[-TAG, 0].astype(jnp.int32))  7.1 us
    all_to_all x1, starting transfers between devices, head_sum(): return jnp.sum(lax.all_to_all(spread, axis, 0, 0, tiled=True), axis=0)  7.05 us
    ppermute x2, starting transfers between devices, swap_cores(): return unpack(lax.ppermute(pack(value), core_axis, [(0, 1), (1, 0)]))  3.97 us
    dot_general x1, matrix products, local_block(): jnp.einsum('hts,shd->thd', probs, vb, preferred_element_type=jnp.float32)  3.34 us
    ppermute x2, waiting for transfers between devices, swap_cores(): return unpack(lax.ppermute(pack(value), core_axis, [(0, 1), (1, 0)]))  2.75 us
  transfers between devices with their start and end apart: 11, of which 8 were waited for; matrix products, arithmetic and copies ran while one was open for 5% of the time, Pallas kernels for 0%

profile of v3, /device:TPU:96, one launch (start us, length us, event | category | flops | bytes accessed | tf_op | source)
XLA Modules:
  0.0 136.5 jit_solution(3970259530329375004)
XLA Ops:
  0.0 1.4 slice.67
  1.4 1.3 broadcast_compare_fusion.1
  3.3 1.3 copy.28
  5.6 1.9 %collective-permute-start = (f32[520,128]{1,0:T(8,128)S(1)}, f32[520,128]{1,0:T(8,128)S(1)}, u32[]{:S(2)}, u32[]{:S(2)}) collective-permute-start(f32[520,128]{1,0:T(8,128)S(1)} %concatenate.34), channel_id=1, source_target_pairs={{0,16},{16,0},{1,17},{17,1},{2,18},{18,2},{3,19},{19,3},{4,20},{20... | collective-permute-start | bytes 798728 | tf_op jit(solution)/shard_map/ppermute | solution.py:35
  7.5 1.5 %collective-permute-done = f32[520,128]{1,0:T(8,128)S(1)} collective-permute-done((f32[520,128]{1,0:T(8,128)S(1)}, f32[520,128]{1,0:T(8,128)S(1)}, u32[]{:S(2)}, u32[]{:S(2)}) %collective-permute-start) | collective-permute-done | bytes 266272 | tf_op jit(solution)/shard_map/ppermute | solution.py:35
  10.5 1.3 collective-permute-start.1
  11.8 6.2 %collective-permute-done.1 = f32[264,128]{1,0:T(8,128)S(1)} collective-permute-done((f32[264,128]{1,0:T(8,128)S(1)}, f32[264,128]{1,0:T(8,128)S(1)}, u32[]{:S(2)}, u32[]{:S(2)}) %collective-permute-start.1) | collective-permute-done | bytes 135200 | tf_op jit(solution)/shard_map/ppermute | solution.py:39
  19.4 1.3 collective-permute-start.2
  20.7 15.2 %collective-permute-done.2 = f32[264,128]{1,0:T(8,128)S(1)} collective-permute-done((f32[264,128]{1,0:T(8,128)S(1)}, f32[264,128]{1,0:T(8,128)S(1)}, u32[]{:S(2)}, u32[]{:S(2)}) %collective-permute-start.2) | collective-permute-done | bytes 135200 | tf_op jit(solution)/shard_map/ppermute | solution.py:39
  37.2 2.6 %collective-permute-start.3 = (f32[264,128]{1,0:T(8,128)S(1)}, f32[264,128]{1,0:T(8,128)S(1)}, u32[]{:S(2)}, u32[]{:S(2)}) collective-permute-start(f32[264,128]{1,0:T(8,128)S(1)} %concatenate.37), channel_id=1, source_target_pairs={{96,224},{224,352},{352,480},{480,608},{608,736},{736,864},{864,99... | collective-permute-start | bytes 405512 | tf_op jit(solution)/shard_map/ppermute | solution.py:39
  39.9 2.8 %collective-permute-done.3 = f32[264,128]{1,0:T(8,128)S(1)} collective-permute-done((f32[264,128]{1,0:T(8,128)S(1)}, f32[264,128]{1,0:T(8,128)S(1)}, u32[]{:S(2)}, u32[]{:S(2)}) %collective-permute-start.3) | collective-permute-done | bytes 135200 | tf_op jit(solution)/shard_map/ppermute | solution.py:39
  44.1 15.7 %collective-permute-start.4 = (f32[264,128]{1,0:T(8,128)S(1)}, f32[264,128]{1,0:T(8,128)S(1)}, u32[]{:S(2)}, u32[]{:S(2)}) collective-permute-start(f32[264,128]{1,0:T(8,128)S(1)} %concatenate.38), channel_id=1, source_target_pairs={{96,352},{224,480},{352,608},{480,736},{608,864},{736,992},{97,353... | collective-permute-start | bytes 405512 | tf_op jit(solution)/shard_map/ppermute | solution.py:39
  59.8 2.5 %collective-permute-done.4 = f32[264,128]{1,0:T(8,128)S(1)} collective-permute-done((f32[264,128]{1,0:T(8,128)S(1)}, f32[264,128]{1,0:T(8,128)S(1)}, u32[]{:S(2)}, u32[]{:S(2)}) %collective-permute-start.4) | collective-permute-done | bytes 135200 | tf_op jit(solution)/shard_map/ppermute | solution.py:39
  63.7 25.4 %collective-permute-start.5 = (f32[264,128]{1,0:T(8,128)S(1)}, f32[264,128]{1,0:T(8,128)S(1)}, u32[]{:S(2)}, u32[]{:S(2)}) collective-permute-start(f32[264,128]{1,0:T(8,128)S(1)} %concatenate.39), channel_id=1, source_target_pairs={{96,608},{224,736},{352,864},{480,992},{97,609},{225,737},{353,865... | collective-permute-start | bytes 405512 | tf_op jit(solution)/shard_map/ppermute | solution.py:39
  90.0 8.4 %collective-permute-done.5 = f32[264,128]{1,0:T(8,128)S(1)} collective-permute-done((f32[264,128]{1,0:T(8,128)S(1)}, f32[264,128]{1,0:T(8,128)S(1)}, u32[]{:S(2)}, u32[]{:S(2)}) %collective-permute-start.5) | collective-permute-done | bytes 135200 | tf_op jit(solution)/shard_map/ppermute | solution.py:39
  100.6 2.0 %collective-permute-start.8 = (f32[264,128]{1,0:T(8,128)S(1)}, f32[264,128]{1,0:T(8,128)}, u32[]{:S(2)}, u32[]{:S(2)}) collective-permute-start(f32[264,128]{1,0:T(8,128)S(1)} %concatenate.41), channel_id=1, source_target_pairs={{96,128},{224,256},{352,384},{480,512},{608,640},{736,768},{864,89... | collective-permute-start | bytes 405512 | tf_op jit(solution)/shard_map/ppermute | solution.py:39
  102.6 1.9 %collective-permute-start.7 = (f32[264,128]{1,0:T(8,128)S(1)}, f32[264,128]{1,0:T(8,128)}, u32[]{:S(2)}, u32[]{:S(2)}) collective-permute-start(f32[264,128]{1,0:T(8,128)S(1)} %concatenate.41), channel_id=1, source_target_pairs={{96,160},{224,288},{352,416},{480,544},{608,672},{736,800},{864,92... | collective-permute-start | bytes 405512 | tf_op jit(solution)/shard_map/ppermute | solution.py:39
  104.5 2.0 %collective-permute-start.6 = (f32[264,128]{1,0:T(8,128)S(1)}, f32[264,128]{1,0:T(8,128)}, u32[]{:S(2)}, u32[]{:S(2)}) collective-permute-start(f32[264,128]{1,0:T(8,128)S(1)} %concatenate.40), channel_id=1, source_target_pairs={{96,64},{224,192},{352,320},{480,448},{608,576},{736,704},{864,832... | collective-permute-start | bytes 405512 | tf_op jit(solution)/shard_map/ppermute | solution.py:39
  106.5 3.3 %fusion.3 = f32[512,4,128]{0,2,1:T(8,128)} fusion(bf16[512,4,128]{0,2,1:T(8,128)(2,1)S(1)} %bitcast.81, pred[512,512]{1,0:T(8,128)(4,1)S(1)} %copy-done.3, bf16[512,512]{1,0:T(8,128)(2,1)} %param.6, bf16[512,512]{1,0:T(8,128)(2,1)S(1)} %copy-done), kind=kOutput, calls=%fused_computation.5 | convolution fusion | flops 538968064 | bytes 2883584 | tf_op jit(solution)/shard_map/while/body/eval_jaxpr/hts,shd->thd/dot_general | solution.py:128
  109.9 1.2 slice.105
  116.4 2.1 %collective-permute-start.9 = (f32[264,128]{1,0:T(8,128)S(1)}, f32[264,128]{1,0:T(8,128)S(1)}, u32[]{:S(2)}, u32[]{:S(2)}) collective-permute-start(f32[264,128]{1,0:T(8,128)S(1)} %concatenate.42), channel_id=1, source_target_pairs={{0,16},{16,0},{1,17},{17,1},{2,18},{18,2},{3,19},{19,3},{4,20},{20... | collective-permute-start | bytes 405512 | tf_op jit(solution)/shard_map/ppermute | solution.py:35
  118.5 1.2 collective-permute-done.9
  120.8 7.1 %all-to-all-start = ((f32[16,1,512]{2,1,0:T(1,128)}), f32[16,1,512]{2,1,0:T(1,128)S(1)}, u32[]{:S(2)}, u32[]{:S(2)}) async-start(f32[16,1,512]{2,1,0:T(1,128)} %broadcast_in_dim.102), calls=%async_computation | async-start | bytes 65536 | tf_op jit(solution)/shard_map/all_to_all | solution.py:109
  128.2 7.3 %all-to-all-done = f32[16,1,512]{2,1,0:T(1,128)S(1)} async-done(((f32[16,1,512]{2,1,0:T(1,128)}), f32[16,1,512]{2,1,0:T(1,128)S(1)}, u32[]{:S(2)}, u32[]{:S(2)}) %all-to-all-start) | async-done | bytes 32800 | tf_op jit(solution)/shard_map/all_to_all | solution.py:109
  (60 shorter events, 12.0 us)
Async XLA Ops:
  0.0 106.5 %copy-start = (bf16[512,512]{1,0:T(8,128)(2,1)S(1)}, bf16[512,512]{1,0:T(8,128)(2,1)}, u32[]{:S(2)}) copy-start(bf16[512,512]{1,0:T(8,128)(2,1)} %param.4) | copy-start | bytes 1572868
  0.0 5.2 %copy-start.6 = (bf16[512,512]{1,0:T(8,128)(2,1)S(1)}, bf16[512,512]{1,0:T(8,128)(2,1)}, u32[]{:S(2)}) copy-start(bf16[512,512]{1,0:T(8,128)(2,1)} %param.6) | copy-start | bytes 1572868
  5.6 3.4 %collective-permute-start = (f32[520,128]{1,0:T(8,128)S(1)}, f32[520,128]{1,0:T(8,128)S(1)}, u32[]{:S(2)}, u32[]{:S(2)}) collective-permute-start(f32[520,128]{1,0:T(8,128)S(1)} %concatenate.34), channel_id=1, source_target_pairs={{0,16},{16,0},{1,17},{17,1},{2,18},{18,2},{3,19},{19,3},{4,20},{20... | collective-permute-start | bytes 798728 | tf_op jit(solution)/shard_map/ppermute | solution.py:35
  9.0 100.8 %copy-start.2 = (f32[520,128]{1,0:T(8,128)}, f32[520,128]{1,0:T(8,128)S(1)}, u32[]{:S(2)}) copy-start(f32[520,128]{1,0:T(8,128)S(1)} %collective-permute-done) | copy-start | bytes 798724
  10.5 7.5 %collective-permute-start.1 = (f32[264,128]{1,0:T(8,128)S(1)}, f32[264,128]{1,0:T(8,128)S(1)}, u32[]{:S(2)}, u32[]{:S(2)}) collective-permute-start(f32[264,128]{1,0:T(8,128)S(1)} %concatenate.35), channel_id=1, source_target_pairs={{0,32},{32,64},{64,96},{128,160},{160,192},{192,224},{256,288},{28... | collective-permute-start | bytes 405512 | tf_op jit(solution)/shard_map/ppermute | solution.py:39
  19.4 16.5 %collective-permute-start.2 = (f32[264,128]{1,0:T(8,128)S(1)}, f32[264,128]{1,0:T(8,128)S(1)}, u32[]{:S(2)}, u32[]{:S(2)}) collective-permute-start(f32[264,128]{1,0:T(8,128)S(1)} %concatenate.36), channel_id=1, source_target_pairs={{0,64},{32,96},{128,192},{160,224},{256,320},{288,352},{384,448},{... | collective-permute-start | bytes 405512 | tf_op jit(solution)/shard_map/ppermute | solution.py:39
  37.2 51.9 %copy-start.5 = (s32[512]{0:T(512)S(1)}, s32[512]{0:T(512)}, u32[]{:S(2)}) copy-start(s32[512]{0:T(512)} %param.7) | copy-start | bytes 6148
  37.2 5.5 %collective-permute-start.3 = (f32[264,128]{1,0:T(8,128)S(1)}, f32[264,128]{1,0:T(8,128)S(1)}, u32[]{:S(2)}, u32[]{:S(2)}) collective-permute-start(f32[264,128]{1,0:T(8,128)S(1)} %concatenate.37), channel_id=1, source_target_pairs={{96,224},{224,352},{352,480},{480,608},{608,736},{736,864},{864,99... | collective-permute-start | bytes 405512 | tf_op jit(solution)/shard_map/ppermute | solution.py:39
  44.1 18.3 %collective-permute-start.4 = (f32[264,128]{1,0:T(8,128)S(1)}, f32[264,128]{1,0:T(8,128)S(1)}, u32[]{:S(2)}, u32[]{:S(2)}) collective-permute-start(f32[264,128]{1,0:T(8,128)S(1)} %concatenate.38), channel_id=1, source_target_pairs={{96,352},{224,480},{352,608},{480,736},{608,864},{736,992},{97,353... | collective-permute-start | bytes 405512 | tf_op jit(solution)/shard_map/ppermute | solution.py:39
  63.7 34.7 %collective-permute-start.5 = (f32[264,128]{1,0:T(8,128)S(1)}, f32[264,128]{1,0:T(8,128)S(1)}, u32[]{:S(2)}, u32[]{:S(2)}) collective-permute-start(f32[264,128]{1,0:T(8,128)S(1)} %concatenate.39), channel_id=1, source_target_pairs={{96,608},{224,736},{352,864},{480,992},{97,609},{225,737},{353,865... | collective-permute-start | bytes 405512 | tf_op jit(solution)/shard_map/ppermute | solution.py:39
  98.4 1.2 copy-start.4
  100.6 5.9 %copy-start.3 = (pred[512,512]{1,0:T(8,128)(4,1)S(1)}, pred[512,512]{1,0:T(8,128)(4,1)}, u32[]{:S(2)}) copy-start(pred[512,512]{1,0:T(8,128)(4,1)} %fusion.4) | copy-start | bytes 786436
  100.6 9.2 %collective-permute-start.8 = (f32[264,128]{1,0:T(8,128)S(1)}, f32[264,128]{1,0:T(8,128)}, u32[]{:S(2)}, u32[]{:S(2)}) collective-permute-start(f32[264,128]{1,0:T(8,128)S(1)} %concatenate.41), channel_id=1, source_target_pairs={{96,128},{224,256},{352,384},{480,512},{608,640},{736,768},{864,89... | collective-permute-start | bytes 405512 | tf_op jit(solution)/shard_map/ppermute | solution.py:39
  102.6 9.0 %collective-permute-start.7 = (f32[264,128]{1,0:T(8,128)S(1)}, f32[264,128]{1,0:T(8,128)}, u32[]{:S(2)}, u32[]{:S(2)}) collective-permute-start(f32[264,128]{1,0:T(8,128)S(1)} %concatenate.41), channel_id=1, source_target_pairs={{96,160},{224,288},{352,416},{480,544},{608,672},{736,800},{864,92... | collective-permute-start | bytes 405512 | tf_op jit(solution)/shard_map/ppermute | solution.py:39
  104.5 8.9 %collective-permute-start.6 = (f32[264,128]{1,0:T(8,128)S(1)}, f32[264,128]{1,0:T(8,128)}, u32[]{:S(2)}, u32[]{:S(2)}) collective-permute-start(f32[264,128]{1,0:T(8,128)S(1)} %concatenate.40), channel_id=1, source_target_pairs={{96,64},{224,192},{352,320},{480,448},{608,576},{736,704},{864,832... | collective-permute-start | bytes 405512 | tf_op jit(solution)/shard_map/ppermute | solution.py:39
  116.3 3.4 %copy-start.1 = (f32[512,4,128]{0,2,1:T(8,128)S(1)}, f32[512,4,128]{0,2,1:T(8,128)}, u32[]{:S(2)}) copy-start(f32[512,4,128]{0,2,1:T(8,128)} %fusion.3) | copy-start | bytes 3145732
  116.4 3.4 %slice-start = ((f32[520,128]{1,0:T(8,128)}), f32[512,128]{1,0:T(8,128)S(1)}, s32[]{:S(2)}) async-start(f32[520,128]{1,0:T(8,128)} %copy-done.2), calls=%async_computation.1 | async-start | bytes 524288 | tf_op jit(solution)/shard_map/slice | solution.py:30
  116.4 3.4 %collective-permute-start.9 = (f32[264,128]{1,0:T(8,128)S(1)}, f32[264,128]{1,0:T(8,128)S(1)}, u32[]{:S(2)}, u32[]{:S(2)}) collective-permute-start(f32[264,128]{1,0:T(8,128)S(1)} %concatenate.42), channel_id=1, source_target_pairs={{0,16},{16,0},{1,17},{17,1},{2,18},{18,2},{3,19},{19,3},{4,20},{20... | collective-permute-start | bytes 405512 | tf_op jit(solution)/shard_map/ppermute | solution.py:35
  120.8 14.7 %all-to-all-start = ((f32[16,1,512]{2,1,0:T(1,128)}), f32[16,1,512]{2,1,0:T(1,128)S(1)}, u32[]{:S(2)}, u32[]{:S(2)}) async-start(f32[16,1,512]{2,1,0:T(1,128)} %broadcast_in_dim.102), calls=%async_computation | async-start | bytes 65536 | tf_op jit(solution)/shard_map/all_to_all | solution.py:109

commit v4 on v3

--- a/solution.py
+++ b/solution.py
@@ -31,17 +31,24 @@
     return (state, packed[-TAG, 0].astype(jnp.int32))
 
 
-def swap_cores(value, core_axis):
-    return unpack(lax.ppermute(pack(value), core_axis, [(0, 1), (1, 0)]))
+def tag_of(packed):
+    return packed[-TAG:-TAG + 1, :1]
 
 
-def received(value, axis, pairs, valid):
-    state, last = unpack(lax.ppermute(pack(value), axis, pairs))
-    return (jnp.where(valid, state, 0.0), jnp.where(valid, last, -1))
+def combine_packed(earlier, later):
+    last_e, last_l = (tag_of(earlier), tag_of(later))
+    is_tag = lax.broadcasted_iota(jnp.int32, later.shape, 0) >= later.shape[0] - TAG
+    joined = later + jnp.where(last_e == last_l, earlier, 0.0)
+    return jnp.where(last_l < 0, earlier, jnp.where(is_tag, later, joined))
 
 
-def select(cond, a, b):
-    return jax.tree.map(lambda x, y: jnp.where(cond, x, y), a, b)
+def empty_like(packed):
+    is_tag = lax.broadcasted_iota(jnp.int32, packed.shape, 0) >= packed.shape[0] - TAG
+    return jnp.where(is_tag, -1.0, 0.0).astype(packed.dtype)
+
+
+def received(packed, axis, pairs, valid):
+    return jnp.where(valid, lax.ppermute(packed, axis, pairs), empty_like(packed))
 
 
 def scan_chips(own, axis):
@@ -49,14 +56,14 @@
     group = GROUP if count % GROUP == 0 else 1
     groups = count // group
     offset, which = (mine % group, mine // group)
-    empty = (jnp.zeros_like(own[0]), jnp.full_like(own[1], -1))
+    empty = empty_like(own)
     incl, excl = (own, empty)
     shift = 1
     while shift < group:
         pairs = [(j, j + shift) for j in range(count - shift) if j % group + shift < group]
         got = received(incl, axis, pairs, offset >= shift)
-        excl = combine_states(got, excl)
-        incl = combine_states(got, incl)
+        excl = combine_packed(got, excl)
+        incl = combine_packed(got, incl)
         shift *= 2
     ends = [group * j + group - 1 for j in range(groups)]
     upto, before = (incl, empty)
@@ -64,11 +71,11 @@
     while shift < groups:
         pairs = [(ends[j], ends[j + shift]) for j in range(groups - shift)]
         got = received(upto, axis, pairs, which >= shift)
-        before = combine_states(got, before)
+        before = combine_packed(got, before)
         if 2 * shift < groups:
-            upto = combine_states(got, upto)
+            upto = combine_packed(got, upto)
         shift *= 2
-    through = combine_states(before, incl)
+    through = combine_packed(before, incl)
     carried = before
     for place in range(group - 1):
         ahead = place + 1
@@ -79,28 +86,34 @@
         else:
             pairs = [(ends[j], ends[j] - behind) for j in range(groups)]
             got = received(before, axis, pairs, which >= 0)
-        carried = select(offset == place, got, carried)
-    return combine_states(carried, excl)
+        carried = jnp.where(offset == place, got, carried)
+    return combine_packed(carried, excl)
 
 
 def carried_in(own, chip_axis, core_axis):
     core = lax.axis_index(core_axis)
-    other = swap_cores(own, core_axis)
-    first = jax.tree.map(lambda a, b: jnp.where(core == 0, a, b), own, other)
-    second = jax.tree.map(lambda a, b: jnp.where(core == 0, b, a), own, other)
-    chip = combine_states(first, second)
-    empty = (jnp.zeros_like(own[0]), jnp.full_like(own[1], -1))
-    in_chip = jax.tree.map(lambda a, b: jnp.where(core == 0, a, b), empty, first)
-    half = chip[0].shape[0] // 2
-    mine = jnp.where(core == 0, chip[0][:half], chip[0][half:])
-    before = scan_chips((mine, chip[1]), chip_axis)
-    theirs = swap_cores(before, core_axis)
+    swap = [(0, 1), (1, 0)]
+    own_p = pack(own)
+    other = lax.ppermute(own_p, core_axis, swap)
+    first = jnp.where(core == 0, own_p, other)
+    second = jnp.where(core == 0, other, own_p)
+    chip = combine_packed(first, second)
+    in_chip = jnp.where(core == 0, empty_like(own_p), first)
+    rows = own[0].shape[0] * DH // 2
+    tag = chip[-TAG:]
+    mine = jnp.where(
+        core == 0,
+        jnp.concatenate([chip[:rows], tag], axis=0),
+        jnp.concatenate([chip[rows:2 * rows], tag], axis=0),
+    )
+    before = scan_chips(mine, chip_axis)
+    theirs = lax.ppermute(before, core_axis, swap)
     whole = jnp.where(
         core == 0,
-        jnp.concatenate([before[0], theirs[0]], axis=0),
-        jnp.concatenate([theirs[0], before[0]], axis=0),
+        jnp.concatenate([before[:rows], theirs[:rows], before[rows:]], axis=0),
+        jnp.concatenate([theirs[:rows], before[:rows], before[rows:]], axis=0),
     )
-    return combine_states((whole, before[1]), in_chip)
+    return unpack(combine_packed(whole, in_chip))
 
 
 def head_sum(x, axis):
@@ -136,26 +149,33 @@
         )
         return (intra, kv_sum, block_last)
 
-    intra_all, kv_all, last_all = lax.map(local_block, (q_all, k_all, v_all, s_all))
-    empty_state = (jnp.zeros((heads, DH, DH), jnp.float32), jnp.int32(-1))
-
-    def fold_local(carry, item):
-        return (combine_states(carry, item), None)
-
-    own_state, _ = lax.scan(fold_local, empty_state, (kv_all, last_all))
-    prefix = carried_in(own_state, "chip", "core")
-
-    def inter_block(carry, item):
-        qb, sb, kv_sum, block_last = item
-        state, last = carry
+    def inter_of(qb, sb, state, last):
         inter = jnp.einsum(
             "thd,hde->the", qb, state.astype(jnp.bfloat16), preferred_element_type=jnp.float32
         )
-        inter = jnp.where((sb == last)[:, None, None], inter, 0.0)
-        return (combine_states(carry, (kv_sum, block_last)), inter)
+        return jnp.where((sb == last)[:, None, None], inter, 0.0)
 
-    _, inter_all = lax.scan(inter_block, prefix, (q_all, s_all, kv_all, last_all))
-    outputs = (intra_all + inter_all).reshape(rows, heads * DH)
+    if blocks == 1:
+        intra, kv_sum, block_last = local_block((q_all[0], k_all[0], v_all[0], s_all[0]))
+        state, last = carried_in((kv_sum, block_last), "chip", "core")
+        outputs = (intra + inter_of(q_all[0], s_all[0], state, last)).reshape(rows, heads * DH)
+    else:
+        intra_all, kv_all, last_all = lax.map(local_block, (q_all, k_all, v_all, s_all))
+        empty_state = (jnp.zeros((heads, DH, DH), jnp.float32), jnp.int32(-1))
+
+        def fold_local(carry, item):
+            return (combine_states(carry, item), None)
+
+        own_state, _ = lax.scan(fold_local, empty_state, (kv_all, last_all))
+        prefix = carried_in(own_state, "chip", "core")
+
+        def inter_block(carry, item):
+            qb, sb, kv_sum, block_last = item
+            inter = inter_of(qb, sb, *carry)
+            return (combine_states(carry, (kv_sum, block_last)), inter)
+
+        _, inter_all = lax.scan(inter_block, prefix, (q_all, s_all, kv_all, last_all))
+        outputs = (intra_all + inter_all).reshape(rows, heads * DH)
     squares = jnp.sum(outputs * outputs, axis=1)
     totals = head_sum(squares, "head")
     scaled = outputs * lax.rsqrt(totals / (HEADS * DH) + 1e-05)[:, None]

time: 137 us -> 148 us (1.080)
  the two profiles are of different devices: /device:TPU:96 before, /device:TPU:64 now
where the time goes in v4:
time: 148 us
  waiting for transfers between devices  78.9 us (53%)
  between operations  25.7 us (17%)
  starting transfers between devices  20.6 us (14%)
  local copies, waits for them, and re-layouts  14.8 us (10%)
  other arithmetic  4.53 us (3%)
  matrix products  2.97 us (2%)
    ppermute x8, waiting for transfers between devices, received(): lax.ppermute(packed, axis, pairs)  70.1 us
    slice x20, local copies, waits for them, and re-layouts, tag_of(): return packed[-TAG:-TAG + 1, :1]  10.7 us
    ppermute x8, starting transfers between devices, received(): lax.ppermute(packed, axis, pairs)  9.76 us
    all_to_all x1, waiting for transfers between devices, head_sum(): return jnp.sum(lax.all_to_all(spread, axis, 0, 0, tiled=True), axis=0)  7.26 us
    all_to_all x1, starting transfers between devices, head_sum(): return jnp.sum(lax.all_to_all(spread, axis, 0, 0, tiled=True), axis=0)  7.01 us
  transfers between devices with their start and end apart: 11, of which 5 were waited for; matrix products, arithmetic and copies ran while one was open for 6% of the time, Pallas kernels for 0%

profile of v4, /device:TPU:64, one launch (start us, length us, event | category | flops | bytes accessed | tf_op | source)
XLA Modules:
  0.0 147.6 jit_solution(3188277808236100702)
XLA Ops:
  0.0 1.4 slice.102
  1.4 1.3 broadcast_compare_fusion.1
  3.3 1.3 copy.35
  4.9 1.9 %collective-permute-start = (f32[520,128]{1,0:T(8,128)S(1)}, f32[520,128]{1,0:T(8,128)S(1)}, u32[]{:S(2)}, u32[]{:S(2)}) collective-permute-start(f32[520,128]{1,0:T(8,128)S(1)} %concatenate.16), channel_id=1, source_target_pairs={{0,16},{16,0},{1,17},{17,1},{2,18},{18,2},{3,19},{19,3},{4,20},{20... | collective-permute-start | bytes 798728 | tf_op jit(solution)/shard_map/ppermute | solution.py:97
  6.9 1.5 %collective-permute-done = f32[520,128]{1,0:T(8,128)S(1)} collective-permute-done((f32[520,128]{1,0:T(8,128)S(1)}, f32[520,128]{1,0:T(8,128)S(1)}, u32[]{:S(2)}, u32[]{:S(2)}) %collective-permute-start) | collective-permute-done | bytes 266272 | tf_op jit(solution)/shard_map/ppermute | solution.py:97
  11.7 3.8 %collective-permute-start.1 = (f32[264,128]{1,0:T(8,128)S(1)}, f32[264,128]{1,0:T(8,128)S(1)}, u32[]{:S(2)}, u32[]{:S(2)}) collective-permute-start(f32[264,128]{1,0:T(8,128)S(1)} %slice_select_fusion), channel_id=1, source_target_pairs={{0,32},{32,64},{64,96},{128,160},{160,192},{192,224},{256,288},{28... | collective-permute-start | bytes 405512 | tf_op jit(solution)/shard_map/ppermute | solution.py:51
  15.6 0.6 slice.104
  17.9 1.3 collective-permute-done.1
  22.5 1.3 collective-permute-start.2
  26.2 10.5 %collective-permute-done.2 = f32[264,128]{1,0:T(8,128)S(1)} collective-permute-done((f32[264,128]{1,0:T(8,128)S(1)}, f32[264,128]{1,0:T(8,128)S(1)}, u32[]{:S(2)}, u32[]{:S(2)}) %collective-permute-start.2) | collective-permute-done | bytes 135200 | tf_op jit(solution)/shard_map/ppermute | solution.py:51
  40.0 0.7 collective-permute-start.3
  45.3 0.7 collective-permute-start.4
  51.8 0.7 collective-permute-start.5
  52.5 0.6 slice.145
  57.8 0.7 collective-permute-start.7
  58.5 0.7 collective-permute-start.8
  59.2 1.3 collective-permute-start.6
  61.9 58.4 %collective-permute-done.6 = f32[264,128]{1,0:T(8,128)S(1)} collective-permute-done((f32[264,128]{1,0:T(8,128)S(1)}, f32[264,128]{1,0:T(8,128)S(1)}, u32[]{:S(2)}, u32[]{:S(2)}) %collective-permute-start.6) | collective-permute-done | bytes 135200 | tf_op jit(solution)/shard_map/ppermute | solution.py:51
  122.3 1.9 %collective-permute-start.9 = (f32[264,128]{1,0:T(8,128)S(1)}, f32[264,128]{1,0:T(8,128)S(1)}, u32[]{:S(2)}, u32[]{:S(2)}) collective-permute-start(f32[264,128]{1,0:T(8,128)S(1)} %fusion.29), channel_id=1, source_target_pairs={{0,16},{16,0},{1,17},{17,1},{2,18},{18,2},{3,19},{19,3},{4,20},{20... | collective-permute-start | bytes 405512 | tf_op jit(solution)/shard_map/ppermute | solution.py:110
  124.3 2.3 %fusion.3 = f32[512,4,128]{0,2,1:T(8,128)} fusion(bf16[512,4,128]{0,2,1:T(8,128)(2,1)S(1)} %bitcast.71, pred[512,512]{1,0:T(8,128)(4,1)S(1)} %fusion.4, bf16[512,512]{1,0:T(8,128)(2,1)S(1)} %copy-done.3, bf16[512,512]{1,0:T(8,128)(2,1)S(1)} %copy-done), kind=kOutput, calls=%fused_computation.5 | convolution fusion | flops 538968064 | bytes 2883584 | tf_op jit(solution)/shard_map/hts,shd->thd/dot_general | solution.py:141
  131.3 0.6 broadcast_in_dim.345
  132.0 7.0 %all-to-all-start = ((f32[16,1,512]{2,1,0:T(1,128)}), f32[16,1,512]{2,1,0:T(1,128)S(1)}, u32[]{:S(2)}, u32[]{:S(2)}) async-start(f32[16,1,512]{2,1,0:T(1,128)} %broadcast_in_dim.345), calls=%async_computation | async-start | bytes 65536 | tf_op jit(solution)/shard_map/all_to_all | solution.py:122
  139.3 7.3 %all-to-all-done = f32[16,1,512]{2,1,0:T(1,128)S(1)} async-done(((f32[16,1,512]{2,1,0:T(1,128)}), f32[16,1,512]{2,1,0:T(1,128)S(1)}, u32[]{:S(2)}, u32[]{:S(2)}) %all-to-all-start) | async-done | bytes 32800 | tf_op jit(solution)/shard_map/all_to_all | solution.py:122
  146.6 0.9 multiply_convert_fusion
  (69 shorter events, 13.4 us)
Async XLA Ops:
  0.0 124.3 %copy-start = (bf16[512,512]{1,0:T(8,128)(2,1)S(1)}, bf16[512,512]{1,0:T(8,128)(2,1)}, u32[]{:S(2)}) copy-start(bf16[512,512]{1,0:T(8,128)(2,1)} %param.4) | copy-start | bytes 1572868
  0.0 4.6 %copy-start.3 = (bf16[512,512]{1,0:T(8,128)(2,1)S(1)}, bf16[512,512]{1,0:T(8,128)(2,1)}, u32[]{:S(2)}) copy-start(bf16[512,512]{1,0:T(8,128)(2,1)} %param.6) | copy-start | bytes 1572868
  4.9 3.4 %collective-permute-start = (f32[520,128]{1,0:T(8,128)S(1)}, f32[520,128]{1,0:T(8,128)S(1)}, u32[]{:S(2)}, u32[]{:S(2)}) collective-permute-start(f32[520,128]{1,0:T(8,128)S(1)} %concatenate.16), channel_id=1, source_target_pairs={{0,16},{16,0},{1,17},{17,1},{2,18},{18,2},{3,19},{19,3},{4,20},{20... | collective-permute-start | bytes 798728 | tf_op jit(solution)/shard_map/ppermute | solution.py:97
  11.7 7.5 %collective-permute-start.1 = (f32[264,128]{1,0:T(8,128)S(1)}, f32[264,128]{1,0:T(8,128)S(1)}, u32[]{:S(2)}, u32[]{:S(2)}) collective-permute-start(f32[264,128]{1,0:T(8,128)S(1)} %slice_select_fusion), channel_id=1, source_target_pairs={{0,32},{32,64},{64,96},{128,160},{160,192},{192,224},{256,288},{28... | collective-permute-start | bytes 405512 | tf_op jit(solution)/shard_map/ppermute | solution.py:51
  22.5 14.1 %collective-permute-start.2 = (f32[264,128]{1,0:T(8,128)S(1)}, f32[264,128]{1,0:T(8,128)S(1)}, u32[]{:S(2)}, u32[]{:S(2)}) collective-permute-start(f32[264,128]{1,0:T(8,128)S(1)} %get-tuple-element.11), channel_id=1, source_target_pairs={{0,64},{32,96},{128,192},{160,224},{256,320},{288,352},{384,448},{... | collective-permute-start | bytes 405512 | tf_op jit(solution)/shard_map/ppermute | solution.py:51
  40.0 1.9 %collective-permute-start.3 = (f32[264,128]{1,0:T(8,128)S(1)}, f32[264,128]{1,0:T(8,128)S(1)}, u32[]{:S(2)}, u32[]{:S(2)}) collective-permute-start(f32[264,128]{1,0:T(8,128)S(1)} %get-tuple-element.9), channel_id=1, source_target_pairs={{96,224},{224,352},{352,480},{480,608},{608,736},{736,864},{864,99... | collective-permute-start | bytes 405512 | tf_op jit(solution)/shard_map/ppermute | solution.py:51
  45.3 3.2 %collective-permute-start.4 = (f32[264,128]{1,0:T(8,128)S(1)}, f32[264,128]{1,0:T(8,128)S(1)}, u32[]{:S(2)}, u32[]{:S(2)}) collective-permute-start(f32[264,128]{1,0:T(8,128)S(1)} %get-tuple-element.15), channel_id=1, source_target_pairs={{96,352},{224,480},{352,608},{480,736},{608,864},{736,992},{97,353... | collective-permute-start | bytes 405512 | tf_op jit(solution)/shard_map/ppermute | solution.py:51
  46.0 14.5 %copy-start.2 = (s32[512]{0:T(512)S(1)}, s32[512]{0:T(512)}, u32[]{:S(2)}) copy-start(s32[512]{0:T(512)} %param.7) | copy-start | bytes 6148
  51.8 2.0 %collective-permute-start.5 = (f32[264,128]{1,0:T(8,128)S(1)}, f32[264,128]{1,0:T(8,128)S(1)}, u32[]{:S(2)}, u32[]{:S(2)}) collective-permute-start(f32[264,128]{1,0:T(8,128)S(1)} %get-tuple-element.13), channel_id=1, source_target_pairs={{96,608},{224,736},{352,864},{480,992},{97,609},{225,737},{353,865... | collective-permute-start | bytes 405512 | tf_op jit(solution)/shard_map/ppermute | solution.py:51
  57.8 4.1 %collective-permute-start.7 = (f32[264,128]{1,0:T(8,128)S(1)}, f32[264,128]{1,0:T(8,128)S(1)}, u32[]{:S(2)}, u32[]{:S(2)}) collective-permute-start(f32[264,128]{1,0:T(8,128)S(1)} %fusion.28), channel_id=1, source_target_pairs={{96,160},{224,288},{352,416},{480,544},{608,672},{736,800},{864,92... | collective-permute-start | bytes 405512 | tf_op jit(solution)/shard_map/ppermute | solution.py:51
  58.5 3.4 %collective-permute-start.8 = (f32[264,128]{1,0:T(8,128)S(1)}, f32[264,128]{1,0:T(8,128)S(1)}, u32[]{:S(2)}, u32[]{:S(2)}) collective-permute-start(f32[264,128]{1,0:T(8,128)S(1)} %fusion.28), channel_id=1, source_target_pairs={{96,128},{224,256},{352,384},{480,512},{608,640},{736,768},{864,89... | collective-permute-start | bytes 405512 | tf_op jit(solution)/shard_map/ppermute | solution.py:51
  59.2 61.1 %collective-permute-start.6 = (f32[264,128]{1,0:T(8,128)S(1)}, f32[264,128]{1,0:T(8,128)S(1)}, u32[]{:S(2)}, u32[]{:S(2)}) collective-permute-start(f32[264,128]{1,0:T(8,128)S(1)} %fusion.27), channel_id=1, source_target_pairs={{96,64},{224,192},{352,320},{480,448},{608,576},{736,704},{864,832... | collective-permute-start | bytes 405512 | tf_op jit(solution)/shard_map/ppermute | solution.py:51
  122.3 5.4 %collective-permute-start.9 = (f32[264,128]{1,0:T(8,128)S(1)}, f32[264,128]{1,0:T(8,128)S(1)}, u32[]{:S(2)}, u32[]{:S(2)}) collective-permute-start(f32[264,128]{1,0:T(8,128)S(1)} %fusion.29), channel_id=1, source_target_pairs={{0,16},{16,0},{1,17},{17,1},{2,18},{18,2},{3,19},{19,3},{4,20},{20... | collective-permute-start | bytes 405512 | tf_op jit(solution)/shard_map/ppermute | solution.py:110
  127.7 3.2 %copy-start.1 = (f32[512,4,128]{0,2,1:T(8,128)S(1)}, f32[512,4,128]{0,2,1:T(8,128)}, u32[]{:S(2)}) copy-start(f32[512,4,128]{0,2,1:T(8,128)} %fusion.3) | copy-start | bytes 3145732
  132.0 14.6 %all-to-all-start = ((f32[16,1,512]{2,1,0:T(1,128)}), f32[16,1,512]{2,1,0:T(1,128)S(1)}, u32[]{:S(2)}, u32[]{:S(2)}) async-start(f32[16,1,512]{2,1,0:T(1,128)} %broadcast_in_dim.345), calls=%async_computation | async-start | bytes 65536 | tf_op jit(solution)/shard_map/all_to_all | solution.py:122

commit v5 on v3

--- a/solution.py
+++ b/solution.py
@@ -93,7 +93,8 @@
     in_chip = jax.tree.map(lambda a, b: jnp.where(core == 0, a, b), empty, first)
     half = chip[0].shape[0] // 2
     mine = jnp.where(core == 0, chip[0][:half], chip[0][half:])
-    before = scan_chips((mine, chip[1]), chip_axis)
+    parts = [scan_chips((mine[i:i + 1], chip[1]), chip_axis) for i in range(half)]
+    before = (jnp.concatenate([p[0] for p in parts], axis=0), parts[0][1])
     theirs = swap_cores(before, core_axis)
     whole = jnp.where(
         core == 0,

time: 137 us -> 153 us (1.12)
  the two profiles are of different devices: /device:TPU:96 before, /device:TPU:64 now
where the time goes in v5:
time: 153 us; the launch traced here: 152 us
  waiting for transfers between devices  90.5 us (59%)
  starting transfers between devices  30.5 us (20%)
  between operations  13.2 us (9%)
  local copies, waits for them, and re-layouts  12.2 us (8%)
  matrix products  3.21 us (2%)
  other arithmetic  2.19 us (1%)
    ppermute x16, waiting for transfers between devices, received(): state, last = unpack(lax.ppermute(pack(value), axis, pairs))  80.5 us
    ppermute x16, starting transfers between devices, received(): state, last = unpack(lax.ppermute(pack(value), axis, pairs))  19.6 us
    slice x17, local copies, waits for them, and re-layouts, unpack(): return (state, packed[-TAG, 0].astype(jnp.int32))  9 us
    all_to_all x1, waiting for transfers between devices, head_sum(): return jnp.sum(lax.all_to_all(spread, axis, 0, 0, tiled=True), axis=0)  7.26 us
    all_to_all x1, starting transfers between devices, head_sum(): return jnp.sum(lax.all_to_all(spread, axis, 0, 0, tiled=True), axis=0)  7.03 us
    ppermute x2, starting transfers between devices, swap_cores(): return unpack(lax.ppermute(pack(value), core_axis, [(0, 1), (1, 0)]))  3.84 us
  transfers between devices with their start and end apart: 19, of which 9 were waited for; matrix products, arithmetic and copies ran while one was open for 6% of the time, Pallas kernels for 0%

profile of v5, /device:TPU:64, one launch (start us, length us, event | category | flops | bytes accessed | tf_op | source)
XLA Modules:
  0.0 151.8 jit_solution(1018330959070640351)
XLA Ops:
  0.0 1.3 copy.28
  4.1 1.9 %collective-permute-start = (f32[520,128]{1,0:T(8,128)S(1)}, f32[520,128]{1,0:T(8,128)S(1)}, u32[]{:S(2)}, u32[]{:S(2)}) collective-permute-start(f32[520,128]{1,0:T(8,128)S(1)} %concatenate.61), channel_id=1, source_target_pairs={{0,16},{16,0},{1,17},{17,1},{2,18},{18,2},{3,19},{19,3},{4,20},{20... | collective-permute-start | bytes 798728 | tf_op jit(solution)/shard_map/ppermute | solution.py:35
  6.1 1.5 collective-permute-done
  8.9 3.8 %collective-permute-start.9 = (f32[136,128]{1,0:T(8,128)S(1)}, f32[136,128]{1,0:T(8,128)S(1)}, u32[]{:S(2)}, u32[]{:S(2)}) collective-permute-start(f32[136,128]{1,0:T(8,128)S(1)} %concatenate.69), channel_id=1, source_target_pairs={{0,32},{32,64},{64,96},{128,160},{160,192},{192,224},{256,288},{28... | collective-permute-start | bytes 208904 | tf_op jit(solution)/shard_map/ppermute | solution.py:39
  12.8 2.3 %collective-permute-done.9 = f32[136,128]{1,0:T(8,128)S(1)} collective-permute-done((f32[136,128]{1,0:T(8,128)S(1)}, f32[136,128]{1,0:T(8,128)S(1)}, u32[]{:S(2)}, u32[]{:S(2)}) %collective-permute-start.9) | collective-permute-done | bytes 69664 | tf_op jit(solution)/shard_map/ppermute | solution.py:39
  16.3 1.3 collective-permute-start.10
  17.7 3.8 %collective-permute-start.1 = (f32[136,128]{1,0:T(8,128)S(1)}, f32[136,128]{1,0:T(8,128)S(1)}, u32[]{:S(2)}, u32[]{:S(2)}) collective-permute-start(f32[136,128]{1,0:T(8,128)S(1)} %concatenate.62), channel_id=1, source_target_pairs={{0,32},{32,64},{64,96},{128,160},{160,192},{192,224},{256,288},{28... | collective-permute-start | bytes 208904 | tf_op jit(solution)/shard_map/ppermute | solution.py:39
  21.5 7.9 %collective-permute-done.10 = f32[136,128]{1,0:T(8,128)S(1)} collective-permute-done((f32[136,128]{1,0:T(8,128)S(1)}, f32[136,128]{1,0:T(8,128)S(1)}, u32[]{:S(2)}, u32[]{:S(2)}) %collective-permute-start.10) | collective-permute-done | bytes 69664 | tf_op jit(solution)/shard_map/ppermute | solution.py:39
  30.6 1.7 %collective-permute-done.1 = f32[136,128]{1,0:T(8,128)S(1)} collective-permute-done((f32[136,128]{1,0:T(8,128)S(1)}, f32[136,128]{1,0:T(8,128)S(1)}, u32[]{:S(2)}, u32[]{:S(2)}) %collective-permute-start.1) | collective-permute-done | bytes 69664 | tf_op jit(solution)/shard_map/ppermute | solution.py:39
  33.5 0.7 collective-permute-start.11
  34.4 1.3 collective-permute-start.2
  37.7 3.9 %collective-permute-done.2 = f32[136,128]{1,0:T(8,128)S(1)} collective-permute-done((f32[136,128]{1,0:T(8,128)S(1)}, f32[136,128]{1,0:T(8,128)S(1)}, u32[]{:S(2)}, u32[]{:S(2)}) %collective-permute-start.2) | collective-permute-done | bytes 69664 | tf_op jit(solution)/shard_map/ppermute | solution.py:39
  47.3 2.5 %fusion.3 = f32[512,4,128]{0,2,1:T(8,128)S(1)} fusion(bf16[512,4,128]{0,2,1:T(8,128)(2,1)} %bitcast.192, pred[512,512]{1,0:T(8,128)(4,1)S(1)} %fusion.4, bf16[512,512]{1,0:T(8,128)(2,1)} %param.6, bf16[512,512]{1,0:T(8,128)(2,1)S(1)} %copy-done), kind=kOutput, calls=%fused_computation.5 | convolution fusion | flops 538968064 | bytes 2883584 | tf_op jit(solution)/shard_map/while/body/eval_jaxpr/hts,shd->thd/dot_general | solution.py:129
  53.8 0.7 collective-permute-start.15
  54.5 1.3 collective-permute-start.14
  57.1 0.8 collective-permute-start.8
  58.6 59.8 %collective-permute-done.14 = f32[136,128]{1,0:T(8,128)S(1)} collective-permute-done((f32[136,128]{1,0:T(8,128)S(1)}, f32[136,128]{1,0:T(8,128)S(1)}, u32[]{:S(2)}, u32[]{:S(2)}) %collective-permute-start.14) | collective-permute-done | bytes 69664 | tf_op jit(solution)/shard_map/ppermute | solution.py:39
  122.0 1.3 collective-permute-start.6
  123.3 4.8 %collective-permute-done.6 = f32[136,128]{1,0:T(8,128)S(1)} collective-permute-done((f32[136,128]{1,0:T(8,128)S(1)}, f32[136,128]{1,0:T(8,128)S(1)}, u32[]{:S(2)}, u32[]{:S(2)}) %collective-permute-start.6) | collective-permute-done | bytes 69664 | tf_op jit(solution)/shard_map/ppermute | solution.py:39
  131.9 1.9 %collective-permute-start.17 = (f32[264,128]{1,0:T(8,128)S(1)}, f32[264,128]{1,0:T(8,128)S(1)}, u32[]{:S(2)}, u32[]{:S(2)}) collective-permute-start(f32[264,128]{1,0:T(8,128)S(1)} %concatenate.77), channel_id=1, source_target_pairs={{0,16},{16,0},{1,17},{17,1},{2,18},{18,2},{3,19},{19,3},{4,20},{20... | collective-permute-start | bytes 405512 | tf_op jit(solution)/shard_map/ppermute | solution.py:35
  133.8 1.3 collective-permute-done.17
  136.1 7.0 %all-to-all-start = ((f32[16,1,512]{2,1,0:T(1,128)}), f32[16,1,512]{2,1,0:T(1,128)S(1)}, u32[]{:S(2)}, u32[]{:S(2)}) async-start(f32[16,1,512]{2,1,0:T(1,128)} %broadcast_in_dim.115), calls=%async_computation | async-start | bytes 65536 | tf_op jit(solution)/shard_map/all_to_all | solution.py:110
  143.5 7.3 %all-to-all-done = f32[16,1,512]{2,1,0:T(1,128)S(1)} async-done(((f32[16,1,512]{2,1,0:T(1,128)}), f32[16,1,512]{2,1,0:T(1,128)S(1)}, u32[]{:S(2)}, u32[]{:S(2)}) %all-to-all-start) | async-done | bytes 32800 | tf_op jit(solution)/shard_map/all_to_all | solution.py:110
  150.8 0.9 multiply_convert_fusion
  (88 shorter events, 17.4 us)
Async XLA Ops:
  0.0 47.3 %copy-start = (bf16[512,512]{1,0:T(8,128)(2,1)S(1)}, bf16[512,512]{1,0:T(8,128)(2,1)}, u32[]{:S(2)}) copy-start(bf16[512,512]{1,0:T(8,128)(2,1)} %param.4) | copy-start | bytes 1572868
  0.0 3.8 %copy-start.4 = (bf16[512,512]{1,0:T(8,128)(2,1)S(1)}, bf16[512,512]{1,0:T(8,128)(2,1)}, u32[]{:S(2)}) copy-start(bf16[512,512]{1,0:T(8,128)(2,1)} %param.6) | copy-start | bytes 1572868
  1.4 2.7 %copy-start.2 = (bf16[512,512]{0,1:T(8,128)(2,1)}, bf16[512,512]{0,1:T(8,128)(2,1)S(1)}, u32[]{:S(2)}) copy-start(bf16[512,512]{0,1:T(8,128)(2,1)S(1)} %copy.28) | copy-start | bytes 1572868
  4.1 3.4 %collective-permute-start = (f32[520,128]{1,0:T(8,128)S(1)}, f32[520,128]{1,0:T(8,128)S(1)}, u32[]{:S(2)}, u32[]{:S(2)}) collective-permute-start(f32[520,128]{1,0:T(8,128)S(1)} %concatenate.61), channel_id=1, source_target_pairs={{0,16},{16,0},{1,17},{17,1},{2,18},{18,2},{3,19},{19,3},{4,20},{20... | collective-permute-start | bytes 798728 | tf_op jit(solution)/shard_map/ppermute | solution.py:35
  7.6 42.3 %copy-start.1 = (f32[520,128]{1,0:T(8,128)}, f32[520,128]{1,0:T(8,128)S(1)}, u32[]{:S(2)}) copy-start(f32[520,128]{1,0:T(8,128)S(1)} %collective-permute-done) | copy-start | bytes 798724
  8.9 6.2 %collective-permute-start.9 = (f32[136,128]{1,0:T(8,128)S(1)}, f32[136,128]{1,0:T(8,128)S(1)}, u32[]{:S(2)}, u32[]{:S(2)}) collective-permute-start(f32[136,128]{1,0:T(8,128)S(1)} %concatenate.69), channel_id=1, source_target_pairs={{0,32},{32,64},{64,96},{128,160},{160,192},{192,224},{256,288},{28... | collective-permute-start | bytes 208904 | tf_op jit(solution)/shard_map/ppermute | solution.py:39
  16.3 13.0 %collective-permute-start.10 = (f32[136,128]{1,0:T(8,128)S(1)}, f32[136,128]{1,0:T(8,128)S(1)}, u32[]{:S(2)}, u32[]{:S(2)}) collective-permute-start(f32[136,128]{1,0:T(8,128)S(1)} %concatenate.70), channel_id=1, source_target_pairs={{0,64},{32,96},{128,192},{160,224},{256,320},{288,352},{384,448},{... | collective-permute-start | bytes 208904 | tf_op jit(solution)/shard_map/ppermute | solution.py:39
  17.7 14.6 %collective-permute-start.1 = (f32[136,128]{1,0:T(8,128)S(1)}, f32[136,128]{1,0:T(8,128)S(1)}, u32[]{:S(2)}, u32[]{:S(2)}) collective-permute-start(f32[136,128]{1,0:T(8,128)S(1)} %concatenate.62), channel_id=1, source_target_pairs={{0,32},{32,64},{64,96},{128,160},{160,192},{192,224},{256,288},{28... | collective-permute-start | bytes 208904 | tf_op jit(solution)/shard_map/ppermute | solution.py:39
  33.5 2.2 %collective-permute-start.11 = (f32[136,128]{1,0:T(8,128)S(1)}, f32[136,128]{1,0:T(8,128)S(1)}, u32[]{:S(2)}, u32[]{:S(2)}) collective-permute-start(f32[136,128]{1,0:T(8,128)S(1)} %concatenate.71), channel_id=1, source_target_pairs={{96,224},{224,352},{352,480},{480,608},{608,736},{736,864},{864,99... | collective-permute-start | bytes 208904 | tf_op jit(solution)/shard_map/ppermute | solution.py:39
  34.4 7.1 %collective-permute-start.2 = (f32[136,128]{1,0:T(8,128)S(1)}, f32[136,128]{1,0:T(8,128)S(1)}, u32[]{:S(2)}, u32[]{:S(2)}) collective-permute-start(f32[136,128]{1,0:T(8,128)S(1)} %concatenate.63), channel_id=1, source_target_pairs={{0,64},{32,96},{128,192},{160,224},{256,320},{288,352},{384,448},{... | collective-permute-start | bytes 208904 | tf_op jit(solution)/shard_map/ppermute | solution.py:39
  37.0 6.5 %collective-permute-start.12 = (f32[136,128]{1,0:T(8,128)S(1)}, f32[136,128]{1,0:T(8,128)S(1)}, u32[]{:S(2)}, u32[]{:S(2)}) collective-permute-start(f32[136,128]{1,0:T(8,128)S(1)} %concatenate.72), channel_id=1, source_target_pairs={{96,352},{224,480},{352,608},{480,736},{608,864},{736,992},{97,353... | collective-permute-start | bytes 208904 | tf_op jit(solution)/shard_map/ppermute | solution.py:39
  42.8 2.6 %collective-permute-start.3 = (f32[136,128]{1,0:T(8,128)S(1)}, f32[136,128]{1,0:T(8,128)S(1)}, u32[]{:S(2)}, u32[]{:S(2)}) collective-permute-start(f32[136,128]{1,0:T(8,128)S(1)} %concatenate.64), channel_id=1, source_target_pairs={{96,224},{224,352},{352,480},{480,608},{608,736},{736,864},{864,99... | collective-permute-start | bytes 208904 | tf_op jit(solution)/shard_map/ppermute | solution.py:39
  44.7 5.2 %collective-permute-start.13 = (f32[136,128]{1,0:T(8,128)S(1)}, f32[136,128]{1,0:T(8,128)S(1)}, u32[]{:S(2)}, u32[]{:S(2)}) collective-permute-start(f32[136,128]{1,0:T(8,128)S(1)} %concatenate.73), channel_id=1, source_target_pairs={{96,608},{224,736},{352,864},{480,992},{97,609},{225,737},{353,865... | collective-permute-start | bytes 208904 | tf_op jit(solution)/shard_map/ppermute | solution.py:39
  46.6 4.5 %collective-permute-start.4 = (f32[136,128]{1,0:T(8,128)S(1)}, f32[136,128]{1,0:T(8,128)S(1)}, u32[]{:S(2)}, u32[]{:S(2)}) collective-permute-start(f32[136,128]{1,0:T(8,128)S(1)} %concatenate.65), channel_id=1, source_target_pairs={{96,352},{224,480},{352,608},{480,736},{608,864},{736,992},{97,353... | collective-permute-start | bytes 208904 | tf_op jit(solution)/shard_map/ppermute | solution.py:39
  52.4 3.4 %collective-permute-start.5 = (f32[136,128]{1,0:T(8,128)S(1)}, f32[136,128]{1,0:T(8,128)S(1)}, u32[]{:S(2)}, u32[]{:S(2)}) collective-permute-start(f32[136,128]{1,0:T(8,128)S(1)} %concatenate.66), channel_id=1, source_target_pairs={{96,608},{224,736},{352,864},{480,992},{97,609},{225,737},{353,865... | collective-permute-start | bytes 208904 | tf_op jit(solution)/shard_map/ppermute | solution.py:39
  53.1 67.6 %collective-permute-start.16 = (f32[136,128]{1,0:T(8,128)S(1)}, f32[136,128]{1,0:T(8,128)S(1)}, u32[]{:S(2)}, u32[]{:S(2)}) collective-permute-start(f32[136,128]{1,0:T(8,128)S(1)} %concatenate.75), channel_id=1, source_target_pairs={{96,128},{224,256},{352,384},{480,512},{608,640},{736,768},{864,89... | collective-permute-start | bytes 208904 | tf_op jit(solution)/shard_map/ppermute | solution.py:39
  53.8 65.8 %collective-permute-start.15 = (f32[136,128]{1,0:T(8,128)S(1)}, f32[136,128]{1,0:T(8,128)S(1)}, u32[]{:S(2)}, u32[]{:S(2)}) collective-permute-start(f32[136,128]{1,0:T(8,128)S(1)} %concatenate.75), channel_id=1, source_target_pairs={{96,160},{224,288},{352,416},{480,544},{608,672},{736,800},{864,92... | collective-permute-start | bytes 208904 | tf_op jit(solution)/shard_map/ppermute | solution.py:39
  54.5 63.9 %collective-permute-start.14 = (f32[136,128]{1,0:T(8,128)S(1)}, f32[136,128]{1,0:T(8,128)S(1)}, u32[]{:S(2)}, u32[]{:S(2)}) collective-permute-start(f32[136,128]{1,0:T(8,128)S(1)} %concatenate.74), channel_id=1, source_target_pairs={{96,64},{224,192},{352,320},{480,448},{608,576},{736,704},{864,832... | collective-permute-start | bytes 208904 | tf_op jit(solution)/shard_map/ppermute | solution.py:39
  57.1 78.1 %slice-start = ((f32[520,128]{1,0:T(8,128)}), f32[512,128]{1,0:T(8,128)S(1)}, s32[]{:S(2)}) async-start(f32[520,128]{1,0:T(8,128)} %copy-done.1), calls=%async_computation.1 | async-start | bytes 524288 | tf_op jit(solution)/shard_map/slice | solution.py:30
  57.1 73.5 %collective-permute-start.8 = (f32[136,128]{1,0:T(8,128)S(1)}, f32[136,128]{1,0:T(8,128)S(1)}, u32[]{:S(2)}, u32[]{:S(2)}) collective-permute-start(f32[136,128]{1,0:T(8,128)S(1)} %concatenate.68), channel_id=1, source_target_pairs={{96,128},{224,256},{352,384},{480,512},{608,640},{736,768},{864,89... | collective-permute-start | bytes 208904 | tf_op jit(solution)/shard_map/ppermute | solution.py:39
  57.9 71.5 %collective-permute-start.7 = (f32[136,128]{1,0:T(8,128)S(1)}, f32[136,128]{1,0:T(8,128)S(1)}, u32[]{:S(2)}, u32[]{:S(2)}) collective-permute-start(f32[136,128]{1,0:T(8,128)S(1)} %concatenate.68), channel_id=1, source_target_pairs={{96,160},{224,288},{352,416},{480,544},{608,672},{736,800},{864,92... | collective-permute-start | bytes 208904 | tf_op jit(solution)/shard_map/ppermute | solution.py:39
  122.0 6.2 %collective-permute-start.6 = (f32[136,128]{1,0:T(8,128)S(1)}, f32[136,128]{1,0:T(8,128)S(1)}, u32[]{:S(2)}, u32[]{:S(2)}) collective-permute-start(f32[136,128]{1,0:T(8,128)S(1)} %concatenate.67), channel_id=1, source_target_pairs={{96,64},{224,192},{352,320},{480,448},{608,576},{736,704},{864,832... | collective-permute-start | bytes 208904 | tf_op jit(solution)/shard_map/ppermute | solution.py:39
  131.9 3.2 %collective-permute-start.17 = (f32[264,128]{1,0:T(8,128)S(1)}, f32[264,128]{1,0:T(8,128)S(1)}, u32[]{:S(2)}, u32[]{:S(2)}) collective-permute-start(f32[264,128]{1,0:T(8,128)S(1)} %concatenate.77), channel_id=1, source_target_pairs={{0,16},{16,0},{1,17},{17,1},{2,18},{18,2},{3,19},{19,3},{4,20},{20... | collective-permute-start | bytes 405512 | tf_op jit(solution)/shard_map/ppermute | solution.py:35
  136.1 14.6 %all-to-all-start = ((f32[16,1,512]{2,1,0:T(1,128)}), f32[16,1,512]{2,1,0:T(1,128)S(1)}, u32[]{:S(2)}, u32[]{:S(2)}) async-start(f32[16,1,512]{2,1,0:T(1,128)} %broadcast_in_dim.115), calls=%async_computation | async-start | bytes 65536 | tf_op jit(solution)/shard_map/all_to_all | solution.py:110
  (1 other events, 1.4 us)

commit v6 on v3

--- a/solution.py
+++ b/solution.py
@@ -68,19 +68,20 @@
         if 2 * shift < groups:
             upto = combine_states(got, upto)
         shift *= 2
-    through = combine_states(before, incl)
-    carried = before
+    through = pack(combine_states(before, incl))
+    carried = pack(before)
     for place in range(group - 1):
         ahead = place + 1
         behind = group - 1 - place
         if ahead <= behind:
             pairs = [(ends[j], ends[j] + ahead) for j in range(groups - 1)]
-            got = received(through, axis, pairs, which >= 1)
+            got = lax.ppermute(through, axis, pairs)
+            got = jnp.where(which >= 1, got, pack(empty))
         else:
             pairs = [(ends[j], ends[j] - behind) for j in range(groups)]
-            got = received(before, axis, pairs, which >= 0)
-        carried = select(offset == place, got, carried)
-    return combine_states(carried, excl)
+            got = lax.ppermute(carried, axis, pairs)
+        carried = jnp.where(offset == place, got, carried)
+    return combine_states(unpack(carried), excl)
 
 
 def carried_in(own, chip_axis, core_axis):

time: 137 us -> 132 us (0.964)
  the two profiles are of different devices: /device:TPU:96 before, /device:TPU:64 now
where the time goes in v6:
time: 132 us
  waiting for transfers between devices  91.1 us (69%)
  starting transfers between devices  20.8 us (16%)
  local copies, waits for them, and re-layouts  7.5 us (6%)
  between operations  6.14 us (5%)
  matrix products  3.21 us (2%)
  other arithmetic  2.88 us (2%)
    ppermute x1, waiting for transfers between devices, scan_chips(): got = lax.ppermute(carried, axis, pairs)  64.5 us
    ppermute x5, waiting for transfers between devices, received(): state, last = unpack(lax.ppermute(pack(value), axis, pairs))  16.5 us
    all_to_all x1, waiting for transfers between devices, head_sum(): return jnp.sum(lax.all_to_all(spread, axis, 0, 0, tiled=True), axis=0)  7.26 us
    ppermute x5, starting transfers between devices, received(): state, last = unpack(lax.ppermute(pack(value), axis, pairs))  7.26 us
    all_to_all x1, starting transfers between devices, head_sum(): return jnp.sum(lax.all_to_all(spread, axis, 0, 0, tiled=True), axis=0)  7.06 us
    ppermute x2, starting transfers between devices, swap_cores(): return unpack(lax.ppermute(pack(value), core_axis, [(0, 1), (1, 0)]))  3.84 us
    slice x7, local copies, waits for them, and re-layouts, unpack(): return (state, packed[-TAG, 0].astype(jnp.int32))  3.8 us
    ppermute x2, waiting for transfers between devices, swap_cores(): return unpack(lax.ppermute(pack(value), core_axis, [(0, 1), (1, 0)]))  2.76 us
  transfers between devices with their start and end apart: 11, of which 6 were waited for; matrix products, arithmetic and copies ran while one was open for 2% of the time, Pallas kernels for 0%

profile of v6, /device:TPU:64, one launch (start us, length us, event | category | flops | bytes accessed | tf_op | source)
XLA Modules:
  0.0 131.6 jit_solution(16927071987750332644)
XLA Ops:
  0.0 1.3 %slice.55 = s32[1]{0:T(128)} slice(s32[512]{0:T(512)} %param.7), slice={[511:512]} | slice | bytes 8 | tf_op jit(solution)/shard_map/while/body/eval_jaxpr/slice | solution.py:130
  1.3 1.2 broadcast_compare_fusion.1
  3.1 1.3 copy.28
  5.3 1.9 %collective-permute-start = (f32[520,128]{1,0:T(8,128)S(1)}, f32[520,128]{1,0:T(8,128)S(1)}, u32[]{:S(2)}, u32[]{:S(2)}) collective-permute-start(f32[520,128]{1,0:T(8,128)S(1)} %concatenate.33), channel_id=1, source_target_pairs={{0,16},{16,0},{1,17},{17,1},{2,18},{18,2},{3,19},{19,3},{4,20},{20... | collective-permute-start | bytes 798728 | tf_op jit(solution)/shard_map/ppermute | solution.py:35
  7.2 1.5 %collective-permute-done = f32[520,128]{1,0:T(8,128)S(1)} collective-permute-done((f32[520,128]{1,0:T(8,128)S(1)}, f32[520,128]{1,0:T(8,128)S(1)}, u32[]{:S(2)}, u32[]{:S(2)}) %collective-permute-start) | collective-permute-done | bytes 266272 | tf_op jit(solution)/shard_map/ppermute | solution.py:35
  8.7 0.6 slice.73
  10.0 3.8 %collective-permute-start.1 = (f32[264,128]{1,0:T(8,128)S(1)}, f32[264,128]{1,0:T(8,128)S(1)}, u32[]{:S(2)}, u32[]{:S(2)}) collective-permute-start(f32[264,128]{1,0:T(8,128)S(1)} %concatenate.34), channel_id=1, source_target_pairs={{0,32},{32,64},{64,96},{128,160},{160,192},{192,224},{256,288},{28... | collective-permute-start | bytes 405512 | tf_op jit(solution)/shard_map/ppermute | solution.py:39
  13.9 3.7 %collective-permute-done.1 = f32[264,128]{1,0:T(8,128)S(1)} collective-permute-done((f32[264,128]{1,0:T(8,128)S(1)}, f32[264,128]{1,0:T(8,128)S(1)}, u32[]{:S(2)}, u32[]{:S(2)}) %collective-permute-start.1) | collective-permute-done | bytes 135200 | tf_op jit(solution)/shard_map/ppermute | solution.py:39
  18.8 1.3 collective-permute-start.2
  20.1 12.8 %collective-permute-done.2 = f32[264,128]{1,0:T(8,128)S(1)} collective-permute-done((f32[264,128]{1,0:T(8,128)S(1)}, f32[264,128]{1,0:T(8,128)S(1)}, u32[]{:S(2)}, u32[]{:S(2)}) %collective-permute-start.2) | collective-permute-done | bytes 135200 | tf_op jit(solution)/shard_map/ppermute | solution.py:39
  34.2 0.7 collective-permute-start.3
  36.1 0.7 collective-permute-start.4
  38.1 0.8 collective-permute-start.5
  40.3 0.7 collective-permute-start.6
  40.9 0.7 collective-permute-start.7
  41.9 1.3 collective-permute-start.8
  43.2 2.5 %fusion.3 = f32[512,4,128]{0,2,1:T(8,128)S(1)} fusion(bf16[512,4,128]{0,2,1:T(8,128)(2,1)} %bitcast.78, pred[512,512]{1,0:T(8,128)(4,1)S(1)} %fusion.4, bf16[512,512]{1,0:T(8,128)(2,1)} %param.6, bf16[512,512]{1,0:T(8,128)(2,1)S(1)} %copy-done), kind=kOutput, calls=%fused_computation.5 | convolution fusion | flops 538968064 | bytes 2883584 | tf_op jit(solution)/shard_map/while/body/eval_jaxpr/hts,shd->thd/dot_general | solution.py:129
  45.8 64.5 %collective-permute-done.8 = f32[264,128]{1,0:T(8,128)S(1)} collective-permute-done((f32[264,128]{1,0:T(8,128)S(1)}, f32[264,128]{1,0:T(8,128)S(1)}, u32[]{:S(2)}, u32[]{:S(2)}) %collective-permute-start.8) | collective-permute-done | bytes 135200 | tf_op jit(solution)/shard_map/ppermute | solution.py:82
  111.6 1.9 %collective-permute-start.9 = (f32[264,128]{1,0:T(8,128)S(1)}, f32[264,128]{1,0:T(8,128)S(1)}, u32[]{:S(2)}, u32[]{:S(2)}) collective-permute-start(f32[264,128]{1,0:T(8,128)S(1)} %concatenate.41), channel_id=1, source_target_pairs={{0,16},{16,0},{1,17},{17,1},{2,18},{18,2},{3,19},{19,3},{4,20},{20... | collective-permute-start | bytes 405512 | tf_op jit(solution)/shard_map/ppermute | solution.py:35
  113.6 1.3 collective-permute-done.9
  115.3 0.6 broadcast_in_dim.98
  115.9 7.1 %all-to-all-start = ((f32[16,1,512]{2,1,0:T(1,128)}), f32[16,1,512]{2,1,0:T(1,128)S(1)}, u32[]{:S(2)}, u32[]{:S(2)}) async-start(f32[16,1,512]{2,1,0:T(1,128)} %broadcast_in_dim.98), calls=%async_computation | async-start | bytes 65536 | tf_op jit(solution)/shard_map/all_to_all | solution.py:110
  123.3 7.3 %all-to-all-done = f32[16,1,512]{2,1,0:T(1,128)S(1)} async-done(((f32[16,1,512]{2,1,0:T(1,128)}), f32[16,1,512]{2,1,0:T(1,128)S(1)}, u32[]{:S(2)}, u32[]{:S(2)}) %all-to-all-start) | async-done | bytes 32800 | tf_op jit(solution)/shard_map/all_to_all | solution.py:110
  130.6 0.9 multiply_convert_fusion
  (57 shorter events, 5.1 us)
Async XLA Ops:
  0.0 43.2 %copy-start = (bf16[512,512]{1,0:T(8,128)(2,1)S(1)}, bf16[512,512]{1,0:T(8,128)(2,1)}, u32[]{:S(2)}) copy-start(bf16[512,512]{1,0:T(8,128)(2,1)} %param.4) | copy-start | bytes 1572868
  0.0 4.9 %copy-start.5 = (bf16[512,512]{1,0:T(8,128)(2,1)S(1)}, bf16[512,512]{1,0:T(8,128)(2,1)}, u32[]{:S(2)}) copy-start(bf16[512,512]{1,0:T(8,128)(2,1)} %param.6) | copy-start | bytes 1572868
  4.4 0.9 copy-start.2
  5.3 3.4 %collective-permute-start = (f32[520,128]{1,0:T(8,128)S(1)}, f32[520,128]{1,0:T(8,128)S(1)}, u32[]{:S(2)}, u32[]{:S(2)}) collective-permute-start(f32[520,128]{1,0:T(8,128)S(1)} %concatenate.33), channel_id=1, source_target_pairs={{0,16},{16,0},{1,17},{17,1},{2,18},{18,2},{3,19},{19,3},{4,20},{20... | collective-permute-start | bytes 798728 | tf_op jit(solution)/shard_map/ppermute | solution.py:35
  8.7 37.1 %copy-start.1 = (f32[520,128]{1,0:T(8,128)}, f32[520,128]{1,0:T(8,128)S(1)}, u32[]{:S(2)}) copy-start(f32[520,128]{1,0:T(8,128)S(1)} %collective-permute-done) | copy-start | bytes 798724
  10.0 7.5 %collective-permute-start.1 = (f32[264,128]{1,0:T(8,128)S(1)}, f32[264,128]{1,0:T(8,128)S(1)}, u32[]{:S(2)}, u32[]{:S(2)}) collective-permute-start(f32[264,128]{1,0:T(8,128)S(1)} %concatenate.34), channel_id=1, source_target_pairs={{0,32},{32,64},{64,96},{128,160},{160,192},{192,224},{256,288},{28... | collective-permute-start | bytes 405512 | tf_op jit(solution)/shard_map/ppermute | solution.py:39
  18.8 14.1 %collective-permute-start.2 = (f32[264,128]{1,0:T(8,128)S(1)}, f32[264,128]{1,0:T(8,128)S(1)}, u32[]{:S(2)}, u32[]{:S(2)}) collective-permute-start(f32[264,128]{1,0:T(8,128)S(1)} %concatenate.35), channel_id=1, source_target_pairs={{0,64},{32,96},{128,192},{160,224},{256,320},{288,352},{384,448},{... | collective-permute-start | bytes 405512 | tf_op jit(solution)/shard_map/ppermute | solution.py:39
  34.2 0.7 collective-permute-start.3
  36.1 0.7 collective-permute-start.4
  38.0 3.6 %copy-start.4 = (s32[512]{0:T(512)S(1)}, s32[512]{0:T(512)}, u32[]{:S(2)}) copy-start(s32[512]{0:T(512)} %param.7) | copy-start | bytes 6148
  38.1 3.8 %copy-start.3 = (f32[264,128]{1,0:T(8,128)S(1)}, f32[264,128]{1,0:T(8,128)}, u32[]{:S(2)}) copy-start(f32[264,128]{1,0:T(8,128)} %constant.93.clone.1) | copy-start | bytes 405508
  38.1 0.8 collective-permute-start.5
  40.3 1.6 %collective-permute-start.6 = (f32[264,128]{1,0:T(8,128)S(1)}, f32[264,128]{1,0:T(8,128)S(1)}, u32[]{:S(2)}, u32[]{:S(2)}) collective-permute-start(f32[264,128]{1,0:T(8,128)S(1)} %concatenate.39), channel_id=1, source_target_pairs={{96,160},{224,288},{352,416},{480,544},{608,672},{736,800},{864,92... | collective-permute-start | bytes 405512 | tf_op jit(solution)/shard_map/ppermute | solution.py:78
  40.9 0.9 collective-permute-start.7
  41.9 68.4 %collective-permute-start.8 = (f32[264,128]{1,0:T(8,128)S(1)}, f32[264,128]{1,0:T(8,128)S(1)}, u32[]{:S(2)}, u32[]{:S(2)}) collective-permute-start(f32[264,128]{1,0:T(8,128)S(1)} %select_select_fusion), channel_id=1, source_target_pairs={{96,64},{224,192},{352,320},{480,448},{608,576},{736,704},{864,832... | collective-permute-start | bytes 405512 | tf_op jit(solution)/shard_map/ppermute | solution.py:82
  45.8 69.1 %slice-start = ((f32[520,128]{1,0:T(8,128)}), f32[512,128]{1,0:T(8,128)S(1)}, s32[]{:S(2)}) async-start(f32[520,128]{1,0:T(8,128)} %copy-done.1), calls=%async_computation.1 | async-start | bytes 524288 | tf_op jit(solution)/shard_map/slice | solution.py:30
  111.6 3.2 %collective-permute-start.9 = (f32[264,128]{1,0:T(8,128)S(1)}, f32[264,128]{1,0:T(8,128)S(1)}, u32[]{:S(2)}, u32[]{:S(2)}) collective-permute-start(f32[264,128]{1,0:T(8,128)S(1)} %concatenate.41), channel_id=1, source_target_pairs={{0,16},{16,0},{1,17},{17,1},{2,18},{18,2},{3,19},{19,3},{4,20},{20... | collective-permute-start | bytes 405512 | tf_op jit(solution)/shard_map/ppermute | solution.py:35
  115.9 14.7 %all-to-all-start = ((f32[16,1,512]{2,1,0:T(1,128)}), f32[16,1,512]{2,1,0:T(1,128)S(1)}, u32[]{:S(2)}, u32[]{:S(2)}) async-start(f32[16,1,512]{2,1,0:T(1,128)} %broadcast_in_dim.98), calls=%async_computation | async-start | bytes 65536 | tf_op jit(solution)/shard_map/all_to_all | solution.py:110

commit v7 on v6

--- a/solution.py
+++ b/solution.py
@@ -50,14 +50,11 @@
     groups = count // group
     offset, which = (mine % group, mine // group)
     empty = (jnp.zeros_like(own[0]), jnp.full_like(own[1], -1))
-    incl, excl = (own, empty)
-    shift = 1
-    while shift < group:
+    excl = empty
+    for shift in range(group - 1, 0, -1):
         pairs = [(j, j + shift) for j in range(count - shift) if j % group + shift < group]
-        got = received(incl, axis, pairs, offset >= shift)
-        excl = combine_states(got, excl)
-        incl = combine_states(got, incl)
-        shift *= 2
+        excl = combine_states(excl, received(own, axis, pairs, offset >= shift))
+    incl = combine_states(excl, own)
     ends = [group * j + group - 1 for j in range(groups)]
     upto, before = (incl, empty)
     shift = 1

time: 132 us -> 133 us (level)
  waiting for transfers between devices: 91.1 us -> 87 us
  other arithmetic: 2.88 us -> 4.81 us
  starting transfers between devices: 20.8 us -> 22.2 us
    ppermute x5 -> x6, waiting for transfers between devices: 16.5 us -> 13.3 us  [received(): state, last = unpack(lax.ppermute(pack(value), axis, pairs))]
    ppermute x5 -> x6, starting transfers between devices: 7.26 us -> 8.55 us  [received(): state, last = unpack(lax.ppermute(pack(value), axis, pairs))]
    slice x7 -> x8, local copies, waits for them, and re-layouts: 3.8 us -> 4.44 us  [unpack(): return (state, packed[-TAG, 0].astype(jnp.int32))]
  transfers between devices with their start and end apart: 11 -> 12, of which waited for: 6 -> 5; matrix products, arithmetic and copies ran while one was open for 2% -> 3% of each run, Pallas kernels for 0% -> 0%
where the time goes in v7:
time: 133 us; the launch traced here: 132 us
  waiting for transfers between devices  87 us (65%)
  starting transfers between devices  22.2 us (17%)
  local copies, waits for them, and re-layouts  8.18 us (6%)
  between operations  6.94 us (5%)
  other arithmetic  4.81 us (4%)
  matrix products  3.07 us (2%)
    ppermute x1, waiting for transfers between devices, scan_chips(): got = lax.ppermute(carried, axis, pairs)  63.6 us
    ppermute x6, waiting for transfers between devices, received(): state, last = unpack(lax.ppermute(pack(value), axis, pairs))  13.3 us
    ppermute x6, starting transfers between devices, received(): state, last = unpack(lax.ppermute(pack(value), axis, pairs))  8.55 us
    all_to_all x1, waiting for transfers between devices, head_sum(): return jnp.sum(lax.all_to_all(spread, axis, 0, 0, tiled=True), axis=0)  7.26 us
    all_to_all x1, starting transfers between devices, head_sum(): return jnp.sum(lax.all_to_all(spread, axis, 0, 0, tiled=True), axis=0)  7.04 us
    slice x8, local copies, waits for them, and re-layouts, unpack(): return (state, packed[-TAG, 0].astype(jnp.int32))  4.44 us
    ppermute x2, starting transfers between devices, swap_cores(): return unpack(lax.ppermute(pack(value), core_axis, [(0, 1), (1, 0)]))  3.84 us
    ppermute x2, waiting for transfers between devices, swap_cores(): return unpack(lax.ppermute(pack(value), core_axis, [(0, 1), (1, 0)]))  2.77 us
  transfers between devices with their start and end apart: 12, of which 5 were waited for; matrix products, arithmetic and copies ran while one was open for 3% of the time, Pallas kernels for 0%

profile of v7, /device:TPU:64, one launch (start us, length us, event | category | flops | bytes accessed | tf_op | source)
XLA Modules:
  0.0 132.1 jit_solution(5539938795111856481)
XLA Ops:
  0.0 1.4 %slice.61 = s32[1]{0:T(128)} slice(s32[512]{0:T(512)} %param.7), slice={[511:512]} | slice | bytes 8 | tf_op jit(solution)/shard_map/while/body/eval_jaxpr/slice | solution.py:127
  1.4 1.3 broadcast_compare_fusion.1
  3.3 1.3 copy.28
  5.6 1.9 %collective-permute-start = (f32[520,128]{1,0:T(8,128)S(1)}, f32[520,128]{1,0:T(8,128)S(1)}, u32[]{:S(2)}, u32[]{:S(2)}) collective-permute-start(f32[520,128]{1,0:T(8,128)S(1)} %concatenate.32), channel_id=1, source_target_pairs={{0,16},{16,0},{1,17},{17,1},{2,18},{18,2},{3,19},{19,3},{4,20},{20... | collective-permute-start | bytes 798728 | tf_op jit(solution)/shard_map/ppermute | solution.py:35
  7.5 1.5 %collective-permute-done = f32[520,128]{1,0:T(8,128)S(1)} collective-permute-done((f32[520,128]{1,0:T(8,128)S(1)}, f32[520,128]{1,0:T(8,128)S(1)}, u32[]{:S(2)}, u32[]{:S(2)}) %collective-permute-start) | collective-permute-done | bytes 266272 | tf_op jit(solution)/shard_map/ppermute | solution.py:35
  10.2 0.7 collective-permute-start.3
  10.9 1.3 collective-permute-start.2
  12.2 4.4 %collective-permute-start.1 = (f32[264,128]{1,0:T(8,128)S(1)}, f32[264,128]{1,0:T(8,128)S(1)}, u32[]{:S(2)}, u32[]{:S(2)}) collective-permute-start(f32[264,128]{1,0:T(8,128)S(1)} %concatenate.33), channel_id=1, source_target_pairs={{0,32},{32,64},{64,96},{128,160},{160,192},{192,224},{256,288},{28... | collective-permute-start | bytes 405512 | tf_op jit(solution)/shard_map/ppermute | solution.py:39
  17.8 13.3 %collective-permute-done.2 = f32[264,128]{1,0:T(8,128)S(1)} collective-permute-done((f32[264,128]{1,0:T(8,128)S(1)}, f32[264,128]{1,0:T(8,128)S(1)}, u32[]{:S(2)}, u32[]{:S(2)}) %collective-permute-start.2) | collective-permute-done | bytes 135200 | tf_op jit(solution)/shard_map/ppermute | solution.py:39
  33.7 0.7 collective-permute-start.4
  35.7 0.7 collective-permute-start.5
  37.7 0.8 collective-permute-start.6
  40.0 0.8 collective-permute-start.7
  40.8 0.7 collective-permute-start.8
  41.8 1.3 collective-permute-start.9
  43.1 2.4 %fusion.3 = f32[512,4,128]{0,2,1:T(8,128)S(1)} fusion(bf16[512,4,128]{0,2,1:T(8,128)(2,1)S(1)} %bitcast.74, pred[512,512]{1,0:T(8,128)(4,1)S(1)} %fusion.4, bf16[512,512]{1,0:T(8,128)(2,1)} %param.6, bf16[512,512]{1,0:T(8,128)(2,1)S(1)} %copy-done), kind=kOutput, calls=%fused_computation.5 | convolution fusion | flops 538968064 | bytes 2883584 | tf_op jit(solution)/shard_map/while/body/eval_jaxpr/hts,shd->thd/dot_general | solution.py:126
  45.5 63.6 %collective-permute-done.9 = f32[264,128]{1,0:T(8,128)} collective-permute-done((f32[264,128]{1,0:T(8,128)S(1)}, f32[264,128]{1,0:T(8,128)}, u32[]{:S(2)}, u32[]{:S(2)}) %collective-permute-start.9) | collective-permute-done | bytes 135200 | tf_op jit(solution)/shard_map/ppermute | solution.py:79
  109.1 0.9 broadcast_select_fusion.2
  111.2 1.0 add_select_fusion.1
  112.2 1.9 %collective-permute-start.10 = (f32[264,128]{1,0:T(8,128)S(1)}, f32[264,128]{1,0:T(8,128)S(1)}, u32[]{:S(2)}, u32[]{:S(2)}) collective-permute-start(f32[264,128]{1,0:T(8,128)S(1)} %concatenate.39), channel_id=1, source_target_pairs={{0,16},{16,0},{1,17},{17,1},{2,18},{18,2},{3,19},{19,3},{4,20},{20... | collective-permute-start | bytes 405512 | tf_op jit(solution)/shard_map/ppermute | solution.py:35
  114.2 1.3 collective-permute-done.10
  116.5 7.0 %all-to-all-start = ((f32[16,1,512]{2,1,0:T(1,128)}), f32[16,1,512]{2,1,0:T(1,128)S(1)}, u32[]{:S(2)}, u32[]{:S(2)}) async-start(f32[16,1,512]{2,1,0:T(1,128)} %broadcast_in_dim.94), calls=%async_computation | async-start | bytes 65536 | tf_op jit(solution)/shard_map/all_to_all | solution.py:107
  123.9 7.3 %all-to-all-done = f32[16,1,512]{2,1,0:T(1,128)S(1)} async-done(((f32[16,1,512]{2,1,0:T(1,128)}), f32[16,1,512]{2,1,0:T(1,128)S(1)}, u32[]{:S(2)}, u32[]{:S(2)}) %all-to-all-start) | async-done | bytes 32800 | tf_op jit(solution)/shard_map/all_to_all | solution.py:107
  131.2 0.9 multiply_convert_fusion
  (63 shorter events, 6.9 us)
Async XLA Ops:
  0.0 43.1 %copy-start = (bf16[512,512]{1,0:T(8,128)(2,1)S(1)}, bf16[512,512]{1,0:T(8,128)(2,1)}, u32[]{:S(2)}) copy-start(bf16[512,512]{1,0:T(8,128)(2,1)} %param.4) | copy-start | bytes 1572868
  0.0 5.2 %copy-start.7 = (bf16[512,512]{1,0:T(8,128)(2,1)S(1)}, bf16[512,512]{1,0:T(8,128)(2,1)}, u32[]{:S(2)}) copy-start(bf16[512,512]{1,0:T(8,128)(2,1)} %param.6) | copy-start | bytes 1572868
  4.6 1.0 copy-start.2
  5.6 3.4 %collective-permute-start = (f32[520,128]{1,0:T(8,128)S(1)}, f32[520,128]{1,0:T(8,128)S(1)}, u32[]{:S(2)}, u32[]{:S(2)}) collective-permute-start(f32[520,128]{1,0:T(8,128)S(1)} %concatenate.32), channel_id=1, source_target_pairs={{0,16},{16,0},{1,17},{17,1},{2,18},{18,2},{3,19},{19,3},{4,20},{20... | collective-permute-start | bytes 798728 | tf_op jit(solution)/shard_map/ppermute | solution.py:35
  9.0 36.5 %copy-start.1 = (f32[520,128]{1,0:T(8,128)}, f32[520,128]{1,0:T(8,128)S(1)}, u32[]{:S(2)}) copy-start(f32[520,128]{1,0:T(8,128)S(1)} %collective-permute-done) | copy-start | bytes 798724
  10.2 6.5 %collective-permute-start.3 = (f32[264,128]{1,0:T(8,128)S(1)}, f32[264,128]{1,0:T(8,128)S(1)}, u32[]{:S(2)}, u32[]{:S(2)}) collective-permute-start(f32[264,128]{1,0:T(8,128)S(1)} %concatenate.33), channel_id=1, source_target_pairs={{0,96},{128,224},{256,352},{384,480},{512,608},{640,736},{768,864}... | collective-permute-start | bytes 405512 | tf_op jit(solution)/shard_map/ppermute | solution.py:39
  10.9 20.2 %collective-permute-start.2 = (f32[264,128]{1,0:T(8,128)S(1)}, f32[264,128]{1,0:T(8,128)S(1)}, u32[]{:S(2)}, u32[]{:S(2)}) collective-permute-start(f32[264,128]{1,0:T(8,128)S(1)} %concatenate.33), channel_id=1, source_target_pairs={{0,64},{32,96},{128,192},{160,224},{256,320},{288,352},{384,448},{... | collective-permute-start | bytes 405512 | tf_op jit(solution)/shard_map/ppermute | solution.py:39
  12.2 20.0 %collective-permute-start.1 = (f32[264,128]{1,0:T(8,128)S(1)}, f32[264,128]{1,0:T(8,128)S(1)}, u32[]{:S(2)}, u32[]{:S(2)}) collective-permute-start(f32[264,128]{1,0:T(8,128)S(1)} %concatenate.33), channel_id=1, source_target_pairs={{0,32},{32,64},{64,96},{128,160},{160,192},{192,224},{256,288},{28... | collective-permute-start | bytes 405512 | tf_op jit(solution)/shard_map/ppermute | solution.py:39
  32.2 3.4 %copy-start.4 = (f32[264,128]{1,0:T(8,128)}, f32[264,128]{1,0:T(8,128)S(1)}, u32[]{:S(2)}) copy-start(f32[264,128]{1,0:T(8,128)S(1)} %collective-permute-done.1) | copy-start | bytes 405508
  33.7 0.7 collective-permute-start.4
  35.7 0.7 collective-permute-start.5
  37.7 3.8 %copy-start.6 = (s32[512]{0:T(512)S(1)}, s32[512]{0:T(512)}, u32[]{:S(2)}) copy-start(s32[512]{0:T(512)} %param.7) | copy-start | bytes 6148
  37.7 4.0 %copy-start.5 = (f32[264,128]{1,0:T(8,128)S(1)}, f32[264,128]{1,0:T(8,128)}, u32[]{:S(2)}) copy-start(f32[264,128]{1,0:T(8,128)} %constant.94.clone.1) | copy-start | bytes 405508
  37.7 0.8 collective-permute-start.6
  39.9 3.2 %copy-start.3 = (bf16[512,512]{0,1:T(8,128)(2,1)S(1)}, bf16[512,512]{0,1:T(8,128)(2,1)}, u32[]{:S(2)}) copy-start(bf16[512,512]{0,1:T(8,128)(2,1)} %copy-done.2) | copy-start | bytes 1572868
  40.0 1.7 %collective-permute-start.7 = (f32[264,128]{1,0:T(8,128)S(1)}, f32[264,128]{1,0:T(8,128)S(1)}, u32[]{:S(2)}, u32[]{:S(2)}) collective-permute-start(f32[264,128]{1,0:T(8,128)S(1)} %concatenate.37), channel_id=1, source_target_pairs={{96,160},{224,288},{352,416},{480,544},{608,672},{736,800},{864,92... | collective-permute-start | bytes 405512 | tf_op jit(solution)/shard_map/ppermute | solution.py:75
  40.8 0.9 collective-permute-start.8
  41.8 67.3 %collective-permute-start.9 = (f32[264,128]{1,0:T(8,128)S(1)}, f32[264,128]{1,0:T(8,128)}, u32[]{:S(2)}, u32[]{:S(2)}) collective-permute-start(f32[264,128]{1,0:T(8,128)S(1)} %select_select_fusion), channel_id=1, source_target_pairs={{96,64},{224,192},{352,320},{480,448},{608,576},{736,704},{864,832... | collective-permute-start | bytes 405512 | tf_op jit(solution)/shard_map/ppermute | solution.py:79
  45.5 70.0 %slice-start = ((f32[520,128]{1,0:T(8,128)}), f32[512,128]{1,0:T(8,128)S(1)}, s32[]{:S(2)}) async-start(f32[520,128]{1,0:T(8,128)} %copy-done.1), calls=%async_computation.1 | async-start | bytes 524288 | tf_op jit(solution)/shard_map/slice | solution.py:30
  112.2 3.2 %collective-permute-start.10 = (f32[264,128]{1,0:T(8,128)S(1)}, f32[264,128]{1,0:T(8,128)S(1)}, u32[]{:S(2)}, u32[]{:S(2)}) collective-permute-start(f32[264,128]{1,0:T(8,128)S(1)} %concatenate.39), channel_id=1, source_target_pairs={{0,16},{16,0},{1,17},{17,1},{2,18},{18,2},{3,19},{19,3},{4,20},{20... | collective-permute-start | bytes 405512 | tf_op jit(solution)/shard_map/ppermute | solution.py:35
  116.5 14.6 %all-to-all-start = ((f32[16,1,512]{2,1,0:T(1,128)}), f32[16,1,512]{2,1,0:T(1,128)S(1)}, u32[]{:S(2)}, u32[]{:S(2)}) async-start(f32[16,1,512]{2,1,0:T(1,128)} %broadcast_in_dim.94), calls=%async_computation | async-start | bytes 65536 | tf_op jit(solution)/shard_map/all_to_all | solution.py:107

commit v8 on v7

--- a/solution.py
+++ b/solution.py
@@ -42,6 +42,36 @@
 
 def select(cond, a, b):
     return jax.tree.map(lambda x, y: jnp.where(cond, x, y), a, b)
+
+
+def group_prefix(total, axis, ends, which, empty):
+    count, groups = (lax.axis_size(axis), len(ends))
+    half = groups // 2
+    upto, before, back = (total, empty, total)
+    shift = 1
+    while shift < half:
+        pairs = [(ends[j - shift], ends[j]) for j in range(groups) if j % half >= shift]
+        got = received(upto, axis, pairs, which % half >= shift)
+        before = combine_states(got, before)
+        upto = combine_states(got, upto)
+        pairs = [(ends[j + shift], ends[j]) for j in range(half - shift)]
+        back = combine_states(back, received(back, axis, pairs, which + shift < half))
+        shift *= 2
+    source = pack(select(which == 0, back, upto))
+    ahead = [g for g in range(half, groups) if ends[g] - ends[half - 1] <= count - ends[g] + ends[0]]
+    behind = [g for g in range(half, groups) if g not in ahead]
+    lower = pack(empty)
+    for k in range(max(len(ahead), len(behind))):
+        pairs, hit = ([], jnp.zeros((), jnp.bool_))
+        if k < len(ahead):
+            pairs.append((ends[half - 1], ends[ahead[k]]))
+            hit = hit | (which == ahead[k])
+        if k < len(behind):
+            pairs.append((ends[0], ends[behind[k]]))
+            hit = hit | (which == behind[k])
+        lower = jnp.where(hit, lax.ppermute(source, axis, pairs), lower)
+    lower = unpack(lower)
+    return (combine_states(lower, before), combine_states(lower, upto))
 
 
 def scan_chips(own, axis):
@@ -56,16 +86,20 @@
         excl = combine_states(excl, received(own, axis, pairs, offset >= shift))
     incl = combine_states(excl, own)
     ends = [group * j + group - 1 for j in range(groups)]
-    upto, before = (incl, empty)
-    shift = 1
-    while shift < groups:
-        pairs = [(ends[j], ends[j + shift]) for j in range(groups - shift)]
-        got = received(upto, axis, pairs, which >= shift)
-        before = combine_states(got, before)
-        if 2 * shift < groups:
-            upto = combine_states(got, upto)
-        shift *= 2
-    through = pack(combine_states(before, incl))
+    if groups >= 4 and groups % 2 == 0:
+        before, through = group_prefix(incl, axis, ends, which, empty)
+    else:
+        upto, before = (incl, empty)
+        shift = 1
+        while shift < groups:
+            pairs = [(ends[j], ends[j + shift]) for j in range(groups - shift)]
+            got = received(upto, axis, pairs, which >= shift)
+            before = combine_states(got, before)
+            if 2 * shift < groups:
+                upto = combine_states(got, upto)
+            shift *= 2
+        through = combine_states(before, incl)
+    through = pack(through)
     carried = pack(before)
     for place in range(group - 1):
         ahead = place + 1

time: 133 us -> 117 us (0.88)
  waiting for transfers between devices: 87 us -> 68 us
  starting transfers between devices: 22.2 us -> 24.1 us
  between operations: 6.94 us -> 8.55 us
    ppermute x1, waiting for transfers between devices: 63.6 us -> 44.7 us  [scan_chips(): got = lax.ppermute(carried, axis, pairs)]
    ppermute x0 -> x2, starting transfers between devices: none -> 1.34 us  [group_prefix(): lower = jnp.where(hit, lax.ppermute(source, axis, pairs), lower)]
    slice x8 -> x10, local copies, waits for them, and re-layouts: 4.44 us -> 5.4 us  [unpack(): return (state, packed[-TAG, 0].astype(jnp.int32))]
    ppermute x6 -> x7, starting transfers between devices: 8.55 us -> 9.22 us  [received(): state, last = unpack(lax.ppermute(pack(value), axis, pairs))]
    ppermute x6 -> x7, waiting for transfers between devices: 13.3 us -> 13.2 us  [received(): state, last = unpack(lax.ppermute(pack(value), axis, pairs))]
  transfers between devices with their start and end apart: 12 -> 15, of which waited for: 5 -> 5; matrix products, arithmetic and copies ran while one was open for 3% -> 5% of each run, Pallas kernels for 0% -> 0%
where the time goes in v8:
time: 117 us
  waiting for transfers between devices  68 us (58%)
  starting transfers between devices  24.1 us (21%)
  local copies, waits for them, and re-layouts  9.15 us (8%)
  between operations  8.55 us (7%)
  other arithmetic  3.78 us (3%)
  matrix products  3.31 us (3%)
    ppermute x1, waiting for transfers between devices, scan_chips(): got = lax.ppermute(carried, axis, pairs)  44.7 us
    ppermute x7, waiting for transfers between devices, received(): state, last = unpack(lax.ppermute(pack(value), axis, pairs))  13.2 us
    ppermute x7, starting transfers between devices, received(): state, last = unpack(lax.ppermute(pack(value), axis, pairs))  9.22 us
    all_to_all x1, waiting for transfers between devices, head_sum(): return jnp.sum(lax.all_to_all(spread, axis, 0, 0, tiled=True), axis=0)  7.26 us
    all_to_all x1, starting transfers between devices, head_sum(): return jnp.sum(lax.all_to_all(spread, axis, 0, 0, tiled=True), axis=0)  7.03 us
    slice x10, local copies, waits for them, and re-layouts, unpack(): return (state, packed[-TAG, 0].astype(jnp.int32))  5.4 us
    ppermute x2, starting transfers between devices, swap_cores(): return unpack(lax.ppermute(pack(value), core_axis, [(0, 1), (1, 0)]))  3.84 us
    ppermute x2, waiting for transfers between devices, swap_cores(): return unpack(lax.ppermute(pack(value), core_axis, [(0, 1), (1, 0)]))  2.76 us
  transfers between devices with their start and end apart: 15, of which 5 were waited for; matrix products, arithmetic and copies ran while one was open for 5% of the time, Pallas kernels for 0%

profile of v8, /device:TPU:64, one launch (start us, length us, event | category | flops | bytes accessed | tf_op | source)
XLA Modules:
  0.0 116.8 jit_solution(15979675650225370272)
XLA Ops:
  0.0 1.4 %slice.73 = s32[1]{0:T(128)} slice(s32[512]{0:T(512)} %param.7), slice={[511:512]} | slice | bytes 8 | tf_op jit(solution)/shard_map/while/body/eval_jaxpr/slice | solution.py:161
  1.4 1.3 %broadcast_compare_fusion.1 = pred[512]{0:T(512)(128)(4,1)S(1)} fusion(s32[512]{0:T(512)} %param.7, s32[]{:T(128)} %bitcast.1), kind=kLoop, calls=%fused_computation.54 | loop fusion | flops 512 | bytes 2564 | tf_op jit(solution)/shard_map/while/body/eval_jaxpr/eq | solution.py:162
  3.3 1.3 %copy.28 = bf16[512,512]{0,1:T(8,128)(2,1)S(1)} copy(bf16[512,512]{1,0:T(8,128)(2,1)} %param.5) | data formatting | bytes 1048576 | tf_op jit(solution)/shard_map/while/body/jit(dynamic_index_in_dim)/squeeze | solution.py:171
  5.6 1.9 %collective-permute-start = (f32[520,128]{1,0:T(8,128)S(1)}, f32[520,128]{1,0:T(8,128)S(1)}, u32[]{:S(2)}, u32[]{:S(2)}) collective-permute-start(f32[520,128]{1,0:T(8,128)S(1)} %concatenate.36), channel_id=1, source_target_pairs={{0,16},{16,0},{1,17},{17,1},{2,18},{18,2},{3,19},{19,3},{4,20},{20... | collective-permute-start | bytes 798728 | tf_op jit(solution)/shard_map/ppermute | solution.py:35
  7.5 1.5 %collective-permute-done = f32[520,128]{1,0:T(8,128)S(1)} collective-permute-done((f32[520,128]{1,0:T(8,128)S(1)}, f32[520,128]{1,0:T(8,128)S(1)}, u32[]{:S(2)}, u32[]{:S(2)}) %collective-permute-start) | collective-permute-done | bytes 266272 | tf_op jit(solution)/shard_map/ppermute | solution.py:35
  10.3 0.7 collective-permute-start.3
  11.0 1.3 %collective-permute-start.2 = (f32[264,128]{1,0:T(8,128)S(1)}, f32[264,128]{1,0:T(8,128)S(1)}, u32[]{:S(2)}, u32[]{:S(2)}) collective-permute-start(f32[264,128]{1,0:T(8,128)S(1)} %concatenate.37), channel_id=1, source_target_pairs={{0,64},{32,96},{128,192},{160,224},{256,320},{288,352},{384,448},{... | collective-permute-start | bytes 405512 | tf_op jit(solution)/shard_map/ppermute | solution.py:39
  12.3 4.5 %collective-permute-start.1 = (f32[264,128]{1,0:T(8,128)S(1)}, f32[264,128]{1,0:T(8,128)S(1)}, u32[]{:S(2)}, u32[]{:S(2)}) collective-permute-start(f32[264,128]{1,0:T(8,128)S(1)} %concatenate.37), channel_id=1, source_target_pairs={{0,32},{32,64},{64,96},{128,160},{160,192},{192,224},{256,288},{28... | collective-permute-start | bytes 405512 | tf_op jit(solution)/shard_map/ppermute | solution.py:39
  18.0 13.2 %collective-permute-done.2 = f32[264,128]{1,0:T(8,128)S(1)} collective-permute-done((f32[264,128]{1,0:T(8,128)S(1)}, f32[264,128]{1,0:T(8,128)S(1)}, u32[]{:S(2)}, u32[]{:S(2)}) %collective-permute-start.2) | collective-permute-done | bytes 135200 | tf_op jit(solution)/shard_map/ppermute | solution.py:39
  33.8 0.7 collective-permute-start.6
  37.7 0.8 collective-permute-start.7
  38.5 0.7 collective-permute-start.5
  41.8 0.7 collective-permute-start.8
  44.6 0.7 collective-permute-start.10
  45.2 0.7 collective-permute-start.11
  45.9 0.9 fusion.4
  46.9 1.3 %collective-permute-start.12 = (f32[264,128]{1,0:T(8,128)S(1)}, f32[264,128]{1,0:T(8,128)S(1)}, u32[]{:S(2)}, u32[]{:S(2)}) collective-permute-start(f32[264,128]{1,0:T(8,128)S(1)} %select_select_fusion), channel_id=1, source_target_pairs={{96,64},{224,192},{352,320},{480,448},{608,576},{736,704},{864,832... | collective-permute-start | bytes 405512 | tf_op jit(solution)/shard_map/ppermute | solution.py:113
  48.2 2.6 %fusion.3 = f32[512,4,128]{0,2,1:T(8,128)S(1)} fusion(bf16[512,4,128]{0,2,1:T(8,128)(2,1)} %bitcast.78, pred[512,512]{1,0:T(8,128)(4,1)} %fusion.4, bf16[512,512]{1,0:T(8,128)(2,1)} %param.6, bf16[512,512]{1,0:T(8,128)(2,1)S(1)} %copy-done), kind=kOutput, calls=%fused_computation.5 | convolution fusion | flops 538968064 | bytes 2883584 | tf_op jit(solution)/shard_map/while/body/eval_jaxpr/hts,shd->thd/dot_general | solution.py:160
  50.9 44.7 %collective-permute-done.12 = f32[264,128]{1,0:T(8,128)S(1)} collective-permute-done((f32[264,128]{1,0:T(8,128)S(1)}, f32[264,128]{1,0:T(8,128)S(1)}, u32[]{:S(2)}, u32[]{:S(2)}) %collective-permute-start.12) | collective-permute-done | bytes 135200 | tf_op jit(solution)/shard_map/ppermute | solution.py:113
  96.9 1.9 %collective-permute-start.13 = (f32[264,128]{1,0:T(8,128)S(1)}, f32[264,128]{1,0:T(8,128)S(1)}, u32[]{:S(2)}, u32[]{:S(2)}) collective-permute-start(f32[264,128]{1,0:T(8,128)S(1)} %concatenate.44), channel_id=1, source_target_pairs={{0,16},{16,0},{1,17},{17,1},{2,18},{18,2},{3,19},{19,3},{4,20},{20... | collective-permute-start | bytes 405512 | tf_op jit(solution)/shard_map/ppermute | solution.py:35
  98.9 1.3 %collective-permute-done.13 = f32[264,128]{1,0:T(8,128)S(1)} collective-permute-done((f32[264,128]{1,0:T(8,128)S(1)}, f32[264,128]{1,0:T(8,128)S(1)}, u32[]{:S(2)}, u32[]{:S(2)}) %collective-permute-start.13) | collective-permute-done | bytes 135200 | tf_op jit(solution)/shard_map/ppermute | solution.py:35
  101.2 7.0 %all-to-all-start = ((f32[16,1,512]{2,1,0:T(1,128)}), f32[16,1,512]{2,1,0:T(1,128)S(1)}, u32[]{:S(2)}, u32[]{:S(2)}) async-start(f32[16,1,512]{2,1,0:T(1,128)} %broadcast_in_dim.97), calls=%async_computation | async-start | bytes 65536 | tf_op jit(solution)/shard_map/all_to_all | solution.py:141
  108.6 7.3 %all-to-all-done = f32[16,1,512]{2,1,0:T(1,128)S(1)} async-done(((f32[16,1,512]{2,1,0:T(1,128)}), f32[16,1,512]{2,1,0:T(1,128)S(1)}, u32[]{:S(2)}, u32[]{:S(2)}) %all-to-all-start) | async-done | bytes 32800 | tf_op jit(solution)/shard_map/all_to_all | solution.py:141
  115.9 0.9 multiply_convert_fusion
  (73 shorter events, 9.2 us)
Async XLA Ops:
  0.0 48.2 %copy-start = (bf16[512,512]{1,0:T(8,128)(2,1)S(1)}, bf16[512,512]{1,0:T(8,128)(2,1)}, u32[]{:S(2)}) copy-start(bf16[512,512]{1,0:T(8,128)(2,1)} %param.4) | copy-start | bytes 1572868
  0.0 5.2 %copy-start.6 = (bf16[512,512]{1,0:T(8,128)(2,1)S(1)}, bf16[512,512]{1,0:T(8,128)(2,1)}, u32[]{:S(2)}) copy-start(bf16[512,512]{1,0:T(8,128)(2,1)} %param.6) | copy-start | bytes 1572868
  4.6 1.0 copy-start.3
  5.6 3.4 %collective-permute-start = (f32[520,128]{1,0:T(8,128)S(1)}, f32[520,128]{1,0:T(8,128)S(1)}, u32[]{:S(2)}, u32[]{:S(2)}) collective-permute-start(f32[520,128]{1,0:T(8,128)S(1)} %concatenate.36), channel_id=1, source_target_pairs={{0,16},{16,0},{1,17},{17,1},{2,18},{18,2},{3,19},{19,3},{4,20},{20... | collective-permute-start | bytes 798728 | tf_op jit(solution)/shard_map/ppermute | solution.py:35
  9.0 41.8 %copy-start.1 = (f32[520,128]{1,0:T(8,128)}, f32[520,128]{1,0:T(8,128)S(1)}, u32[]{:S(2)}) copy-start(f32[520,128]{1,0:T(8,128)S(1)} %collective-permute-done) | copy-start | bytes 798724
  10.3 6.5 %collective-permute-start.3 = (f32[264,128]{1,0:T(8,128)S(1)}, f32[264,128]{1,0:T(8,128)S(1)}, u32[]{:S(2)}, u32[]{:S(2)}) collective-permute-start(f32[264,128]{1,0:T(8,128)S(1)} %concatenate.37), channel_id=1, source_target_pairs={{0,96},{128,224},{256,352},{384,480},{512,608},{640,736},{768,864}... | collective-permute-start | bytes 405512 | tf_op jit(solution)/shard_map/ppermute | solution.py:39
  11.0 20.2 %collective-permute-start.2 = (f32[264,128]{1,0:T(8,128)S(1)}, f32[264,128]{1,0:T(8,128)S(1)}, u32[]{:S(2)}, u32[]{:S(2)}) collective-permute-start(f32[264,128]{1,0:T(8,128)S(1)} %concatenate.37), channel_id=1, source_target_pairs={{0,64},{32,96},{128,192},{160,224},{256,320},{288,352},{384,448},{... | collective-permute-start | bytes 405512 | tf_op jit(solution)/shard_map/ppermute | solution.py:39
  12.3 20.1 %collective-permute-start.1 = (f32[264,128]{1,0:T(8,128)S(1)}, f32[264,128]{1,0:T(8,128)S(1)}, u32[]{:S(2)}, u32[]{:S(2)}) collective-permute-start(f32[264,128]{1,0:T(8,128)S(1)} %concatenate.37), channel_id=1, source_target_pairs={{0,32},{32,64},{64,96},{128,160},{160,192},{192,224},{256,288},{28... | collective-permute-start | bytes 405512 | tf_op jit(solution)/shard_map/ppermute | solution.py:39
  33.8 1.4 %collective-permute-start.6 = (f32[264,128]{1,0:T(8,128)S(1)}, f32[264,128]{1,0:T(8,128)S(1)}, u32[]{:S(2)}, u32[]{:S(2)}) collective-permute-start(f32[264,128]{1,0:T(8,128)S(1)} %concatenate.38), channel_id=1, source_target_pairs={{224,96},{352,224},{480,352},{225,97},{353,225},{481,353},{226,98}... | collective-permute-start | bytes 405512 | tf_op jit(solution)/shard_map/ppermute | solution.py:39
  34.5 1.9 %collective-permute-start.4 = (f32[264,128]{1,0:T(8,128)S(1)}, f32[264,128]{1,0:T(8,128)S(1)}, u32[]{:S(2)}, u32[]{:S(2)}) collective-permute-start(f32[264,128]{1,0:T(8,128)S(1)} %concatenate.38), channel_id=1, source_target_pairs={{96,224},{224,352},{352,480},{608,736},{736,864},{864,992},{97,225... | collective-permute-start | bytes 405512 | tf_op jit(solution)/shard_map/ppermute | solution.py:39
  37.7 5.5 %copy-start.2 = (f32[264,128]{1,0:T(8,128)S(1)}, f32[264,128]{1,0:T(8,128)}, u32[]{:S(2)}) copy-start(f32[264,128]{1,0:T(8,128)} %constant.106.clone.1) | copy-start | bytes 405508
  37.7 1.5 %collective-permute-start.7 = (f32[264,128]{1,0:T(8,128)S(1)}, f32[264,128]{1,0:T(8,128)S(1)}, u32[]{:S(2)}, u32[]{:S(2)}) collective-permute-start(f32[264,128]{1,0:T(8,128)S(1)} %concatenate.40), channel_id=1, source_target_pairs={{352,96},{480,224},{353,97},{481,225},{354,98},{482,226},{355,99},... | collective-permute-start | bytes 405512 | tf_op jit(solution)/shard_map/ppermute | solution.py:39
  38.5 1.9 %collective-permute-start.5 = (f32[264,128]{1,0:T(8,128)S(1)}, f32[264,128]{1,0:T(8,128)S(1)}, u32[]{:S(2)}, u32[]{:S(2)}) collective-permute-start(f32[264,128]{1,0:T(8,128)S(1)} %concatenate.39), channel_id=1, source_target_pairs={{96,352},{224,480},{608,864},{736,992},{97,353},{225,481},{609,865... | collective-permute-start | bytes 405512 | tf_op jit(solution)/shard_map/ppermute | solution.py:39
  41.8 4.1 %copy-start.4 = (s32[512]{0:T(512)S(1)}, s32[512]{0:T(512)}, u32[]{:S(2)}) copy-start(s32[512]{0:T(512)} %param.7) | copy-start | bytes 6148
  41.8 1.4 %collective-permute-start.8 = (f32[264,128]{1,0:T(8,128)S(1)}, f32[264,128]{1,0:T(8,128)S(1)}, u32[]{:S(2)}, u32[]{:S(2)}) collective-permute-start(f32[264,128]{1,0:T(8,128)S(1)} %concatenate.41), channel_id=1, source_target_pairs={{480,736},{96,992},{481,737},{97,993},{482,738},{98,994},{483,739}... | collective-permute-start | bytes 405512 | tf_op jit(solution)/shard_map/ppermute | solution.py:72
  42.5 0.7 collective-permute-start.9
  44.6 2.3 %collective-permute-start.10 = (f32[264,128]{1,0:T(8,128)S(1)}, f32[264,128]{1,0:T(8,128)S(1)}, u32[]{:S(2)}, u32[]{:S(2)}) collective-permute-start(f32[264,128]{1,0:T(8,128)S(1)} %concatenate.42), channel_id=1, source_target_pairs={{96,160},{224,288},{352,416},{480,544},{608,672},{736,800},{864,92... | collective-permute-start | bytes 405512 | tf_op jit(solution)/shard_map/ppermute | solution.py:109
  45.2 1.6 %collective-permute-start.11 = (f32[264,128]{1,0:T(8,128)S(1)}, f32[264,128]{1,0:T(8,128)S(1)}, u32[]{:S(2)}, u32[]{:S(2)}) collective-permute-start(f32[264,128]{1,0:T(8,128)S(1)} %concatenate.42), channel_id=1, source_target_pairs={{96,128},{224,256},{352,384},{480,512},{608,640},{736,768},{864,89... | collective-permute-start | bytes 405512 | tf_op jit(solution)/shard_map/ppermute | solution.py:109
  46.9 48.7 %collective-permute-start.12 = (f32[264,128]{1,0:T(8,128)S(1)}, f32[264,128]{1,0:T(8,128)S(1)}, u32[]{:S(2)}, u32[]{:S(2)}) collective-permute-start(f32[264,128]{1,0:T(8,128)S(1)} %select_select_fusion), channel_id=1, source_target_pairs={{96,64},{224,192},{352,320},{480,448},{608,576},{736,704},{864,832... | collective-permute-start | bytes 405512 | tf_op jit(solution)/shard_map/ppermute | solution.py:113
  50.8 48.0 %copy-start.5 = (s32[512]{0:T(512)S(1)}, s32[512]{0:T(512)}, u32[]{:S(2)}) copy-start(s32[512]{0:T(512)} %param.7) | copy-start | bytes 6148
  50.9 49.3 %slice-start = ((f32[520,128]{1,0:T(8,128)}), f32[512,128]{1,0:T(8,128)S(1)}, s32[]{:S(2)}) async-start(f32[520,128]{1,0:T(8,128)} %copy-done.1), calls=%async_computation.1 | async-start | bytes 524288 | tf_op jit(solution)/shard_map/slice | solution.py:30
  96.9 3.2 %collective-permute-start.13 = (f32[264,128]{1,0:T(8,128)S(1)}, f32[264,128]{1,0:T(8,128)S(1)}, u32[]{:S(2)}, u32[]{:S(2)}) collective-permute-start(f32[264,128]{1,0:T(8,128)S(1)} %concatenate.44), channel_id=1, source_target_pairs={{0,16},{16,0},{1,17},{17,1},{2,18},{18,2},{3,19},{19,3},{4,20},{20... | collective-permute-start | bytes 405512 | tf_op jit(solution)/shard_map/ppermute | solution.py:35
  101.2 14.6 %all-to-all-start = ((f32[16,1,512]{2,1,0:T(1,128)}), f32[16,1,512]{2,1,0:T(1,128)S(1)}, u32[]{:S(2)}, u32[]{:S(2)}) async-start(f32[16,1,512]{2,1,0:T(1,128)} %broadcast_in_dim.97), calls=%async_computation | async-start | bytes 65536 | tf_op jit(solution)/shard_map/all_to_all | solution.py:141

commit v9 on v8

--- a/solution.py
+++ b/solution.py
@@ -74,7 +74,7 @@
     return (combine_states(lower, before), combine_states(lower, upto))
 
 
-def scan_chips(own, axis):
+def scan_chips(own, axis, core_axis):
     count, mine = (lax.axis_size(axis), lax.axis_index(axis))
     group = GROUP if count % GROUP == 0 else 1
     groups = count // group
@@ -100,19 +100,34 @@
             shift *= 2
         through = combine_states(before, incl)
     through = pack(through)
-    carried = pack(before)
+    both = (axis, core_axis)
+    core = lax.axis_index(core_axis)
+    excl_other = swap_cores(excl, core_axis)
+    mine_p = pack(before)
+    carried, carried_other = (mine_p, lax.ppermute(mine_p, core_axis, [(0, 1), (1, 0)]))
     for place in range(group - 1):
         ahead = place + 1
         behind = group - 1 - place
         if ahead <= behind:
             pairs = [(ends[j], ends[j] + ahead) for j in range(groups - 1)]
-            got = lax.ppermute(through, axis, pairs)
-            got = jnp.where(which >= 1, got, pack(empty))
+            sent, valid = (through, which >= 1)
         else:
             pairs = [(ends[j], ends[j] - behind) for j in range(groups)]
-            got = lax.ppermute(carried, axis, pairs)
+            sent, valid = (mine_p, which >= 0)
+        straight = [(2 * s + c, 2 * t + c) for s, t in pairs for c in range(2)]
+        crossed = [(2 * s + c, 2 * t + 1 - c) for s, t in pairs for c in range(2)]
+        got = jnp.where(valid, lax.ppermute(sent, both, straight), pack(empty))
+        got_other = jnp.where(valid, lax.ppermute(sent, both, crossed), pack(empty))
         carried = jnp.where(offset == place, got, carried)
-    return combine_states(unpack(carried), excl)
+        carried_other = jnp.where(offset == place, got_other, carried_other)
+    done = combine_states(unpack(carried), excl)
+    done_other = combine_states(unpack(carried_other), excl_other)
+    whole = jnp.where(
+        core == 0,
+        jnp.concatenate([done[0], done_other[0]], axis=0),
+        jnp.concatenate([done_other[0], done[0]], axis=0),
+    )
+    return (whole, done[1])
 
 
 def carried_in(own, chip_axis, core_axis):
@@ -125,14 +140,7 @@
     in_chip = jax.tree.map(lambda a, b: jnp.where(core == 0, a, b), empty, first)
     half = chip[0].shape[0] // 2
     mine = jnp.where(core == 0, chip[0][:half], chip[0][half:])
-    before = scan_chips((mine, chip[1]), chip_axis)
-    theirs = swap_cores(before, core_axis)
-    whole = jnp.where(
-        core == 0,
-        jnp.concatenate([before[0], theirs[0]], axis=0),
-        jnp.concatenate([theirs[0], before[0]], axis=0),
-    )
-    return combine_states((whole, before[1]), in_chip)
+    return combine_states(scan_chips((mine, chip[1]), chip_axis, core_axis), in_chip)
 
 
 def head_sum(x, axis):

time: 117 us -> 122 us (1.043)
  the two profiles are of different devices: /device:TPU:64 before, /device:TPU:96 now
where the time goes in v9:
time: 122 us
  starting transfers between devices  67.8 us (56%)
  waiting for transfers between devices  25.8 us (21%)
  local copies, waits for them, and re-layouts  11.2 us (9%)
  between operations  9.25 us (8%)
  other arithmetic  4.25 us (3%)
  matrix products  3.23 us (3%)
    ppermute x7, starting transfers between devices, received(): state, last = unpack(lax.ppermute(pack(value), axis, pairs))  28.4 us
    ppermute x7, waiting for transfers between devices, received(): state, last = unpack(lax.ppermute(pack(value), axis, pairs))  16.5 us
    ppermute x2, starting transfers between devices, group_prefix(): lower = jnp.where(hit, lax.ppermute(source, axis, pairs), lower)  16.3 us
    all_to_all x1, waiting for transfers between devices, head_sum(): return jnp.sum(lax.all_to_all(spread, axis, 0, 0, tiled=True), axis=0)  7.26 us
    all_to_all x1, starting transfers between devices, head_sum(): return jnp.sum(lax.all_to_all(spread, axis, 0, 0, tiled=True), axis=0)  7.03 us
    slice x12, local copies, waits for them, and re-layouts, unpack(): return (state, packed[-TAG, 0].astype(jnp.int32))  6.03 us
    ppermute x3, starting transfers between devices, scan_chips(): got_other = jnp.where(valid, lax.ppermute(sent, both, crossed), pack(empty))  5.81 us
    ppermute x3, starting transfers between devices, scan_chips(): got = jnp.where(valid, lax.ppermute(sent, both, straight), pack(empty))  4.53 us
  transfers between devices with their start and end apart: 19, of which 8 were waited for; matrix products, arithmetic and copies ran while one was open for 6% of the time, Pallas kernels for 0%

profile of v9, /device:TPU:96, one launch (start us, length us, event | category | flops | bytes accessed | tf_op | source)
XLA Modules:
  0.0 121.5 jit_solution(12701738822316165756)
XLA Ops:
  0.0 1.4 %slice.82 = s32[1]{0:T(128)} slice(s32[512]{0:T(512)} %param.7), slice={[511:512]} | slice | bytes 8 | tf_op jit(solution)/shard_map/while/body/eval_jaxpr/slice | solution.py:169
  1.4 1.4 %broadcast_compare_fusion.1 = pred[512]{0:T(512)(128)(4,1)S(1)} fusion(s32[512]{0:T(512)} %param.7, s32[]{:T(128)} %bitcast.1), kind=kLoop, calls=%fused_computation.55 | loop fusion | flops 512 | bytes 2564 | tf_op jit(solution)/shard_map/while/body/eval_jaxpr/eq | solution.py:170
  5.8 1.9 %collective-permute-start = (f32[520,128]{1,0:T(8,128)S(1)}, f32[520,128]{1,0:T(8,128)S(1)}, u32[]{:S(2)}, u32[]{:S(2)}) collective-permute-start(f32[520,128]{1,0:T(8,128)S(1)} %concatenate.36), channel_id=1, source_target_pairs={{0,16},{16,0},{1,17},{17,1},{2,18},{18,2},{3,19},{19,3},{4,20},{20... | collective-permute-start | bytes 798728 | tf_op jit(solution)/shard_map/ppermute | solution.py:35
  7.8 1.5 %collective-permute-done = f32[520,128]{1,0:T(8,128)S(1)} collective-permute-done((f32[520,128]{1,0:T(8,128)S(1)}, f32[520,128]{1,0:T(8,128)S(1)}, u32[]{:S(2)}, u32[]{:S(2)}) %collective-permute-start) | collective-permute-done | bytes 266272 | tf_op jit(solution)/shard_map/ppermute | solution.py:35
  10.4 1.3 %collective-permute-start.3 = (f32[264,128]{1,0:T(8,128)S(1)}, f32[264,128]{1,0:T(8,128)S(1)}, u32[]{:S(2)}, u32[]{:S(2)}) collective-permute-start(f32[264,128]{1,0:T(8,128)S(1)} %concatenate.37), channel_id=1, source_target_pairs={{0,96},{128,224},{256,352},{384,480},{512,608},{640,736},{768,864}... | collective-permute-start | bytes 405512 | tf_op jit(solution)/shard_map/ppermute | solution.py:39
  11.7 1.3 %collective-permute-start.2 = (f32[264,128]{1,0:T(8,128)S(1)}, f32[264,128]{1,0:T(8,128)S(1)}, u32[]{:S(2)}, u32[]{:S(2)}) collective-permute-start(f32[264,128]{1,0:T(8,128)S(1)} %concatenate.37), channel_id=1, source_target_pairs={{0,64},{32,96},{128,192},{160,224},{256,320},{288,352},{384,448},{... | collective-permute-start | bytes 405512 | tf_op jit(solution)/shard_map/ppermute | solution.py:39
  13.0 1.3 %collective-permute-start.1 = (f32[264,128]{1,0:T(8,128)S(1)}, f32[264,128]{1,0:T(8,128)S(1)}, u32[]{:S(2)}, u32[]{:S(2)}) collective-permute-start(f32[264,128]{1,0:T(8,128)S(1)} %concatenate.37), channel_id=1, source_target_pairs={{0,32},{32,64},{64,96},{128,160},{160,192},{192,224},{256,288},{28... | collective-permute-start | bytes 405512 | tf_op jit(solution)/shard_map/ppermute | solution.py:39
  14.4 13.6 %collective-permute-done.3 = f32[264,128]{1,0:T(8,128)S(1)} collective-permute-done((f32[264,128]{1,0:T(8,128)S(1)}, f32[264,128]{1,0:T(8,128)S(1)}, u32[]{:S(2)}, u32[]{:S(2)}) %collective-permute-start.3) | collective-permute-done | bytes 135200 | tf_op jit(solution)/shard_map/ppermute | solution.py:39
  31.3 1.3 %collective-permute-start.6 = (f32[264,128]{1,0:T(8,128)S(1)}, f32[264,128]{1,0:T(8,128)S(1)}, u32[]{:S(2)}, u32[]{:S(2)}) collective-permute-start(f32[264,128]{1,0:T(8,128)S(1)} %concatenate.38), channel_id=1, source_target_pairs={{224,96},{352,224},{480,352},{225,97},{353,225},{481,353},{226,98}... | collective-permute-start | bytes 405512 | tf_op jit(solution)/shard_map/ppermute | solution.py:39
  32.6 8.5 %collective-permute-start.4 = (f32[264,128]{1,0:T(8,128)S(1)}, f32[264,128]{1,0:T(8,128)S(1)}, u32[]{:S(2)}, u32[]{:S(2)}) collective-permute-start(f32[264,128]{1,0:T(8,128)S(1)} %concatenate.38), channel_id=1, source_target_pairs={{96,224},{224,352},{352,480},{608,736},{736,864},{864,992},{97,225... | collective-permute-start | bytes 405512 | tf_op jit(solution)/shard_map/ppermute | solution.py:39
  44.8 1.4 %collective-permute-start.7 = (f32[264,128]{1,0:T(8,128)S(1)}, f32[264,128]{1,0:T(8,128)S(1)}, u32[]{:S(2)}, u32[]{:S(2)}) collective-permute-start(f32[264,128]{1,0:T(8,128)S(1)} %concatenate.40), channel_id=1, source_target_pairs={{352,96},{480,224},{353,97},{481,225},{354,98},{482,226},{355,99},... | collective-permute-start | bytes 405512 | tf_op jit(solution)/shard_map/ppermute | solution.py:39
  46.3 13.4 %collective-permute-start.5 = (f32[264,128]{1,0:T(8,128)S(1)}, f32[264,128]{1,0:T(8,128)S(1)}, u32[]{:S(2)}, u32[]{:S(2)}) collective-permute-start(f32[264,128]{1,0:T(8,128)S(1)} %concatenate.39), channel_id=1, source_target_pairs={{96,352},{224,480},{608,864},{736,992},{97,353},{225,481},{609,865... | collective-permute-start | bytes 405512 | tf_op jit(solution)/shard_map/ppermute | solution.py:39
  63.4 14.1 %collective-permute-start.8 = (f32[264,128]{1,0:T(8,128)S(1)}, f32[264,128]{1,0:T(8,128)S(1)}, u32[]{:S(2)}, u32[]{:S(2)}) collective-permute-start(f32[264,128]{1,0:T(8,128)S(1)} %concatenate.41), channel_id=1, source_target_pairs={{480,736},{96,992},{481,737},{97,993},{482,738},{98,994},{483,739}... | collective-permute-start | bytes 405512 | tf_op jit(solution)/shard_map/ppermute | solution.py:72
  77.4 2.2 %collective-permute-start.9 = (f32[264,128]{1,0:T(8,128)S(1)}, f32[264,128]{1,0:T(8,128)S(1)}, u32[]{:S(2)}, u32[]{:S(2)}) collective-permute-start(f32[264,128]{1,0:T(8,128)S(1)} %concatenate.41), channel_id=1, source_target_pairs={{480,608},{96,864},{481,609},{97,865},{482,610},{98,866},{483,611}... | collective-permute-start | bytes 405512 | tf_op jit(solution)/shard_map/ppermute | solution.py:72
  79.7 1.9 %collective-permute-start.13 = (f32[264,128]{1,0:T(8,128)S(1)}, f32[264,128]{1,0:T(8,128)S(1)}, u32[]{:S(2)}, u32[]{:S(2)}) collective-permute-start(f32[264,128]{1,0:T(8,128)S(1)} %concatenate.44), channel_id=1, source_target_pairs={{0,16},{16,0},{1,17},{17,1},{2,18},{18,2},{3,19},{19,3},{4,20},{20... | collective-permute-start | bytes 405512 | tf_op jit(solution)/shard_map/ppermute | solution.py:35
  85.4 1.3 %collective-permute-start.12 = (f32[264,128]{1,0:T(8,128)}, f32[264,128]{1,0:T(8,128)S(1)}, u32[]{:S(2)}, u32[]{:S(2)}) collective-permute-start(f32[264,128]{1,0:T(8,128)} %concatenate.43), channel_id=1, source_target_pairs={{96,128},{112,144},{224,256},{240,272},{352,384},{368,400},{480,51... | collective-permute-start | bytes 405512 | tf_op jit(solution)/shard_map/ppermute | solution.py:119
  87.0 1.9 %collective-permute-start.15 = (f32[264,128]{1,0:T(8,128)}, f32[264,128]{1,0:T(8,128)}, u32[]{:S(2)}, u32[]{:S(2)}) collective-permute-start(f32[264,128]{1,0:T(8,128)} %concatenate.43), channel_id=1, source_target_pairs={{96,176},{112,160},{224,304},{240,288},{352,432},{368,416},{480,56... | collective-permute-start | bytes 405512 | tf_op jit(solution)/shard_map/ppermute | solution.py:120
  88.9 1.9 %collective-permute-start.16 = (f32[264,128]{1,0:T(8,128)}, f32[264,128]{1,0:T(8,128)}, u32[]{:S(2)}, u32[]{:S(2)}) collective-permute-start(f32[264,128]{1,0:T(8,128)} %concatenate.43), channel_id=1, source_target_pairs={{96,144},{112,128},{224,272},{240,256},{352,400},{368,384},{480,52... | collective-permute-start | bytes 405512 | tf_op jit(solution)/shard_map/ppermute | solution.py:120
  91.5 1.9 %collective-permute-start.10 = (f32[264,128]{1,0:T(8,128)}, f32[264,128]{1,0:T(8,128)}, u32[]{:S(2)}, u32[]{:S(2)}) collective-permute-start(f32[264,128]{1,0:T(8,128)} %concatenate.42), channel_id=1, source_target_pairs={{96,64},{112,80},{224,192},{240,208},{352,320},{368,336},{480,448}... | collective-permute-start | bytes 405512 | tf_op jit(solution)/shard_map/ppermute | solution.py:119
  93.5 1.9 %collective-permute-start.14 = (f32[264,128]{1,0:T(8,128)}, f32[264,128]{1,0:T(8,128)}, u32[]{:S(2)}, u32[]{:S(2)}) collective-permute-start(f32[264,128]{1,0:T(8,128)} %concatenate.42), channel_id=1, source_target_pairs={{96,80},{112,64},{224,208},{240,192},{352,336},{368,320},{480,464}... | collective-permute-start | bytes 405512 | tf_op jit(solution)/shard_map/ppermute | solution.py:120
  95.4 1.9 %collective-permute-start.17 = (f32[264,128]{1,0:T(8,128)}, f32[264,128]{1,0:T(8,128)}, u32[]{:S(2)}, u32[]{:S(2)}) collective-permute-start(f32[264,128]{1,0:T(8,128)} %concatenate.42), channel_id=1, source_target_pairs={{0,16},{16,0},{1,17},{17,1},{2,18},{18,2},{3,19},{19,3},{4,20},{20... | collective-permute-start | bytes 405512 | tf_op jit(solution)/shard_map/ppermute | solution.py:107
  97.3 2.5 %fusion.3 = f32[512,4,128]{0,2,1:T(8,128)S(1)} fusion(bf16[512,4,128]{0,2,1:T(8,128)(2,1)} %bitcast.84, pred[512,512]{1,0:T(8,128)(4,1)S(1)} %fusion.4, bf16[512,512]{1,0:T(8,128)(2,1)} %param.6, bf16[512,512]{1,0:T(8,128)(2,1)S(1)} %copy-done), kind=kOutput, calls=%fused_computation.5 | convolution fusion | flops 538968064 | bytes 2883584 | tf_op jit(solution)/shard_map/while/body/eval_jaxpr/hts,shd->thd/dot_general | solution.py:168
  105.9 7.0 %all-to-all-start = ((f32[16,1,512]{2,1,0:T(1,128)}), f32[16,1,512]{2,1,0:T(1,128)S(1)}, u32[]{:S(2)}, u32[]{:S(2)}) async-start(f32[16,1,512]{2,1,0:T(1,128)} %broadcast_in_dim.97), calls=%async_computation | async-start | bytes 65536 | tf_op jit(solution)/shard_map/all_to_all | solution.py:149
  113.3 7.3 %all-to-all-done = f32[16,1,512]{2,1,0:T(1,128)S(1)} async-done(((f32[16,1,512]{2,1,0:T(1,128)}), f32[16,1,512]{2,1,0:T(1,128)S(1)}, u32[]{:S(2)}, u32[]{:S(2)}) %all-to-all-start) | async-done | bytes 32800 | tf_op jit(solution)/shard_map/all_to_all | solution.py:149
  (84 shorter events, 18.0 us)
Async XLA Ops:
  0.0 97.3 %copy-start = (bf16[512,512]{1,0:T(8,128)(2,1)S(1)}, bf16[512,512]{1,0:T(8,128)(2,1)}, u32[]{:S(2)}) copy-start(bf16[512,512]{1,0:T(8,128)(2,1)} %param.4) | copy-start | bytes 1572868
  5.8 3.4 %collective-permute-start = (f32[520,128]{1,0:T(8,128)S(1)}, f32[520,128]{1,0:T(8,128)S(1)}, u32[]{:S(2)}, u32[]{:S(2)}) collective-permute-start(f32[520,128]{1,0:T(8,128)S(1)} %concatenate.36), channel_id=1, source_target_pairs={{0,16},{16,0},{1,17},{17,1},{2,18},{18,2},{3,19},{19,3},{4,20},{20... | collective-permute-start | bytes 798728 | tf_op jit(solution)/shard_map/ppermute | solution.py:35
  9.3 90.6 %copy-start.1 = (f32[520,128]{1,0:T(8,128)}, f32[520,128]{1,0:T(8,128)S(1)}, u32[]{:S(2)}) copy-start(f32[520,128]{1,0:T(8,128)S(1)} %collective-permute-done) | copy-start | bytes 798724
  10.4 17.5 %collective-permute-start.3 = (f32[264,128]{1,0:T(8,128)S(1)}, f32[264,128]{1,0:T(8,128)S(1)}, u32[]{:S(2)}, u32[]{:S(2)}) collective-permute-start(f32[264,128]{1,0:T(8,128)S(1)} %concatenate.37), channel_id=1, source_target_pairs={{0,96},{128,224},{256,352},{384,480},{512,608},{640,736},{768,864}... | collective-permute-start | bytes 405512 | tf_op jit(solution)/shard_map/ppermute | solution.py:39
  11.7 17.3 %collective-permute-start.2 = (f32[264,128]{1,0:T(8,128)S(1)}, f32[264,128]{1,0:T(8,128)S(1)}, u32[]{:S(2)}, u32[]{:S(2)}) collective-permute-start(f32[264,128]{1,0:T(8,128)S(1)} %concatenate.37), channel_id=1, source_target_pairs={{0,64},{32,96},{128,192},{160,224},{256,320},{288,352},{384,448},{... | collective-permute-start | bytes 405512 | tf_op jit(solution)/shard_map/ppermute | solution.py:39
  13.0 17.0 %collective-permute-start.1 = (f32[264,128]{1,0:T(8,128)S(1)}, f32[264,128]{1,0:T(8,128)S(1)}, u32[]{:S(2)}, u32[]{:S(2)}) collective-permute-start(f32[264,128]{1,0:T(8,128)S(1)} %concatenate.37), channel_id=1, source_target_pairs={{0,32},{32,64},{64,96},{128,160},{160,192},{192,224},{256,288},{28... | collective-permute-start | bytes 405512 | tf_op jit(solution)/shard_map/ppermute | solution.py:39
  31.3 10.8 %collective-permute-start.6 = (f32[264,128]{1,0:T(8,128)S(1)}, f32[264,128]{1,0:T(8,128)S(1)}, u32[]{:S(2)}, u32[]{:S(2)}) collective-permute-start(f32[264,128]{1,0:T(8,128)S(1)} %concatenate.38), channel_id=1, source_target_pairs={{224,96},{352,224},{480,352},{225,97},{353,225},{481,353},{226,98}... | collective-permute-start | bytes 405512 | tf_op jit(solution)/shard_map/ppermute | solution.py:39
  32.6 11.0 %collective-permute-start.4 = (f32[264,128]{1,0:T(8,128)S(1)}, f32[264,128]{1,0:T(8,128)S(1)}, u32[]{:S(2)}, u32[]{:S(2)}) collective-permute-start(f32[264,128]{1,0:T(8,128)S(1)} %concatenate.38), channel_id=1, source_target_pairs={{96,224},{224,352},{352,480},{608,736},{736,864},{864,992},{97,225... | collective-permute-start | bytes 405512 | tf_op jit(solution)/shard_map/ppermute | solution.py:39
  44.8 37.4 %copy-start.2 = (f32[264,128]{1,0:T(8,128)S(1)}, f32[264,128]{1,0:T(8,128)}, u32[]{:S(2)}) copy-start(f32[264,128]{1,0:T(8,128)} %constant.107.clone.1) | copy-start | bytes 405508
  44.8 15.9 %collective-permute-start.7 = (f32[264,128]{1,0:T(8,128)S(1)}, f32[264,128]{1,0:T(8,128)S(1)}, u32[]{:S(2)}, u32[]{:S(2)}) collective-permute-start(f32[264,128]{1,0:T(8,128)S(1)} %concatenate.40), channel_id=1, source_target_pairs={{352,96},{480,224},{353,97},{481,225},{354,98},{482,226},{355,99},... | collective-permute-start | bytes 405512 | tf_op jit(solution)/shard_map/ppermute | solution.py:39
  46.3 15.9 %collective-permute-start.5 = (f32[264,128]{1,0:T(8,128)S(1)}, f32[264,128]{1,0:T(8,128)S(1)}, u32[]{:S(2)}, u32[]{:S(2)}) collective-permute-start(f32[264,128]{1,0:T(8,128)S(1)} %concatenate.39), channel_id=1, source_target_pairs={{96,352},{224,480},{608,864},{736,992},{97,353},{225,481},{609,865... | collective-permute-start | bytes 405512 | tf_op jit(solution)/shard_map/ppermute | solution.py:39
  63.4 18.3 %collective-permute-start.8 = (f32[264,128]{1,0:T(8,128)S(1)}, f32[264,128]{1,0:T(8,128)S(1)}, u32[]{:S(2)}, u32[]{:S(2)}) collective-permute-start(f32[264,128]{1,0:T(8,128)S(1)} %concatenate.41), channel_id=1, source_target_pairs={{480,736},{96,992},{481,737},{97,993},{482,738},{98,994},{483,739}... | collective-permute-start | bytes 405512 | tf_op jit(solution)/shard_map/ppermute | solution.py:72
  77.4 4.7 %collective-permute-start.9 = (f32[264,128]{1,0:T(8,128)S(1)}, f32[264,128]{1,0:T(8,128)S(1)}, u32[]{:S(2)}, u32[]{:S(2)}) collective-permute-start(f32[264,128]{1,0:T(8,128)S(1)} %concatenate.41), channel_id=1, source_target_pairs={{480,608},{96,864},{481,609},{97,865},{482,610},{98,866},{483,611}... | collective-permute-start | bytes 405512 | tf_op jit(solution)/shard_map/ppermute | solution.py:72
  79.7 7.1 %copy-start.5 = (s32[512]{0:T(512)S(1)}, s32[512]{0:T(512)}, u32[]{:S(2)}) copy-start(s32[512]{0:T(512)} %param.7) | copy-start | bytes 6148
  79.7 11.8 %collective-permute-start.13 = (f32[264,128]{1,0:T(8,128)S(1)}, f32[264,128]{1,0:T(8,128)S(1)}, u32[]{:S(2)}, u32[]{:S(2)}) collective-permute-start(f32[264,128]{1,0:T(8,128)S(1)} %concatenate.44), channel_id=1, source_target_pairs={{0,16},{16,0},{1,17},{17,1},{2,18},{18,2},{3,19},{19,3},{4,20},{20... | collective-permute-start | bytes 405512 | tf_op jit(solution)/shard_map/ppermute | solution.py:35
  84.2 9.3 %collective-permute-start.11 = (f32[264,128]{1,0:T(8,128)}, f32[264,128]{1,0:T(8,128)S(1)}, u32[]{:S(2)}, u32[]{:S(2)}) collective-permute-start(f32[264,128]{1,0:T(8,128)} %concatenate.43), channel_id=1, source_target_pairs={{96,160},{112,176},{224,288},{240,304},{352,416},{368,432},{480,54... | collective-permute-start | bytes 405512 | tf_op jit(solution)/shard_map/ppermute | solution.py:119
  85.4 10.0 %collective-permute-start.12 = (f32[264,128]{1,0:T(8,128)}, f32[264,128]{1,0:T(8,128)S(1)}, u32[]{:S(2)}, u32[]{:S(2)}) collective-permute-start(f32[264,128]{1,0:T(8,128)} %concatenate.43), channel_id=1, source_target_pairs={{96,128},{112,144},{224,256},{240,272},{352,384},{368,400},{480,51... | collective-permute-start | bytes 405512 | tf_op jit(solution)/shard_map/ppermute | solution.py:119
  87.0 14.1 %collective-permute-start.15 = (f32[264,128]{1,0:T(8,128)}, f32[264,128]{1,0:T(8,128)}, u32[]{:S(2)}, u32[]{:S(2)}) collective-permute-start(f32[264,128]{1,0:T(8,128)} %concatenate.43), channel_id=1, source_target_pairs={{96,176},{112,160},{224,304},{240,288},{352,432},{368,416},{480,56... | collective-permute-start | bytes 405512 | tf_op jit(solution)/shard_map/ppermute | solution.py:120
  88.9 12.2 %collective-permute-start.16 = (f32[264,128]{1,0:T(8,128)}, f32[264,128]{1,0:T(8,128)}, u32[]{:S(2)}, u32[]{:S(2)}) collective-permute-start(f32[264,128]{1,0:T(8,128)} %concatenate.43), channel_id=1, source_target_pairs={{96,144},{112,128},{224,272},{240,256},{352,400},{368,384},{480,52... | collective-permute-start | bytes 405512 | tf_op jit(solution)/shard_map/ppermute | solution.py:120
  91.5 9.6 %copy-start.3 = (f32[264,128]{1,0:T(8,128)}, f32[264,128]{1,0:T(8,128)S(1)}, u32[]{:S(2)}) copy-start(f32[264,128]{1,0:T(8,128)S(1)} %collective-permute-done.13) | copy-start | bytes 405508
  91.5 9.6 %collective-permute-start.10 = (f32[264,128]{1,0:T(8,128)}, f32[264,128]{1,0:T(8,128)}, u32[]{:S(2)}, u32[]{:S(2)}) collective-permute-start(f32[264,128]{1,0:T(8,128)} %concatenate.42), channel_id=1, source_target_pairs={{96,64},{112,80},{224,192},{240,208},{352,320},{368,336},{480,448}... | collective-permute-start | bytes 405512 | tf_op jit(solution)/shard_map/ppermute | solution.py:119
  93.5 7.7 %collective-permute-start.14 = (f32[264,128]{1,0:T(8,128)}, f32[264,128]{1,0:T(8,128)}, u32[]{:S(2)}, u32[]{:S(2)}) collective-permute-start(f32[264,128]{1,0:T(8,128)} %concatenate.42), channel_id=1, source_target_pairs={{96,80},{112,64},{224,208},{240,192},{352,336},{368,320},{480,464}... | collective-permute-start | bytes 405512 | tf_op jit(solution)/shard_map/ppermute | solution.py:120
  95.4 5.8 %collective-permute-start.17 = (f32[264,128]{1,0:T(8,128)}, f32[264,128]{1,0:T(8,128)}, u32[]{:S(2)}, u32[]{:S(2)}) collective-permute-start(f32[264,128]{1,0:T(8,128)} %concatenate.42), channel_id=1, source_target_pairs={{0,16},{16,0},{1,17},{17,1},{2,18},{18,2},{3,19},{19,3},{4,20},{20... | collective-permute-start | bytes 405512 | tf_op jit(solution)/shard_map/ppermute | solution.py:107
  105.9 14.6 %all-to-all-start = ((f32[16,1,512]{2,1,0:T(1,128)}), f32[16,1,512]{2,1,0:T(1,128)S(1)}, u32[]{:S(2)}, u32[]{:S(2)}) async-start(f32[16,1,512]{2,1,0:T(1,128)} %broadcast_in_dim.97), calls=%async_computation | async-start | bytes 65536 | tf_op jit(solution)/shard_map/all_to_all | solution.py:149
  (4 other events, 14.0 us)

commit v10 on v8

--- a/solution.py
+++ b/solution.py
@@ -60,6 +60,8 @@
     source = pack(select(which == 0, back, upto))
     ahead = [g for g in range(half, groups) if ends[g] - ends[half - 1] <= count - ends[g] + ends[0]]
     behind = [g for g in range(half, groups) if g not in ahead]
+    ahead = sorted(ahead, key=lambda g: ends[g] - ends[half - 1])
+    behind = sorted(behind, key=lambda g: ends[0] - ends[g] + count)
     lower = pack(empty)
     for k in range(max(len(ahead), len(behind))):
         pairs, hit = ([], jnp.zeros((), jnp.bool_))

time: 117 us -> 118 us (level)
  no operation moved by 1% of the time
where the time goes in v10:
time: 118 us; the launch traced here: 117 us
  waiting for transfers between devices  68.6 us (58%)
  starting transfers between devices  24.1 us (20%)
  local copies, waits for them, and re-layouts  9.15 us (8%)
  between operations  8.55 us (7%)
  other arithmetic  3.78 us (3%)
  matrix products  3.3 us (3%)
    ppermute x1, waiting for transfers between devices, scan_chips(): got = lax.ppermute(carried, axis, pairs)  45.3 us
    ppermute x7, waiting for transfers between devices, received(): state, last = unpack(lax.ppermute(pack(value), axis, pairs))  13.2 us
    ppermute x7, starting transfers between devices, received(): state, last = unpack(lax.ppermute(pack(value), axis, pairs))  9.22 us
    all_to_all x1, waiting for transfers between devices, head_sum(): return jnp.sum(lax.all_to_all(spread, axis, 0, 0, tiled=True), axis=0)  7.26 us
    all_to_all x1, starting transfers between devices, head_sum(): return jnp.sum(lax.all_to_all(spread, axis, 0, 0, tiled=True), axis=0)  7.03 us
    slice x10, local copies, waits for them, and re-layouts, unpack(): return (state, packed[-TAG, 0].astype(jnp.int32))  5.4 us
    ppermute x2, starting transfers between devices, swap_cores(): return unpack(lax.ppermute(pack(value), core_axis, [(0, 1), (1, 0)]))  3.84 us
    ppermute x2, waiting for transfers between devices, swap_cores(): return unpack(lax.ppermute(pack(value), core_axis, [(0, 1), (1, 0)]))  2.76 us
  transfers between devices with their start and end apart: 15, of which 5 were waited for; matrix products, arithmetic and copies ran while one was open for 5% of the time, Pallas kernels for 0%

profile of v10, /device:TPU:64, one launch (start us, length us, event | category | flops | bytes accessed | tf_op | source)
XLA Modules:
  0.0 117.4 jit_solution(4043202151790529596)
XLA Ops:
  0.0 1.4 %slice.73 = s32[1]{0:T(128)} slice(s32[512]{0:T(512)} %param.7), slice={[511:512]} | slice | bytes 8 | tf_op jit(solution)/shard_map/while/body/eval_jaxpr/slice | solution.py:163
  1.4 1.3 %broadcast_compare_fusion.1 = pred[512]{0:T(512)(128)(4,1)S(1)} fusion(s32[512]{0:T(512)} %param.7, s32[]{:T(128)} %bitcast.1), kind=kLoop, calls=%fused_computation.54 | loop fusion | flops 512 | bytes 2564 | tf_op jit(solution)/shard_map/while/body/eval_jaxpr/eq | solution.py:164
  3.3 1.3 %copy.28 = bf16[512,512]{0,1:T(8,128)(2,1)S(1)} copy(bf16[512,512]{1,0:T(8,128)(2,1)} %param.5) | data formatting | bytes 1048576 | tf_op jit(solution)/shard_map/while/body/jit(dynamic_index_in_dim)/squeeze | solution.py:173
  5.6 1.9 %collective-permute-start = (f32[520,128]{1,0:T(8,128)S(1)}, f32[520,128]{1,0:T(8,128)S(1)}, u32[]{:S(2)}, u32[]{:S(2)}) collective-permute-start(f32[520,128]{1,0:T(8,128)S(1)} %concatenate.36), channel_id=1, source_target_pairs={{0,16},{16,0},{1,17},{17,1},{2,18},{18,2},{3,19},{19,3},{4,20},{20... | collective-permute-start | bytes 798728 | tf_op jit(solution)/shard_map/ppermute | solution.py:35
  7.5 1.5 %collective-permute-done = f32[520,128]{1,0:T(8,128)S(1)} collective-permute-done((f32[520,128]{1,0:T(8,128)S(1)}, f32[520,128]{1,0:T(8,128)S(1)}, u32[]{:S(2)}, u32[]{:S(2)}) %collective-permute-start) | collective-permute-done | bytes 266272 | tf_op jit(solution)/shard_map/ppermute | solution.py:35
  10.3 0.7 collective-permute-start.3
  11.0 1.3 %collective-permute-start.2 = (f32[264,128]{1,0:T(8,128)S(1)}, f32[264,128]{1,0:T(8,128)S(1)}, u32[]{:S(2)}, u32[]{:S(2)}) collective-permute-start(f32[264,128]{1,0:T(8,128)S(1)} %concatenate.37), channel_id=1, source_target_pairs={{0,64},{32,96},{128,192},{160,224},{256,320},{288,352},{384,448},{... | collective-permute-start | bytes 405512 | tf_op jit(solution)/shard_map/ppermute | solution.py:39
  12.3 4.5 %collective-permute-start.1 = (f32[264,128]{1,0:T(8,128)S(1)}, f32[264,128]{1,0:T(8,128)S(1)}, u32[]{:S(2)}, u32[]{:S(2)}) collective-permute-start(f32[264,128]{1,0:T(8,128)S(1)} %concatenate.37), channel_id=1, source_target_pairs={{0,32},{32,64},{64,96},{128,160},{160,192},{192,224},{256,288},{28... | collective-permute-start | bytes 405512 | tf_op jit(solution)/shard_map/ppermute | solution.py:39
  18.0 13.2 %collective-permute-done.2 = f32[264,128]{1,0:T(8,128)S(1)} collective-permute-done((f32[264,128]{1,0:T(8,128)S(1)}, f32[264,128]{1,0:T(8,128)S(1)}, u32[]{:S(2)}, u32[]{:S(2)}) %collective-permute-start.2) | collective-permute-done | bytes 135200 | tf_op jit(solution)/shard_map/ppermute | solution.py:39
  33.8 0.7 collective-permute-start.6
  34.5 0.7 collective-permute-start.4
  37.7 0.8 collective-permute-start.7
  38.5 0.7 collective-permute-start.5
  42.5 0.7 collective-permute-start.9
  44.6 0.7 collective-permute-start.10
  45.9 0.9 fusion.4
  46.9 1.3 %collective-permute-start.12 = (f32[264,128]{1,0:T(8,128)S(1)}, f32[264,128]{1,0:T(8,128)S(1)}, u32[]{:S(2)}, u32[]{:S(2)}) collective-permute-start(f32[264,128]{1,0:T(8,128)S(1)} %select_select_fusion), channel_id=1, source_target_pairs={{96,64},{224,192},{352,320},{480,448},{608,576},{736,704},{864,832... | collective-permute-start | bytes 405512 | tf_op jit(solution)/shard_map/ppermute | solution.py:115
  48.2 2.6 %fusion.3 = f32[512,4,128]{0,2,1:T(8,128)S(1)} fusion(bf16[512,4,128]{0,2,1:T(8,128)(2,1)} %bitcast.78, pred[512,512]{1,0:T(8,128)(4,1)} %fusion.4, bf16[512,512]{1,0:T(8,128)(2,1)} %param.6, bf16[512,512]{1,0:T(8,128)(2,1)S(1)} %copy-done), kind=kOutput, calls=%fused_computation.5 | convolution fusion | flops 538968064 | bytes 2883584 | tf_op jit(solution)/shard_map/while/body/eval_jaxpr/hts,shd->thd/dot_general | solution.py:162
  50.9 45.3 %collective-permute-done.12 = f32[264,128]{1,0:T(8,128)S(1)} collective-permute-done((f32[264,128]{1,0:T(8,128)S(1)}, f32[264,128]{1,0:T(8,128)S(1)}, u32[]{:S(2)}, u32[]{:S(2)}) %collective-permute-start.12) | collective-permute-done | bytes 135200 | tf_op jit(solution)/shard_map/ppermute | solution.py:115
  97.5 1.9 %collective-permute-start.13 = (f32[264,128]{1,0:T(8,128)S(1)}, f32[264,128]{1,0:T(8,128)S(1)}, u32[]{:S(2)}, u32[]{:S(2)}) collective-permute-start(f32[264,128]{1,0:T(8,128)S(1)} %concatenate.44), channel_id=1, source_target_pairs={{0,16},{16,0},{1,17},{17,1},{2,18},{18,2},{3,19},{19,3},{4,20},{20... | collective-permute-start | bytes 405512 | tf_op jit(solution)/shard_map/ppermute | solution.py:35
  99.5 1.3 %collective-permute-done.13 = f32[264,128]{1,0:T(8,128)S(1)} collective-permute-done((f32[264,128]{1,0:T(8,128)S(1)}, f32[264,128]{1,0:T(8,128)S(1)}, u32[]{:S(2)}, u32[]{:S(2)}) %collective-permute-start.13) | collective-permute-done | bytes 135200 | tf_op jit(solution)/shard_map/ppermute | solution.py:35
  101.8 7.0 %all-to-all-start = ((f32[16,1,512]{2,1,0:T(1,128)}), f32[16,1,512]{2,1,0:T(1,128)S(1)}, u32[]{:S(2)}, u32[]{:S(2)}) async-start(f32[16,1,512]{2,1,0:T(1,128)} %broadcast_in_dim.97), calls=%async_computation | async-start | bytes 65536 | tf_op jit(solution)/shard_map/all_to_all | solution.py:143
  109.2 7.3 %all-to-all-done = f32[16,1,512]{2,1,0:T(1,128)S(1)} async-done(((f32[16,1,512]{2,1,0:T(1,128)}), f32[16,1,512]{2,1,0:T(1,128)S(1)}, u32[]{:S(2)}, u32[]{:S(2)}) %all-to-all-start) | async-done | bytes 32800 | tf_op jit(solution)/shard_map/all_to_all | solution.py:143
  116.5 0.9 multiply_convert_fusion
  (73 shorter events, 9.2 us)
Async XLA Ops:
  0.0 48.2 %copy-start = (bf16[512,512]{1,0:T(8,128)(2,1)S(1)}, bf16[512,512]{1,0:T(8,128)(2,1)}, u32[]{:S(2)}) copy-start(bf16[512,512]{1,0:T(8,128)(2,1)} %param.4) | copy-start | bytes 1572868
  0.0 5.2 %copy-start.6 = (bf16[512,512]{1,0:T(8,128)(2,1)S(1)}, bf16[512,512]{1,0:T(8,128)(2,1)}, u32[]{:S(2)}) copy-start(bf16[512,512]{1,0:T(8,128)(2,1)} %param.6) | copy-start | bytes 1572868
  4.6 1.0 copy-start.3
  5.6 3.4 %collective-permute-start = (f32[520,128]{1,0:T(8,128)S(1)}, f32[520,128]{1,0:T(8,128)S(1)}, u32[]{:S(2)}, u32[]{:S(2)}) collective-permute-start(f32[520,128]{1,0:T(8,128)S(1)} %concatenate.36), channel_id=1, source_target_pairs={{0,16},{16,0},{1,17},{17,1},{2,18},{18,2},{3,19},{19,3},{4,20},{20... | collective-permute-start | bytes 798728 | tf_op jit(solution)/shard_map/ppermute | solution.py:35
  9.0 41.8 %copy-start.1 = (f32[520,128]{1,0:T(8,128)}, f32[520,128]{1,0:T(8,128)S(1)}, u32[]{:S(2)}) copy-start(f32[520,128]{1,0:T(8,128)S(1)} %collective-permute-done) | copy-start | bytes 798724
  10.3 6.5 %collective-permute-start.3 = (f32[264,128]{1,0:T(8,128)S(1)}, f32[264,128]{1,0:T(8,128)S(1)}, u32[]{:S(2)}, u32[]{:S(2)}) collective-permute-start(f32[264,128]{1,0:T(8,128)S(1)} %concatenate.37), channel_id=1, source_target_pairs={{0,96},{128,224},{256,352},{384,480},{512,608},{640,736},{768,864}... | collective-permute-start | bytes 405512 | tf_op jit(solution)/shard_map/ppermute | solution.py:39
  11.0 20.2 %collective-permute-start.2 = (f32[264,128]{1,0:T(8,128)S(1)}, f32[264,128]{1,0:T(8,128)S(1)}, u32[]{:S(2)}, u32[]{:S(2)}) collective-permute-start(f32[264,128]{1,0:T(8,128)S(1)} %concatenate.37), channel_id=1, source_target_pairs={{0,64},{32,96},{128,192},{160,224},{256,320},{288,352},{384,448},{... | collective-permute-start | bytes 405512 | tf_op jit(solution)/shard_map/ppermute | solution.py:39
  12.3 20.1 %collective-permute-start.1 = (f32[264,128]{1,0:T(8,128)S(1)}, f32[264,128]{1,0:T(8,128)S(1)}, u32[]{:S(2)}, u32[]{:S(2)}) collective-permute-start(f32[264,128]{1,0:T(8,128)S(1)} %concatenate.37), channel_id=1, source_target_pairs={{0,32},{32,64},{64,96},{128,160},{160,192},{192,224},{256,288},{28... | collective-permute-start | bytes 405512 | tf_op jit(solution)/shard_map/ppermute | solution.py:39
  33.8 1.4 %collective-permute-start.6 = (f32[264,128]{1,0:T(8,128)S(1)}, f32[264,128]{1,0:T(8,128)S(1)}, u32[]{:S(2)}, u32[]{:S(2)}) collective-permute-start(f32[264,128]{1,0:T(8,128)S(1)} %concatenate.38), channel_id=1, source_target_pairs={{224,96},{352,224},{480,352},{225,97},{353,225},{481,353},{226,98}... | collective-permute-start | bytes 405512 | tf_op jit(solution)/shard_map/ppermute | solution.py:39
  34.5 1.9 %collective-permute-start.4 = (f32[264,128]{1,0:T(8,128)S(1)}, f32[264,128]{1,0:T(8,128)S(1)}, u32[]{:S(2)}, u32[]{:S(2)}) collective-permute-start(f32[264,128]{1,0:T(8,128)S(1)} %concatenate.38), channel_id=1, source_target_pairs={{96,224},{224,352},{352,480},{608,736},{736,864},{864,992},{97,225... | collective-permute-start | bytes 405512 | tf_op jit(solution)/shard_map/ppermute | solution.py:39
  37.7 5.5 %copy-start.2 = (f32[264,128]{1,0:T(8,128)S(1)}, f32[264,128]{1,0:T(8,128)}, u32[]{:S(2)}) copy-start(f32[264,128]{1,0:T(8,128)} %constant.106.clone.1) | copy-start | bytes 405508
  37.7 1.5 %collective-permute-start.7 = (f32[264,128]{1,0:T(8,128)S(1)}, f32[264,128]{1,0:T(8,128)S(1)}, u32[]{:S(2)}, u32[]{:S(2)}) collective-permute-start(f32[264,128]{1,0:T(8,128)S(1)} %concatenate.40), channel_id=1, source_target_pairs={{352,96},{480,224},{353,97},{481,225},{354,98},{482,226},{355,99},... | collective-permute-start | bytes 405512 | tf_op jit(solution)/shard_map/ppermute | solution.py:39
  38.5 1.9 %collective-permute-start.5 = (f32[264,128]{1,0:T(8,128)S(1)}, f32[264,128]{1,0:T(8,128)S(1)}, u32[]{:S(2)}, u32[]{:S(2)}) collective-permute-start(f32[264,128]{1,0:T(8,128)S(1)} %concatenate.39), channel_id=1, source_target_pairs={{96,352},{224,480},{608,864},{736,992},{97,353},{225,481},{609,865... | collective-permute-start | bytes 405512 | tf_op jit(solution)/shard_map/ppermute | solution.py:39
  41.8 4.1 %copy-start.4 = (s32[512]{0:T(512)S(1)}, s32[512]{0:T(512)}, u32[]{:S(2)}) copy-start(s32[512]{0:T(512)} %param.7) | copy-start | bytes 6148
  41.8 1.4 %collective-permute-start.8 = (f32[264,128]{1,0:T(8,128)S(1)}, f32[264,128]{1,0:T(8,128)S(1)}, u32[]{:S(2)}, u32[]{:S(2)}) collective-permute-start(f32[264,128]{1,0:T(8,128)S(1)} %concatenate.41), channel_id=1, source_target_pairs={{480,736},{96,864},{481,737},{97,865},{482,738},{98,866},{483,739}... | collective-permute-start | bytes 405512 | tf_op jit(solution)/shard_map/ppermute | solution.py:74
  42.5 0.7 collective-permute-start.9
  44.6 2.3 %collective-permute-start.10 = (f32[264,128]{1,0:T(8,128)S(1)}, f32[264,128]{1,0:T(8,128)S(1)}, u32[]{:S(2)}, u32[]{:S(2)}) collective-permute-start(f32[264,128]{1,0:T(8,128)S(1)} %concatenate.42), channel_id=1, source_target_pairs={{96,160},{224,288},{352,416},{480,544},{608,672},{736,800},{864,92... | collective-permute-start | bytes 405512 | tf_op jit(solution)/shard_map/ppermute | solution.py:111
  45.2 1.6 %collective-permute-start.11 = (f32[264,128]{1,0:T(8,128)S(1)}, f32[264,128]{1,0:T(8,128)S(1)}, u32[]{:S(2)}, u32[]{:S(2)}) collective-permute-start(f32[264,128]{1,0:T(8,128)S(1)} %concatenate.42), channel_id=1, source_target_pairs={{96,128},{224,256},{352,384},{480,512},{608,640},{736,768},{864,89... | collective-permute-start | bytes 405512 | tf_op jit(solution)/shard_map/ppermute | solution.py:111
  46.9 49.3 %collective-permute-start.12 = (f32[264,128]{1,0:T(8,128)S(1)}, f32[264,128]{1,0:T(8,128)S(1)}, u32[]{:S(2)}, u32[]{:S(2)}) collective-permute-start(f32[264,128]{1,0:T(8,128)S(1)} %select_select_fusion), channel_id=1, source_target_pairs={{96,64},{224,192},{352,320},{480,448},{608,576},{736,704},{864,832... | collective-permute-start | bytes 405512 | tf_op jit(solution)/shard_map/ppermute | solution.py:115
  50.8 48.6 %copy-start.5 = (s32[512]{0:T(512)S(1)}, s32[512]{0:T(512)}, u32[]{:S(2)}) copy-start(s32[512]{0:T(512)} %param.7) | copy-start | bytes 6148
  50.9 49.9 %slice-start = ((f32[520,128]{1,0:T(8,128)}), f32[512,128]{1,0:T(8,128)S(1)}, s32[]{:S(2)}) async-start(f32[520,128]{1,0:T(8,128)} %copy-done.1), calls=%async_computation.1 | async-start | bytes 524288 | tf_op jit(solution)/shard_map/slice | solution.py:30
  97.5 3.2 %collective-permute-start.13 = (f32[264,128]{1,0:T(8,128)S(1)}, f32[264,128]{1,0:T(8,128)S(1)}, u32[]{:S(2)}, u32[]{:S(2)}) collective-permute-start(f32[264,128]{1,0:T(8,128)S(1)} %concatenate.44), channel_id=1, source_target_pairs={{0,16},{16,0},{1,17},{17,1},{2,18},{18,2},{3,19},{19,3},{4,20},{20... | collective-permute-start | bytes 405512 | tf_op jit(solution)/shard_map/ppermute | solution.py:35
  101.8 14.6 %all-to-all-start = ((f32[16,1,512]{2,1,0:T(1,128)}), f32[16,1,512]{2,1,0:T(1,128)S(1)}, u32[]{:S(2)}, u32[]{:S(2)}) async-start(f32[16,1,512]{2,1,0:T(1,128)} %broadcast_in_dim.97), calls=%async_computation | async-start | bytes 65536 | tf_op jit(solution)/shard_map/all_to_all | solution.py:143

commit v11 on v8

--- a/solution.py
+++ b/solution.py
@@ -71,7 +71,7 @@
             hit = hit | (which == behind[k])
         lower = jnp.where(hit, lax.ppermute(source, axis, pairs), lower)
     lower = unpack(lower)
-    return (combine_states(lower, before), combine_states(lower, upto))
+    return (combine_states(lower, before), combine_states(lower, upto), before, upto, half)
 
 
 def scan_chips(own, axis):
@@ -87,7 +87,7 @@
     incl = combine_states(excl, own)
     ends = [group * j + group - 1 for j in range(groups)]
     if groups >= 4 and groups % 2 == 0:
-        before, through = group_prefix(incl, axis, ends, which, empty)
+        before, through, early_before, early_through, split = group_prefix(incl, axis, ends, which, empty)
     else:
         upto, before = (incl, empty)
         shift = 1
@@ -99,18 +99,24 @@
                 upto = combine_states(got, upto)
             shift *= 2
         through = combine_states(before, incl)
-    through = pack(through)
-    carried = pack(before)
+        early_before, early_through, split = (before, through, groups)
+    late = (pack(before), pack(through))
+    early = (pack(early_before), pack(early_through))
+    carried = late[0]
     for place in range(group - 1):
         ahead = place + 1
         behind = group - 1 - place
         if ahead <= behind:
-            pairs = [(ends[j], ends[j] + ahead) for j in range(groups - 1)]
-            got = lax.ppermute(through, axis, pairs)
-            got = jnp.where(which >= 1, got, pack(empty))
+            sources, step, kind = (range(groups - 1), ahead, 1)
         else:
-            pairs = [(ends[j], ends[j] - behind) for j in range(groups)]
-            got = lax.ppermute(carried, axis, pairs)
+            sources, step, kind = (range(groups), -behind, 0)
+        got = pack(empty)
+        for sent, chosen in ((early, [j for j in sources if j < split]), (late, [j for j in sources if j >= split])):
+            if chosen:
+                pairs = [(ends[j], ends[j] + step) for j in chosen]
+                targets = [j + kind for j in chosen]
+                hit = (which >= min(targets)) & (which <= max(targets))
+                got = jnp.where(hit, lax.ppermute(sent[kind], axis, pairs), got)
         carried = jnp.where(offset == place, got, carried)
     return combine_states(unpack(carried), excl)
 

time: 117 us -> 118 us (level)
  the two profiles are of different devices: /device:TPU:64 before, /device:TPU:96 now
where the time goes in v11:
time: 118 us
  starting transfers between devices  63.3 us (54%)
  waiting for transfers between devices  26.5 us (22%)
  local copies, waits for them, and re-layouts  12.7 us (11%)
  between operations  7.9 us (7%)
  other arithmetic  3.88 us (3%)
  matrix products  3.33 us (3%)
    ppermute x7, starting transfers between devices, received(): state, last = unpack(lax.ppermute(pack(value), axis, pairs))  28.3 us
    ppermute x7, waiting for transfers between devices, received(): state, last = unpack(lax.ppermute(pack(value), axis, pairs))  16.5 us
    ppermute x2, starting transfers between devices, group_prefix(): lower = jnp.where(hit, lax.ppermute(source, axis, pairs), lower)  16.3 us
    ppermute x6, starting transfers between devices, scan_chips(): got = jnp.where(hit, lax.ppermute(sent[kind], axis, pairs), got)  7.82 us
    all_to_all x1, waiting for transfers between devices, head_sum(): return jnp.sum(lax.all_to_all(spread, axis, 0, 0, tiled=True), axis=0)  7.26 us
    all_to_all x1, starting transfers between devices, head_sum(): return jnp.sum(lax.all_to_all(spread, axis, 0, 0, tiled=True), axis=0)  7.04 us
    slice x10, local copies, waits for them, and re-layouts, unpack(): return (state, packed[-TAG, 0].astype(jnp.int32))  4.92 us
    ppermute x2, starting transfers between devices, swap_cores(): return unpack(lax.ppermute(pack(value), core_axis, [(0, 1), (1, 0)]))  3.84 us
  transfers between devices with their start and end apart: 18, of which 8 were waited for; matrix products, arithmetic and copies ran while one was open for 8% of the time, Pallas kernels for 0%

profile of v11, /device:TPU:96, one launch (start us, length us, event | category | flops | bytes accessed | tf_op | source)
XLA Modules:
  0.0 117.6 jit_solution(3408494980939024241)
XLA Ops:
  0.0 1.4 %slice.73 = s32[1]{0:T(128)} slice(s32[512]{0:T(512)} %param.7), slice={[511:512]} | slice | bytes 8 | tf_op jit(solution)/shard_map/while/body/eval_jaxpr/slice | solution.py:167
  1.4 1.4 %broadcast_compare_fusion.1 = pred[512]{0:T(512)(128)(4,1)S(1)} fusion(s32[512]{0:T(512)} %param.7, s32[]{:T(128)} %bitcast.1), kind=kLoop, calls=%fused_computation.54 | loop fusion | flops 512 | bytes 2564 | tf_op jit(solution)/shard_map/while/body/eval_jaxpr/eq | solution.py:168
  5.8 1.9 %collective-permute-start = (f32[520,128]{1,0:T(8,128)S(1)}, f32[520,128]{1,0:T(8,128)S(1)}, u32[]{:S(2)}, u32[]{:S(2)}) collective-permute-start(f32[520,128]{1,0:T(8,128)S(1)} %concatenate.42), channel_id=1, source_target_pairs={{0,16},{16,0},{1,17},{17,1},{2,18},{18,2},{3,19},{19,3},{4,20},{20... | collective-permute-start | bytes 798728 | tf_op jit(solution)/shard_map/ppermute | solution.py:35
  7.8 1.5 %collective-permute-done = f32[520,128]{1,0:T(8,128)S(1)} collective-permute-done((f32[520,128]{1,0:T(8,128)S(1)}, f32[520,128]{1,0:T(8,128)S(1)}, u32[]{:S(2)}, u32[]{:S(2)}) %collective-permute-start) | collective-permute-done | bytes 266272 | tf_op jit(solution)/shard_map/ppermute | solution.py:35
  10.4 1.3 %collective-permute-start.3 = (f32[264,128]{1,0:T(8,128)S(1)}, f32[264,128]{1,0:T(8,128)S(1)}, u32[]{:S(2)}, u32[]{:S(2)}) collective-permute-start(f32[264,128]{1,0:T(8,128)S(1)} %concatenate.43), channel_id=1, source_target_pairs={{0,96},{128,224},{256,352},{384,480},{512,608},{640,736},{768,864}... | collective-permute-start | bytes 405512 | tf_op jit(solution)/shard_map/ppermute | solution.py:39
  11.7 1.3 %collective-permute-start.2 = (f32[264,128]{1,0:T(8,128)S(1)}, f32[264,128]{1,0:T(8,128)S(1)}, u32[]{:S(2)}, u32[]{:S(2)}) collective-permute-start(f32[264,128]{1,0:T(8,128)S(1)} %concatenate.43), channel_id=1, source_target_pairs={{0,64},{32,96},{128,192},{160,224},{256,320},{288,352},{384,448},{... | collective-permute-start | bytes 405512 | tf_op jit(solution)/shard_map/ppermute | solution.py:39
  13.0 1.3 %collective-permute-start.1 = (f32[264,128]{1,0:T(8,128)S(1)}, f32[264,128]{1,0:T(8,128)S(1)}, u32[]{:S(2)}, u32[]{:S(2)}) collective-permute-start(f32[264,128]{1,0:T(8,128)S(1)} %concatenate.43), channel_id=1, source_target_pairs={{0,32},{32,64},{64,96},{128,160},{160,192},{192,224},{256,288},{28... | collective-permute-start | bytes 405512 | tf_op jit(solution)/shard_map/ppermute | solution.py:39
  14.4 13.6 %collective-permute-done.3 = f32[264,128]{1,0:T(8,128)S(1)} collective-permute-done((f32[264,128]{1,0:T(8,128)S(1)}, f32[264,128]{1,0:T(8,128)S(1)}, u32[]{:S(2)}, u32[]{:S(2)}) %collective-permute-start.3) | collective-permute-done | bytes 135200 | tf_op jit(solution)/shard_map/ppermute | solution.py:39
  31.3 1.3 %collective-permute-start.6 = (f32[264,128]{1,0:T(8,128)S(1)}, f32[264,128]{1,0:T(8,128)S(1)}, u32[]{:S(2)}, u32[]{:S(2)}) collective-permute-start(f32[264,128]{1,0:T(8,128)S(1)} %concatenate.44), channel_id=1, source_target_pairs={{224,96},{352,224},{480,352},{225,97},{353,225},{481,353},{226,98}... | collective-permute-start | bytes 405512 | tf_op jit(solution)/shard_map/ppermute | solution.py:39
  32.6 8.5 %collective-permute-start.4 = (f32[264,128]{1,0:T(8,128)S(1)}, f32[264,128]{1,0:T(8,128)S(1)}, u32[]{:S(2)}, u32[]{:S(2)}) collective-permute-start(f32[264,128]{1,0:T(8,128)S(1)} %concatenate.44), channel_id=1, source_target_pairs={{96,224},{224,352},{352,480},{608,736},{736,864},{864,992},{97,225... | collective-permute-start | bytes 405512 | tf_op jit(solution)/shard_map/ppermute | solution.py:39
  44.8 1.3 %collective-permute-start.7 = (f32[264,128]{1,0:T(8,128)S(1)}, f32[264,128]{1,0:T(8,128)S(1)}, u32[]{:S(2)}, u32[]{:S(2)}) collective-permute-start(f32[264,128]{1,0:T(8,128)S(1)} %concatenate.46), channel_id=1, source_target_pairs={{352,96},{480,224},{353,97},{481,225},{354,98},{482,226},{355,99},... | collective-permute-start | bytes 405512 | tf_op jit(solution)/shard_map/ppermute | solution.py:39
  46.1 13.4 %collective-permute-start.5 = (f32[264,128]{1,0:T(8,128)S(1)}, f32[264,128]{1,0:T(8,128)S(1)}, u32[]{:S(2)}, u32[]{:S(2)}) collective-permute-start(f32[264,128]{1,0:T(8,128)S(1)} %concatenate.45), channel_id=1, source_target_pairs={{96,352},{224,480},{608,864},{736,992},{97,353},{225,481},{609,865... | collective-permute-start | bytes 405512 | tf_op jit(solution)/shard_map/ppermute | solution.py:39
  63.2 14.1 %collective-permute-start.8 = (f32[264,128]{1,0:T(8,128)S(1)}, f32[264,128]{1,0:T(8,128)S(1)}, u32[]{:S(2)}, u32[]{:S(2)}) collective-permute-start(f32[264,128]{1,0:T(8,128)S(1)} %concatenate.47), channel_id=1, source_target_pairs={{480,736},{96,992},{481,737},{97,993},{482,738},{98,994},{483,739}... | collective-permute-start | bytes 405512 | tf_op jit(solution)/shard_map/ppermute | solution.py:72
  77.3 2.2 %collective-permute-start.9 = (f32[264,128]{1,0:T(8,128)S(1)}, f32[264,128]{1,0:T(8,128)S(1)}, u32[]{:S(2)}, u32[]{:S(2)}) collective-permute-start(f32[264,128]{1,0:T(8,128)S(1)} %concatenate.47), channel_id=1, source_target_pairs={{480,608},{96,864},{481,609},{97,865},{482,610},{98,866},{483,611}... | collective-permute-start | bytes 405512 | tf_op jit(solution)/shard_map/ppermute | solution.py:72
  81.1 1.3 %collective-permute-start.13 = (f32[264,128]{1,0:T(8,128)}, f32[264,128]{1,0:T(8,128)S(1)}, u32[]{:S(2)}, u32[]{:S(2)}) collective-permute-start(f32[264,128]{1,0:T(8,128)} %concatenate.51), channel_id=1, source_target_pairs={{96,160},{224,288},{352,416},{480,544},{97,161},{225,289},{353,417... | collective-permute-start | bytes 405512 | tf_op jit(solution)/shard_map/ppermute | solution.py:119
  82.4 1.9 %collective-permute-start.15 = (f32[264,128]{1,0:T(8,128)}, f32[264,128]{1,0:T(8,128)}, u32[]{:S(2)}, u32[]{:S(2)}) collective-permute-start(f32[264,128]{1,0:T(8,128)} %concatenate.51), channel_id=1, source_target_pairs={{96,128},{224,256},{352,384},{480,512},{97,129},{225,257},{353,385... | collective-permute-start | bytes 405512 | tf_op jit(solution)/shard_map/ppermute | solution.py:119
  86.9 1.3 %collective-permute-start.14 = (f32[264,128]{1,0:T(8,128)}, f32[264,128]{1,0:T(8,128)}, u32[]{:S(2)}, u32[]{:S(2)}) collective-permute-start(f32[264,128]{1,0:T(8,128)} %concatenate.50), channel_id=1, source_target_pairs={{608,640},{736,768},{864,896},{609,641},{737,769},{865,897},{610,6... | collective-permute-start | bytes 405512 | tf_op jit(solution)/shard_map/ppermute | solution.py:119
  89.0 1.3 %collective-permute-start.11 = (f32[264,128]{1,0:T(8,128)}, f32[264,128]{1,0:T(8,128)S(1)}, u32[]{:S(2)}, u32[]{:S(2)}) collective-permute-start(f32[264,128]{1,0:T(8,128)} %concatenate.49), channel_id=1, source_target_pairs={{96,64},{224,192},{352,320},{480,448},{97,65},{225,193},{353,321},... | collective-permute-start | bytes 405512 | tf_op jit(solution)/shard_map/ppermute | solution.py:119
  91.6 1.3 %collective-permute-start.10 = (f32[264,128]{1,0:T(8,128)}, f32[264,128]{1,0:T(8,128)}, u32[]{:S(2)}, u32[]{:S(2)}) collective-permute-start(f32[264,128]{1,0:T(8,128)} %concatenate.48), channel_id=1, source_target_pairs={{608,576},{736,704},{864,832},{992,960},{609,577},{737,705},{865,8... | collective-permute-start | bytes 405512 | tf_op jit(solution)/shard_map/ppermute | solution.py:119
  92.9 2.6 %fusion.3 = f32[512,4,128]{0,2,1:T(8,128)S(1)} fusion(bf16[512,4,128]{0,2,1:T(8,128)(2,1)} %bitcast.79, pred[512,512]{1,0:T(8,128)(4,1)} %fusion.4, bf16[512,512]{1,0:T(8,128)(2,1)} %param.6, bf16[512,512]{1,0:T(8,128)(2,1)S(1)} %copy-done), kind=kOutput, calls=%fused_computation.5 | convolution fusion | flops 538968064 | bytes 2883584 | tf_op jit(solution)/shard_map/while/body/eval_jaxpr/hts,shd->thd/dot_general | solution.py:166
  97.7 1.9 %collective-permute-start.16 = (f32[264,128]{1,0:T(8,128)S(1)}, f32[264,128]{1,0:T(8,128)S(1)}, u32[]{:S(2)}, u32[]{:S(2)}) collective-permute-start(f32[264,128]{1,0:T(8,128)S(1)} %concatenate.52), channel_id=1, source_target_pairs={{0,16},{16,0},{1,17},{17,1},{2,18},{18,2},{3,19},{19,3},{4,20},{20... | collective-permute-start | bytes 405512 | tf_op jit(solution)/shard_map/ppermute | solution.py:35
  99.7 1.3 %collective-permute-done.16 = f32[264,128]{1,0:T(8,128)S(1)} collective-permute-done((f32[264,128]{1,0:T(8,128)S(1)}, f32[264,128]{1,0:T(8,128)S(1)}, u32[]{:S(2)}, u32[]{:S(2)}) %collective-permute-start.16) | collective-permute-done | bytes 135200 | tf_op jit(solution)/shard_map/ppermute | solution.py:35
  102.0 7.0 %all-to-all-start = ((f32[16,1,512]{2,1,0:T(1,128)}), f32[16,1,512]{2,1,0:T(1,128)S(1)}, u32[]{:S(2)}, u32[]{:S(2)}) async-start(f32[16,1,512]{2,1,0:T(1,128)} %broadcast_in_dim.99), calls=%async_computation | async-start | bytes 65536 | tf_op jit(solution)/shard_map/all_to_all | solution.py:147
  109.4 7.3 %all-to-all-done = f32[16,1,512]{2,1,0:T(1,128)S(1)} async-done(((f32[16,1,512]{2,1,0:T(1,128)}), f32[16,1,512]{2,1,0:T(1,128)S(1)}, u32[]{:S(2)}, u32[]{:S(2)}) %all-to-all-start) | async-done | bytes 32800 | tf_op jit(solution)/shard_map/all_to_all | solution.py:147
  (87 shorter events, 18.1 us)
Async XLA Ops:
  0.0 92.9 %copy-start = (bf16[512,512]{1,0:T(8,128)(2,1)S(1)}, bf16[512,512]{1,0:T(8,128)(2,1)}, u32[]{:S(2)}) copy-start(bf16[512,512]{1,0:T(8,128)(2,1)} %param.4) | copy-start | bytes 1572868
  0.0 5.5 %copy-start.9 = (bf16[512,512]{1,0:T(8,128)(2,1)S(1)}, bf16[512,512]{1,0:T(8,128)(2,1)}, u32[]{:S(2)}) copy-start(bf16[512,512]{1,0:T(8,128)(2,1)} %param.6) | copy-start | bytes 1572868
  5.8 3.4 %collective-permute-start = (f32[520,128]{1,0:T(8,128)S(1)}, f32[520,128]{1,0:T(8,128)S(1)}, u32[]{:S(2)}, u32[]{:S(2)}) collective-permute-start(f32[520,128]{1,0:T(8,128)S(1)} %concatenate.42), channel_id=1, source_target_pairs={{0,16},{16,0},{1,17},{17,1},{2,18},{18,2},{3,19},{19,3},{4,20},{20... | collective-permute-start | bytes 798728 | tf_op jit(solution)/shard_map/ppermute | solution.py:35
  9.3 86.3 %copy-start.1 = (f32[520,128]{1,0:T(8,128)}, f32[520,128]{1,0:T(8,128)S(1)}, u32[]{:S(2)}) copy-start(f32[520,128]{1,0:T(8,128)S(1)} %collective-permute-done) | copy-start | bytes 798724
  10.4 17.5 %collective-permute-start.3 = (f32[264,128]{1,0:T(8,128)S(1)}, f32[264,128]{1,0:T(8,128)S(1)}, u32[]{:S(2)}, u32[]{:S(2)}) collective-permute-start(f32[264,128]{1,0:T(8,128)S(1)} %concatenate.43), channel_id=1, source_target_pairs={{0,96},{128,224},{256,352},{384,480},{512,608},{640,736},{768,864}... | collective-permute-start | bytes 405512 | tf_op jit(solution)/shard_map/ppermute | solution.py:39
  11.7 17.3 %collective-permute-start.2 = (f32[264,128]{1,0:T(8,128)S(1)}, f32[264,128]{1,0:T(8,128)S(1)}, u32[]{:S(2)}, u32[]{:S(2)}) collective-permute-start(f32[264,128]{1,0:T(8,128)S(1)} %concatenate.43), channel_id=1, source_target_pairs={{0,64},{32,96},{128,192},{160,224},{256,320},{288,352},{384,448},{... | collective-permute-start | bytes 405512 | tf_op jit(solution)/shard_map/ppermute | solution.py:39
  13.0 17.0 %collective-permute-start.1 = (f32[264,128]{1,0:T(8,128)S(1)}, f32[264,128]{1,0:T(8,128)S(1)}, u32[]{:S(2)}, u32[]{:S(2)}) collective-permute-start(f32[264,128]{1,0:T(8,128)S(1)} %concatenate.43), channel_id=1, source_target_pairs={{0,32},{32,64},{64,96},{128,160},{160,192},{192,224},{256,288},{28... | collective-permute-start | bytes 405512 | tf_op jit(solution)/shard_map/ppermute | solution.py:39
  31.3 10.8 %collective-permute-start.6 = (f32[264,128]{1,0:T(8,128)S(1)}, f32[264,128]{1,0:T(8,128)S(1)}, u32[]{:S(2)}, u32[]{:S(2)}) collective-permute-start(f32[264,128]{1,0:T(8,128)S(1)} %concatenate.44), channel_id=1, source_target_pairs={{224,96},{352,224},{480,352},{225,97},{353,225},{481,353},{226,98}... | collective-permute-start | bytes 405512 | tf_op jit(solution)/shard_map/ppermute | solution.py:39
  32.6 11.0 %collective-permute-start.4 = (f32[264,128]{1,0:T(8,128)S(1)}, f32[264,128]{1,0:T(8,128)S(1)}, u32[]{:S(2)}, u32[]{:S(2)}) collective-permute-start(f32[264,128]{1,0:T(8,128)S(1)} %concatenate.44), channel_id=1, source_target_pairs={{96,224},{224,352},{352,480},{608,736},{736,864},{864,992},{97,225... | collective-permute-start | bytes 405512 | tf_op jit(solution)/shard_map/ppermute | solution.py:39
  44.8 34.8 %copy-start.7 = (s32[512]{0:T(512)S(1)}, s32[512]{0:T(512)}, u32[]{:S(2)}) copy-start(s32[512]{0:T(512)} %param.7) | copy-start | bytes 6148
  44.8 15.7 %collective-permute-start.7 = (f32[264,128]{1,0:T(8,128)S(1)}, f32[264,128]{1,0:T(8,128)S(1)}, u32[]{:S(2)}, u32[]{:S(2)}) collective-permute-start(f32[264,128]{1,0:T(8,128)S(1)} %concatenate.46), channel_id=1, source_target_pairs={{352,96},{480,224},{353,97},{481,225},{354,98},{482,226},{355,99},... | collective-permute-start | bytes 405512 | tf_op jit(solution)/shard_map/ppermute | solution.py:39
  46.1 15.9 %collective-permute-start.5 = (f32[264,128]{1,0:T(8,128)S(1)}, f32[264,128]{1,0:T(8,128)S(1)}, u32[]{:S(2)}, u32[]{:S(2)}) collective-permute-start(f32[264,128]{1,0:T(8,128)S(1)} %concatenate.45), channel_id=1, source_target_pairs={{96,352},{224,480},{608,864},{736,992},{97,353},{225,481},{609,865... | collective-permute-start | bytes 405512 | tf_op jit(solution)/shard_map/ppermute | solution.py:39
  63.1 21.3 %copy-start.2 = (f32[264,128]{1,0:T(8,128)S(1)}, f32[264,128]{1,0:T(8,128)}, u32[]{:S(2)}) copy-start(f32[264,128]{1,0:T(8,128)} %constant.106.clone.1) | copy-start | bytes 405508
  63.2 21.1 %collective-permute-start.8 = (f32[264,128]{1,0:T(8,128)S(1)}, f32[264,128]{1,0:T(8,128)S(1)}, u32[]{:S(2)}, u32[]{:S(2)}) collective-permute-start(f32[264,128]{1,0:T(8,128)S(1)} %concatenate.47), channel_id=1, source_target_pairs={{480,736},{96,992},{481,737},{97,993},{482,738},{98,994},{483,739}... | collective-permute-start | bytes 405512 | tf_op jit(solution)/shard_map/ppermute | solution.py:72
  77.3 7.1 %collective-permute-start.9 = (f32[264,128]{1,0:T(8,128)S(1)}, f32[264,128]{1,0:T(8,128)S(1)}, u32[]{:S(2)}, u32[]{:S(2)}) collective-permute-start(f32[264,128]{1,0:T(8,128)S(1)} %concatenate.47), channel_id=1, source_target_pairs={{480,608},{96,864},{481,609},{97,865},{482,610},{98,866},{483,611}... | collective-permute-start | bytes 405512 | tf_op jit(solution)/shard_map/ppermute | solution.py:72
  81.1 9.8 %collective-permute-start.13 = (f32[264,128]{1,0:T(8,128)}, f32[264,128]{1,0:T(8,128)S(1)}, u32[]{:S(2)}, u32[]{:S(2)}) collective-permute-start(f32[264,128]{1,0:T(8,128)} %concatenate.51), channel_id=1, source_target_pairs={{96,160},{224,288},{352,416},{480,544},{97,161},{225,289},{353,417... | collective-permute-start | bytes 405512 | tf_op jit(solution)/shard_map/ppermute | solution.py:119
  82.4 13.2 %collective-permute-start.15 = (f32[264,128]{1,0:T(8,128)}, f32[264,128]{1,0:T(8,128)}, u32[]{:S(2)}, u32[]{:S(2)}) collective-permute-start(f32[264,128]{1,0:T(8,128)} %concatenate.51), channel_id=1, source_target_pairs={{96,128},{224,256},{352,384},{480,512},{97,129},{225,257},{353,385... | collective-permute-start | bytes 405512 | tf_op jit(solution)/shard_map/ppermute | solution.py:119
  86.3 9.4 %collective-permute-start.12 = (f32[264,128]{1,0:T(8,128)}, f32[264,128]{1,0:T(8,128)S(1)}, u32[]{:S(2)}, u32[]{:S(2)}) collective-permute-start(f32[264,128]{1,0:T(8,128)} %concatenate.50), channel_id=1, source_target_pairs={{608,672},{736,800},{864,928},{609,673},{737,801},{865,929},{610,6... | collective-permute-start | bytes 405512 | tf_op jit(solution)/shard_map/ppermute | solution.py:119
  86.9 9.4 %collective-permute-start.14 = (f32[264,128]{1,0:T(8,128)}, f32[264,128]{1,0:T(8,128)}, u32[]{:S(2)}, u32[]{:S(2)}) collective-permute-start(f32[264,128]{1,0:T(8,128)} %concatenate.50), channel_id=1, source_target_pairs={{608,640},{736,768},{864,896},{609,641},{737,769},{865,897},{610,6... | collective-permute-start | bytes 405512 | tf_op jit(solution)/shard_map/ppermute | solution.py:119
  89.0 6.7 %collective-permute-start.11 = (f32[264,128]{1,0:T(8,128)}, f32[264,128]{1,0:T(8,128)S(1)}, u32[]{:S(2)}, u32[]{:S(2)}) collective-permute-start(f32[264,128]{1,0:T(8,128)} %concatenate.49), channel_id=1, source_target_pairs={{96,64},{224,192},{352,320},{480,448},{97,65},{225,193},{353,321},... | collective-permute-start | bytes 405512 | tf_op jit(solution)/shard_map/ppermute | solution.py:119
  91.6 4.0 %collective-permute-start.10 = (f32[264,128]{1,0:T(8,128)}, f32[264,128]{1,0:T(8,128)}, u32[]{:S(2)}, u32[]{:S(2)}) collective-permute-start(f32[264,128]{1,0:T(8,128)} %concatenate.48), channel_id=1, source_target_pairs={{608,576},{736,704},{864,832},{992,960},{609,577},{737,705},{865,8... | collective-permute-start | bytes 405512 | tf_op jit(solution)/shard_map/ppermute | solution.py:119
  96.4 4.6 %slice-start = ((f32[520,128]{1,0:T(8,128)}), f32[512,128]{1,0:T(8,128)S(1)}, s32[]{:S(2)}) async-start(f32[520,128]{1,0:T(8,128)} %copy-done.1), calls=%async_computation.1 | async-start | bytes 524288 | tf_op jit(solution)/shard_map/slice | solution.py:30
  97.7 3.2 %collective-permute-start.16 = (f32[264,128]{1,0:T(8,128)S(1)}, f32[264,128]{1,0:T(8,128)S(1)}, u32[]{:S(2)}, u32[]{:S(2)}) collective-permute-start(f32[264,128]{1,0:T(8,128)S(1)} %concatenate.52), channel_id=1, source_target_pairs={{0,16},{16,0},{1,17},{17,1},{2,18},{18,2},{3,19},{19,3},{4,20},{20... | collective-permute-start | bytes 405512 | tf_op jit(solution)/shard_map/ppermute | solution.py:35
  102.0 14.6 %all-to-all-start = ((f32[16,1,512]{2,1,0:T(1,128)}), f32[16,1,512]{2,1,0:T(1,128)S(1)}, u32[]{:S(2)}, u32[]{:S(2)}) async-start(f32[16,1,512]{2,1,0:T(1,128)} %broadcast_in_dim.99), calls=%async_computation | async-start | bytes 65536 | tf_op jit(solution)/shard_map/all_to_all | solution.py:147
  (5 other events, 9.8 us)
